TPU v7x, 32 devices: a whole 2x2x4 slice. The times are simulated.
32 devices in a mesh: gx: 4 (over z), gy: 4 (over y, x), dp: 2 (over core).
Axes of the slice: x: 2, y: 2, z: 4, core: 2. Of those that a mesh axis runs over, the one named last changes fastest.
Arguments:
- volumes: bfloat16 [6, 32, 32, 32, 128], P('dp', 'gx', 'gy'), may hold values from -6 to 6
- weight_one: bfloat16 [27, 128, 128], replicated, may hold values from -0.109375 to 0.109375
- weight_two: bfloat16 [27, 128, 128], replicated, may hold values from -0.109375 to 0.109375
- cotangent: bfloat16 [6, 32, 32, 32, 128], P('dp', 'gx', 'gy'), may hold values from -0.013671875 to 0.013671875
Outputs:
- features: bfloat16 [6, 32, 32, 32, 128], P('dp', 'gx', 'gy')
- grad_one: float32 [27, 128, 128], replicated
- grad_two: float32 [27, 128, 128], replicated
All inputs are finite; a program needn't handle non-finite values.
Results may differ from a plain program's by a relative error of at most 0.0054.
Values may be sent and summed in bfloat16 or wider, within the bound.
No kernel may reach another device: no remote copies, remote signals or barrier semaphores. Data moves between devices by JAX's collectives and lax.ppermute only.
A program may use at most 128 MiB of HBM per device.

v0:
```python
import jax
import jax.numpy as jnp
from jax import lax
from jax.sharding import PartitionSpec as P


def extended(cells, sides, width):
    for axis, dim in sides:
        count = lax.axis_size(axis)
        ends = count - 1
        head = lax.slice_in_dim(cells, 0, width, axis=dim)
        tail = lax.slice_in_dim(cells, cells.shape[dim] - width, cells.shape[dim], axis=dim)
        cells = jnp.concatenate(
            [
                lax.ppermute(tail, axis, [(i, (i + 1) % count) for i in range(ends)]),
                cells,
                lax.ppermute(head, axis, [((i + 1) % count, i) for i in range(ends)]),
            ],
            axis=dim,
        )
    return cells


def conv_block(padded, kernel):
    depth = kernel.shape[1]
    cube_kernel = kernel.reshape(3, 3, 3, depth, depth)
    return lax.conv_general_dilated(
        padded,
        cube_kernel,
        (1, 1, 1),
        ((0, 0), (0, 0), (1, 1)),
        dimension_numbers=("NDHWC", "DHWIO", "NDHWC"),
        preferred_element_type=jnp.float32,
    )


def kernel_grad(padded, delta_field):
    depth = delta_field.shape[4]
    result = lax.conv_general_dilated(
        padded,
        delta_field,
        (1, 1, 1),
        ((0, 0), (0, 0), (1, 1)),
        dimension_numbers=("CDHWN", "IDHWO", "DHWNC"),
        preferred_element_type=jnp.float32,
    )
    return result.reshape(27 * depth, depth)


def swish_slope(value):
    sigma = jax.nn.sigmoid(value)
    return sigma * (1.0 + value * (1.0 - sigma))


def weight_grad(padded, delta_field):
    local_grad = kernel_grad(padded, delta_field)
    return lax.psum(local_grad, ("gx", "gy", "dp"))


def per_device(volumes, weight_one, weight_two, cotangent):
    layout = volumes.shape
    depth = layout[4]
    flipped = jnp.transpose(weight_two[::-1], (0, 2, 1))
    rim_input = extended(volumes, (("gx", 1), ("gy", 2)), 1)
    act_one = conv_block(rim_input, weight_one)
    hidden = jax.nn.silu(act_one).astype(jnp.bfloat16)
    rim_hidden = extended(hidden, (("gx", 1), ("gy", 2)), 1)
    act_two = conv_block(rim_hidden, weight_two)
    features = jax.nn.silu(act_two).astype(jnp.bfloat16)
    delta_two = (cotangent.astype(jnp.float32) * swish_slope(act_two)).astype(jnp.bfloat16)
    grad_two = weight_grad(rim_hidden, delta_two)
    rim_delta = extended(delta_two, (("gx", 1), ("gy", 2)), 1)
    back_grad = conv_block(rim_delta, flipped)
    delta_one = (back_grad * swish_slope(act_one)).astype(jnp.bfloat16)
    grad_one = weight_grad(rim_input, delta_one)
    return (features, grad_one.reshape(27, depth, depth), grad_two.reshape(27, depth, depth))


def solution(mesh):
    in_specs = (P("dp", "gx", "gy", None, None), P(), P(), P("dp", "gx", "gy", None, None))
    out_specs = (P("dp", "gx", "gy", None, None), P(), P())
    return jax.shard_map(
        per_device, mesh=mesh, in_specs=in_specs, out_specs=out_specs, check_vma=False
    )
```

profile of v0, /device:TPU:0, one launch (start us, length us, event | category | flops | bytes accessed | tf_op | source)
XLA Modules:
  0.0 528.0 jit_solution(5061200848195463211)
XLA Ops:
  8.4 4.9 collective-permute-start
  14.6 2.8 collective-permute-done
  19.4 2.2 collective-permute-done.1
  22.4 3.4 collective-permute-start.2
  27.1 2.3 rev.3
  30.1 7.1 %collective-permute-done.3 = bf16[3,10,1,32,128]{4,3,2,1,0:T(8,128)(2,1)S(1)} collective-permute-done((bf16[3,10,1,32,128]{4,3,2,1,0:T(8,128)(2,1)}, bf16[3,10,1,32,128]{4,3,2,1,0:T(8,128)(2,1)S(1)}, u32[]{:S(2)}, u32[]{:S(2)}) %collective-permute-start.3) | collective-permute-done | bytes 245792 | tf_op jit(solution)/shard_map/ppermute | solution.py:17
  37.2 3.3 fusion.51
  40.6 6.7 %reshape.38 = bf16[10,10,3,8,5,128]{5,4,3,2,1,0:T(8,128)(2,1)} reshape(bf16[10,10,3,40,128]{4,3,2,1,0:T(8,128)(2,1)} %get-tuple-element.17) | data formatting | bytes 6144000 | tf_op jit(solution)/shard_map/conv_general_dilated | solution.py:27
  47.3 3.0 slice.64
  50.3 5.1 fusion.13
  55.4 141.8 %multiply_convert_fusion.2 = (bf16[8,8,24,5,128]{4,2,3,1,0:T(8,128)(2,1)S(1)}, f32[8,8,24,5,128]{4,2,3,1,0:T(8,128)}) fusion(pred[24,5]{0,1:T(8,128)(4,1)S(1)} %copy-done.17, bf16[3,3,3,128,128]{4,3,2,1,0:T(8,128)(2,1)S(1)} %bitcast.90, bf16[10,10,3,8,7,128]{5,4,3,2,1,0:T(8,128)(2,1)S(1)} %fusion.13), kind=kOutput, calls=%fused_computation.36 | convolution fusion | flops 6800670720 | bytes 11083896 | tf_op jit(solution)/shard_map/conv_general_dilated | solution.py:27
  199.1 4.6 collective-permute-start.4
  203.6 6.8 %reshape.60 = bf16[10,10,3,8,5,128]{5,4,3,2,1,0:T(8,128)(2,1)} reshape(bf16[10,10,3,40,128]{4,3,2,1,0:T(8,128)(2,1)} %get-tuple-element.16) | data formatting | bytes 6144000 | tf_op jit(solution)/shard_map/concatenate | solution.py:13
  210.4 5.3 fusion.50
  218.0 3.4 collective-permute-start.6
  223.0 2.4 fusion.49
  225.9 7.6 %collective-permute-done.7 = bf16[3,10,1,32,128]{4,0,3,2,1:T(4,128)(2,1)S(1)} collective-permute-done((bf16[3,10,1,32,128]{4,0,3,2,1:T(4,128)(2,1)S(1)}, bf16[3,10,1,32,128]{4,0,3,2,1:T(4,128)(2,1)S(1)}, u32[]{:S(2)}, u32[]{:S(2)}) %collective-permute-start.7) | collective-permute-done | bytes 245792 | tf_op jit(solution)/shard_map/ppermute | solution.py:17
  233.6 3.1 fusion.60
  239.6 17.1 %add_multiply_fusion = (f32[8,8,24,5,128]{4,2,3,1,0:T(8,128)S(1)}, bf16[8,8,24,5,128]{4,2,3,1,0:T(8,128)(2,1)}) fusion(pred[24,5]{0,1:T(8,128)(4,1)S(1)} %copy-done.17, bf16[3,3,3,128,128]{4,3,2,1,0:T(8,128)(2,1)S(1)} %bitcast.107, bf16[10,10,3,7,2,128]{5,3,2,4,1,0:T(8,128)(2,1)S(1)} %slice.70, bf16[10,10,3,8,5,128]{5,3,2,4,1,0:T(8,128)(2,1)S(1)} %copy.28), kind=kOutput, calls=%fused_computation.33 | convolution fusion | flops 6817505280 | bytes 10930296 | tf_op jit(solution)/shard_map/conv_general_dilated | solution.py:27
  261.2 3.5 collective-permute-start.8
  266.0 19.1 %fusion.11 = (bf16[10,10,3,8,5,128]{5,4,3,2,1,0:T(8,128)(2,1)}, bf16[10,10,3,8,5,128]{5,4,3,2,1,0:T(8,128)(2,1)}) fusion(bf16[10,10,3,7,1,128]{5,4,3,2,1,0:T(2,128)(2,1)S(1)} %copy-done.4, bf16[10,10,3,8,4,128]{5,4,3,2,1,0:T(4,128)(2,1)S(1)} %get-tuple-element.9, bf16[10,10,3,8,4,128]{5,4,3,2,1,0:T(4,128)(2,1)S(1)} %get-tuple-element.8, ...), kind=kLoop, calls=%fused_computation.15 | loop fusion | flops 18432000 | bytes 12134400 | tf_op jit(solution)/shard_map/concatenate | solution.py:13
  285.1 6.7 %reshape.65 = bf16[10,10,24,5,128,1]{4,3,2,1,0,5:T(8,128)(2,1)} reshape(bf16[10,10,3,40,128]{4,3,2,1,0:T(8,128)(2,1)} %get-tuple-element.16) | data formatting | bytes 6144000 | tf_op jit(solution)/shard_map/concatenate | solution.py:13
  291.8 4.8 copy.34
  296.6 4.8 copy.76
  305.2 2.3 collective-permute-start.10
  308.9 24.3 %fusion.31 = f32[3,3,3,128,128]{4,3,2,1,0:T(8,128)} fusion(bf16[3,8,8,32,128]{4,2,3,0,1:T(8,128)(2,1)S(1)} %copy-done.3, bf16[3,10,1,32,128]{4,0,3,2,1:T(4,128)(2,1)S(1)} %copy-done.16, bf16[3,1,8,32,128]{4,0,3,2,1:T(4,128)(2,1)S(1)} %collective-permute-done.5, bf16[3,8,8,32,128]{4,0,3,2,1:T(4,128)(2,1)S(1)} %bitcast.98, ...), kind=kOutput, calls=%fused_computation.47 | convolution fusion | flops 5334859776 | bytes 5799936 | tf_op jit(solution)/shard_map/conv_general_dilated | solution.py:39
  333.1 4.2 maximum_bitcast_fusion
  340.8 2.8 fusion.14
  343.6 15.4 %fusion.76 = bf16[8,8,24,5,128,1]{4,2,5,3,1,0:T(8,128)(2,1)S(1)} fusion(f32[8,8,24,5,128]{4,2,3,1,0:T(8,128)S(1)} %copy-done.19, pred[24,5]{0,1:T(8,128)(4,1)S(1)} %copy-done.18, bf16[3,3,3,128,128]{3,4,2,1,0:T(8,128)(2,1)S(1)} %bitcast.108, bf16[10,10,3,8,7,128]{5,4,3,2,1,0:T(8,128)(2,1)S(1)} %fusion.14), kind=kOutput, calls=%fused_computation.49.clone.2 | convolution fusion | flops 6806568960 | bytes 11083896 | tf_op jit(solution)/shard_map/conv_general_dilated | solution.py:27
  359.1 16.1 %fusion.4 = f32[3,3,3,128,128,1]{4,3,2,5,1,0:T(8,128)} fusion(bf16[10,10,24,5,128,1]{4,2,5,3,1,0:T(8,128)(2,1)S(1)} %bitcast.103, bf16[10,10,24,5,128,1]{4,2,5,3,1,0:T(8,128)(2,1)S(1)} %copy-done.5, bf16[10,10,24,5,128,1]{4,2,5,3,1,0:T(8,128)(2,1)S(1)} %bitcast.104, bf16[8,8,24,5,128,1]{4,2,5,3,1,0:T(8,128)(2,1)S(1)} %fusion.76), kind=kOutput, calls=%fused_computation.7 | convolution fusion | flops 6803988480 | bytes 12951552 | tf_op jit(solution)/shard_map/conv_general_dilated | solution.py:39
  378.7 137.8 %all-reduce.3.cloned.1.call-done = (f32[27,128,128]{2,1,0:T(8,128)}, f32[27,128,128]{2,1,0:T(8,128)}) async-done(((f32[27,128,128]{2,1,0:T(8,128)}, f32[27,128,128]{2,1,0:T(8,128)}), (f32[27,128,128]{2,1,0:T(8,128)}, f32[27,128,128]{2,1,0:T(8,128)})) %all-reduce.3.cloned.1.call-update) | async-done | bytes 3538960 | tf_op jit(solution)/shard_map/psum | solution.py:57
  516.5 3.0 copy.85
  (97 shorter events, 35.2 us)
Async XLA Ops:
  7.2 48.3 %copy-start = (bf16[27,128,128]{2,1,0:T(8,128)(2,1)S(1)}, bf16[27,128,128]{2,1,0:T(8,128)(2,1)}, u32[]{:S(2)}) copy-start(bf16[27,128,128]{2,1,0:T(8,128)(2,1)} %param.5) | copy-start | bytes 2654212
  7.2 509.3 %all-reduce.3.cloned.1.call-start = ((), (), s32[]{:S(2)}) async-start(), calls=%async_computation | async-start | bytes 7077888 | tf_op jit(solution)/shard_map/psum | solution.py:57
  8.4 9.1 %collective-permute-start = (bf16[3,1,8,32,128]{4,3,2,1,0:T(8,128)(2,1)S(1)}, bf16[3,1,8,32,128]{4,3,2,1,0:T(8,128)(2,1)S(1)}, u32[]{:S(2)}, u32[]{:S(2)}) collective-permute-start(bf16[3,1,8,32,128]{4,3,2,1,0:T(8,128)(2,1)S(1)} %get-tuple-element.27), channel_id=1, source_target_pairs={{0,8},{8,16},{16,24},{1,9},{9,17},{17,25},{2,10},{10,18},{18,26},{... | collective-permute-start | bytes 589832 | tf_op jit(solution)/shard_map/ppermute | solution.py:15
  13.3 8.3 %collective-permute-start.1 = (bf16[3,1,8,32,128]{4,3,2,1,0:T(8,128)(2,1)S(1)}, bf16[3,1,8,32,128]{4,3,2,1,0:T(8,128)(2,1)S(1)}, u32[]{:S(2)}, u32[]{:S(2)}) collective-permute-start(bf16[3,1,8,32,128]{4,3,2,1,0:T(8,128)(2,1)S(1)} %get-tuple-element.26), channel_id=1, source_target_pairs={{8,0},{16,8},{24,16},{9,1},{17,9},{25,17},{10,2},{18,10},{26,18},{... | collective-permute-start | bytes 589832 | tf_op jit(solution)/shard_map/ppermute | solution.py:17
  22.4 7.7 %collective-permute-start.2 = (bf16[3,10,1,32,128]{4,3,2,1,0:T(8,128)(2,1)}, bf16[3,10,1,32,128]{4,3,2,1,0:T(8,128)(2,1)S(1)}, u32[]{:S(2)}, u32[]{:S(2)}) collective-permute-start(bf16[3,10,1,32,128]{4,3,2,1,0:T(8,128)(2,1)} %get-tuple-element.22), channel_id=1, source_target_pairs={{0,2},{2,4},{4,6},{1,3},{3,5},{5,7},{8,10},{10,12},{12,14},{9,11},... | collective-permute-start | bytes 737288 | tf_op jit(solution)/shard_map/ppermute | solution.py:15
  25.8 11.4 %collective-permute-start.3 = (bf16[3,10,1,32,128]{4,3,2,1,0:T(8,128)(2,1)}, bf16[3,10,1,32,128]{4,3,2,1,0:T(8,128)(2,1)S(1)}, u32[]{:S(2)}, u32[]{:S(2)}) collective-permute-start(bf16[3,10,1,32,128]{4,3,2,1,0:T(8,128)(2,1)} %get-tuple-element.23), channel_id=1, source_target_pairs={{2,0},{4,2},{6,4},{3,1},{5,3},{7,5},{10,8},{12,10},{14,12},{11,9},... | collective-permute-start | bytes 737288 | tf_op jit(solution)/shard_map/ppermute | solution.py:17
  50.3 5.2 copy-start.17
  197.8 19.7 %collective-permute-start.5 = (bf16[3,1,8,32,128]{4,0,3,2,1:T(4,128)(2,1)S(1)}, bf16[3,1,8,32,128]{4,0,3,2,1:T(4,128)(2,1)S(1)}, u32[]{:S(2)}, u32[]{:S(2)}) collective-permute-start(bf16[3,1,8,32,128]{4,0,3,2,1:T(4,128)(2,1)S(1)} %bitcast.112), channel_id=1, source_target_pairs={{8,0},{16,8},{24,16},{9,1},{17,9},{25,17},{10,2},{18,10},{26,18},{... | collective-permute-start | bytes 589832 | tf_op jit(solution)/shard_map/ppermute | solution.py:17
  199.1 18.4 %collective-permute-start.4 = (bf16[3,1,8,32,128]{4,0,3,2,1:T(4,128)(2,1)S(1)}, bf16[3,1,8,32,128]{4,0,3,2,1:T(4,128)(2,1)S(1)}, u32[]{:S(2)}, u32[]{:S(2)}) collective-permute-start(bf16[3,1,8,32,128]{4,0,3,2,1:T(4,128)(2,1)S(1)} %bitcast.111), channel_id=1, source_target_pairs={{0,8},{8,16},{16,24},{1,9},{9,17},{17,25},{2,10},{10,18},{18,26},{... | collective-permute-start | bytes 589832 | tf_op jit(solution)/shard_map/ppermute | solution.py:15
  215.7 7.3 %slice-start = ((s8[4915200]{0:T(1024)(128)(4,1)}), s8[4194304]{0:T(1024)(128)(4,1)S(1)}, s32[]{:S(2)}) async-start(s8[4915200]{0:T(1024)(128)(4,1)} %bitcast.91), calls=%async_computation.1 | async-start | bytes 8388608
  215.9 7.0 %slice-start.1 = ((s8[4915200]{0:T(1024)(128)(4,1)}), s8[720896]{0:T(1024)(128)(4,1)S(1)}, s32[]{:S(2)}) async-start(s8[4915200]{0:T(1024)(128)(4,1)} %bitcast.91), calls=%async_computation.2 | async-start | bytes 1441792
  218.0 8.0 %collective-permute-start.6 = (bf16[3,10,1,32,128]{4,0,3,2,1:T(4,128)(2,1)S(1)}, bf16[3,10,1,32,128]{4,0,3,2,1:T(4,128)(2,1)S(1)}, u32[]{:S(2)}, u32[]{:S(2)}) collective-permute-start(bf16[3,10,1,32,128]{4,0,3,2,1:T(4,128)(2,1)S(1)} %get-tuple-element.14), channel_id=1, source_target_pairs={{0,2},{2,4},{4,6},{1,3},{3,5},{5,7},{8,10},{10,12},{12,14},{9,11},... | collective-permute-start | bytes 737288 | tf_op jit(solution)/shard_map/ppermute | solution.py:15
  221.4 12.2 %collective-permute-start.7 = (bf16[3,10,1,32,128]{4,0,3,2,1:T(4,128)(2,1)S(1)}, bf16[3,10,1,32,128]{4,0,3,2,1:T(4,128)(2,1)S(1)}, u32[]{:S(2)}, u32[]{:S(2)}) collective-permute-start(bf16[3,10,1,32,128]{4,0,3,2,1:T(4,128)(2,1)S(1)} %get-tuple-element.15), channel_id=1, source_target_pairs={{2,0},{4,2},{6,4},{3,1},{5,3},{7,5},{10,8},{12,10},{14,12},{11,9},... | collective-permute-start | bytes 737288 | tf_op jit(solution)/shard_map/ppermute | solution.py:17
  233.6 4.9 copy-start.15
  257.4 8.6 %copy-start.4 = (bf16[10,10,3,7,1,128]{5,4,3,2,1,0:T(2,128)(2,1)S(1)}, bf16[10,10,3,7,1,128]{5,4,3,2,1,0:T(2,128)(2,1)}, u32[]{:S(2)}) copy-start(bf16[10,10,3,7,1,128]{5,4,3,2,1,0:T(2,128)(2,1)} %get-tuple-element.11) | copy-start | bytes 1612804
  261.2 42.4 %collective-permute-start.8 = (bf16[3,1,8,32,128]{4,2,3,0,1:T(8,128)(2,1)}, bf16[3,1,8,32,128]{4,2,3,0,1:T(8,128)(2,1)S(1)}, u32[]{:S(2)}, u32[]{:S(2)}) collective-permute-start(bf16[3,1,8,32,128]{4,2,3,0,1:T(8,128)(2,1)} %get-tuple-element.24), channel_id=1, source_target_pairs={{0,8},{8,16},{16,24},{1,9},{9,17},{17,25},{2,10},{10,18},{18,26},{... | collective-permute-start | bytes 589832 | tf_op jit(solution)/shard_map/ppermute | solution.py:15
  264.7 38.9 %collective-permute-start.9 = (bf16[3,1,8,32,128]{4,2,3,0,1:T(8,128)(2,1)}, bf16[3,1,8,32,128]{4,2,3,0,1:T(8,128)(2,1)S(1)}, u32[]{:S(2)}, u32[]{:S(2)}) collective-permute-start(bf16[3,1,8,32,128]{4,2,3,0,1:T(8,128)(2,1)} %get-tuple-element.25), channel_id=1, source_target_pairs={{8,0},{16,8},{24,16},{9,1},{17,9},{25,17},{10,2},{18,10},{26,18},{... | collective-permute-start | bytes 589832 | tf_op jit(solution)/shard_map/ppermute | solution.py:17
  291.8 9.6 %slice-start.2 = ((s8[4915200]{0:T(1024)(128)(4,1)}), s8[4194304]{0:T(1024)(128)(4,1)S(1)}, s32[]{:S(2)}) async-start(s8[4915200]{0:T(1024)(128)(4,1)} %bitcast.93), calls=%async_computation.3 | async-start | bytes 8388608
  296.6 4.8 slice-start.3
  301.4 7.4 %copy-start.16 = (bf16[3,10,1,32,128]{4,0,3,2,1:T(4,128)(2,1)S(1)}, bf16[3,10,1,32,128]{4,0,3,2,1:T(4,128)(2,1)}, u32[]{:S(2)}) copy-start(bf16[3,10,1,32,128]{4,0,3,2,1:T(4,128)(2,1)} %copy-done.15) | copy-start | bytes 737284
  303.6 29.5 %copy-start.13 = (bf16[3,1,8,32,128]{4,2,3,0,1:T(8,128)(2,1)}, bf16[3,1,8,32,128]{4,2,3,0,1:T(8,128)(2,1)S(1)}, u32[]{:S(2)}) copy-start(bf16[3,1,8,32,128]{4,2,3,0,1:T(8,128)(2,1)S(1)} %collective-permute-done.8) | copy-start | bytes 589828
  303.6 29.5 %copy-start.14 = (bf16[3,1,8,32,128]{4,2,3,0,1:T(8,128)(2,1)}, bf16[3,1,8,32,128]{4,2,3,0,1:T(8,128)(2,1)S(1)}, u32[]{:S(2)}) copy-start(bf16[3,1,8,32,128]{4,2,3,0,1:T(8,128)(2,1)S(1)} %collective-permute-done.9) | copy-start | bytes 589828
  305.2 27.9 %collective-permute-start.10 = (bf16[3,10,1,32,128]{4,2,3,0,1:T(2,128)(2,1)}, bf16[3,10,1,32,128]{4,2,3,0,1:T(2,128)(2,1)}, u32[]{:S(2)}, u32[]{:S(2)}) collective-permute-start(bf16[3,10,1,32,128]{4,2,3,0,1:T(2,128)(2,1)} %get-tuple-element.18), channel_id=1, source_target_pairs={{0,2},{2,4},{4,6},{1,3},{3,5},{5,7},{8,10},{10,12},{12,14},{9,11},... | collective-permute-start | bytes 737288 | tf_op jit(solution)/shard_map/ppermute | solution.py:15
  307.6 25.6 %collective-permute-start.11 = (bf16[3,10,1,32,128]{4,2,3,0,1:T(2,128)(2,1)}, bf16[3,10,1,32,128]{4,2,3,0,1:T(2,128)(2,1)}, u32[]{:S(2)}, u32[]{:S(2)}) collective-permute-start(bf16[3,10,1,32,128]{4,2,3,0,1:T(2,128)(2,1)} %get-tuple-element.19), channel_id=1, source_target_pairs={{2,0},{4,2},{6,4},{3,1},{5,3},{7,5},{10,8},{12,10},{14,12},{11,9},... | collective-permute-start | bytes 737288 | tf_op jit(solution)/shard_map/ppermute | solution.py:17
  340.7 2.8 copy-start.12
  340.8 2.8 copy-start.18
  340.8 2.8 copy-start.19
  343.6 15.5 %copy-start.5 = (bf16[10,10,24,5,128,1]{4,2,5,3,1,0:T(8,128)(2,1)S(1)}, bf16[10,10,24,5,128,1]{4,2,5,3,1,0:T(8,128)(2,1)}, u32[]{:S(2)}) copy-start(bf16[10,10,24,5,128,1]{4,2,5,3,1,0:T(8,128)(2,1)} %copy.34) | copy-start | bytes 9216004
  343.6 15.5 %copy-start.6 = (bf16[10,10,3,8,5,128]{5,3,2,4,1,0:T(8,128)(2,1)S(1)}, bf16[10,10,3,8,5,128]{5,3,2,4,1,0:T(8,128)(2,1)}, u32[]{:S(2)}) copy-start(bf16[10,10,3,8,5,128]{5,3,2,4,1,0:T(8,128)(2,1)} %copy.76) | copy-start | bytes 9216004
  343.6 15.5 %copy-start.7 = (bf16[10,10,3,8,5,128]{5,3,2,4,1,0:T(8,128)(2,1)S(1)}, bf16[10,10,3,8,5,128]{5,3,2,4,1,0:T(8,128)(2,1)}, u32[]{:S(2)}) copy-start(bf16[10,10,3,8,5,128]{5,3,2,4,1,0:T(8,128)(2,1)} %copy.77) | copy-start | bytes 9216004
  377.1 143.6 %copy-start.1 = (bf16[27,128,128]{2,1,0:T(8,128)(2,1)S(1)}, bf16[27,128,128]{2,1,0:T(8,128)(2,1)}, u32[]{:S(2)}) copy-start(bf16[27,128,128]{2,1,0:T(8,128)(2,1)} %param.5) | copy-start | bytes 2654212
  516.5 3.0 copy-start.9
  (5 other events, 7.5 us)
Sparse Core Ops, SparseCore 0:
  375.4 141.0 all-reduce.2
where the time goes:
time: 537 us; the launch traced here: 528 us
  matrix products  215 us (40%)
  waiting for transfers between devices  159 us (30%)
  local copies, waits for them, and re-layouts  68.3 us (13%)
  other arithmetic  40.9 us (8%)
  starting transfers between devices  30.1 us (6%)
  between operations  15.1 us (3%)
    conv_general_dilated x3, matrix products, conv_block(): lax.conv_general_dilated(padded, cube_kernel, (1, 1, 1), ((0, 0), (0, 0),...  174 us
    psum x1, waiting for transfers between devices, weight_grad(): return lax.psum(local_grad, ('gx', 'gy', 'dp'))  138 us
    conv_general_dilated x2, matrix products, kernel_grad(): lax.conv_general_dilated(padded, delta_field, (1, 1, 1), ((0, 0), (0, 0),...  40.4 us
    concatenate x10, local copies, waits for them, and re-layouts, extended(): jnp.concatenate([lax.ppermute(tail, axis, [(i, (i + 1) % count) for i in...  35.8 us
    concatenate x4, other arithmetic, extended(): jnp.concatenate([lax.ppermute(tail, axis, [(i, (i + 1) % count) for i in...  29.7 us
    ppermute x6, starting transfers between devices, extended(): lax.ppermute(tail, axis, [(i, (i + 1) % count) for i in range(ends)])  22.1 us
    ppermute x6, waiting for transfers between devices, extended(): lax.ppermute(head, axis, [((i + 1) % count, i) for i in range(ends)])  16.9 us
    unnamed x56, local copies, waits for them, and re-layouts  13.1 us
  transfers between devices with their start and end apart: 13, of which 7 were waited for; matrix products, arithmetic and copies ran while one was open for 16% of the time, Pallas kernels for 0%

commit v1 on v0

--- a/solution.py
+++ b/solution.py
@@ -52,9 +52,43 @@
     return sigma * (1.0 + value * (1.0 - sigma))
 
 
+def tree_sum(value, axes):
+    sizes = [lax.axis_size(axis) for axis in axes]
+    if any(n & (n - 1) for n in sizes):
+        return lax.psum(value, axes)
+    steps = []
+    total = 1
+    for axis, n in zip(axes, sizes):
+        bit = n // 2
+        while bit >= 1:
+            steps.append((axis, n, bit))
+            bit //= 2
+        total *= n
+    flat = value.reshape(-1)
+    unit = total * 8 * 128
+    size = flat.shape[0]
+    rows = jnp.pad(flat, (0, -(-size // unit) * unit - size)).reshape(-1, 128)
+    sides = []
+    for axis, n, bit in steps:
+        side = (lax.axis_index(axis) // bit) % 2
+        half = rows.shape[0] // 2
+        pairs = [(i, i ^ bit) for i in range(n)]
+        keep = lax.dynamic_slice_in_dim(rows, side * half, half, 0)
+        send = lax.dynamic_slice_in_dim(rows, (1 - side) * half, half, 0)
+        rows = keep + lax.ppermute(send, axis, pairs)
+        sides.append(side)
+    for (axis, n, bit), side in zip(reversed(steps), reversed(sides)):
+        pairs = [(i, i ^ bit) for i in range(n)]
+        other = lax.ppermute(rows, axis, pairs)
+        low = jnp.where(side == 0, rows, other)
+        high = jnp.where(side == 0, other, rows)
+        rows = jnp.concatenate([low, high], 0)
+    return rows.reshape(-1)[:size].reshape(value.shape)
+
+
 def weight_grad(padded, delta_field):
     local_grad = kernel_grad(padded, delta_field)
-    return lax.psum(local_grad, ("gx", "gy", "dp"))
+    return tree_sum(local_grad, ("dp", "gy", "gx"))
 
 
 def per_device(volumes, weight_one, weight_two, cotangent):
@@ -62,7 +96,7 @@
     depth = layout[4]
     flipped = jnp.transpose(weight_two[::-1], (0, 2, 1))
     rim_input = extended(volumes, (("gx", 1), ("gy", 2)), 1)
-    act_one = conv_block(rim_input, weight_one)
+    act_one = lax.optimization_barrier(conv_block(rim_input, weight_one))
     hidden = jax.nn.silu(act_one).astype(jnp.bfloat16)
     rim_hidden = extended(hidden, (("gx", 1), ("gy", 2)), 1)
     act_two = conv_block(rim_hidden, weight_two)

time: 537 us -> 320 us (0.60); the launches traced: 528 us -> 316 us
  matrix products: 215 us -> 105 us
  waiting for transfers between devices: 159 us -> 107 us
  local copies, waits for them, and re-layouts: 68.3 us -> 29.8 us
  between operations: 15.1 us -> 1.85 us
  starting transfers between devices: 30.1 us -> 43 us
  other arithmetic: 40.9 us -> 29.9 us
    psum x1 -> x0, waiting for transfers between devices: 138 us -> none  [weight_grad(): return lax.psum(local_grad, ('gx', 'gy', 'dp'))]
    conv_general_dilated x3, matrix products: 174 us -> 53.1 us  [conv_block(): lax.conv_general_dilated(padded, cube_kernel, (1, 1, 1), ((0, 0), (0, 0),...]
    ppermute x0 -> x20, waiting for transfers between devices: none -> 55.7 us  [the longest x10 34.5 us: tree_sum(): rows = keep + lax.ppermute(send, axis, pairs)]
    concatenate x10 -> x4, local copies, waits for them, and re-layouts: 35.8 us -> 4.67 us  [extended(): jnp.concatenate([lax.ppermute(tail, axis, [(i, (i + 1) % count) for i in...]
    concatenate x4 -> x3, other arithmetic: 29.7 us -> 10.5 us  [extended(): jnp.concatenate([lax.ppermute(tail, axis, [(i, (i + 1) % count) for i in...]
    ppermute x6, waiting for transfers between devices: 16.9 us -> 33.1 us  [extended(): lax.ppermute(head, axis, [((i + 1) % count, i) for i in range(ends)])]
    ppermute x6, waiting for transfers between devices: 4.13 us -> 18.3 us  [extended(): lax.ppermute(tail, axis, [(i, (i + 1) % count) for i in range(ends)])]
    ppermute x0 -> x20, starting transfers between devices: none -> 13 us  [the longest x10 8.75 us: tree_sum(): rows = keep + lax.ppermute(send, axis, pairs)]
  transfers between devices with their start and end apart: 13 -> 32, of which waited for: 7 -> 25; matrix products, arithmetic and copies ran while one was open for 16% -> 32% of each run, Pallas kernels for 0% -> 0%
where the time goes in v1:
time: 320 us; the launch traced here: 316 us
  waiting for transfers between devices  107 us (33%)
  matrix products  105 us (33%)
  starting transfers between devices  43 us (13%)
  other arithmetic  29.9 us (9%)
  local copies, waits for them, and re-layouts  29.8 us (9%)
    conv_general_dilated x3, matrix products, conv_block(): lax.conv_general_dilated(padded, cube_kernel, (1, 1, 1), ((0, 0), (0, 0),...  53.1 us
    conv_general_dilated x2, matrix products, kernel_grad(): lax.conv_general_dilated(padded, delta_field, (1, 1, 1), ((0, 0), (0, 0),...  51.6 us
    ppermute x10, waiting for transfers between devices, tree_sum(): rows = keep + lax.ppermute(send, axis, pairs)  34.5 us
    ppermute x6, waiting for transfers between devices, extended(): lax.ppermute(head, axis, [((i + 1) % count, i) for i in range(ends)])  33.1 us
    ppermute x6, starting transfers between devices, extended(): lax.ppermute(tail, axis, [(i, (i + 1) % count) for i in range(ends)])  21.9 us
    ppermute x10, waiting for transfers between devices, tree_sum(): other = lax.ppermute(rows, axis, pairs)  21.2 us
    ppermute x6, waiting for transfers between devices, extended(): lax.ppermute(tail, axis, [(i, (i + 1) % count) for i in range(ends)])  18.3 us
    unnamed x40, local copies, waits for them, and re-layouts  10.7 us
  transfers between devices with their start and end apart: 32, of which 25 were waited for; matrix products, arithmetic and copies ran while one was open for 32% of the time, Pallas kernels for 0%

profile of v1, /device:TPU:0, one launch (start us, length us, event | category | flops | bytes accessed | tf_op | source)
XLA Modules:
  0.0 316.4 jit_solution(7989769138579043566)
XLA Ops:
  2.0 4.9 %collective-permute-start = (bf16[3,1,8,32,128]{4,0,3,2,1:T(4,128)(2,1)S(1)}, bf16[3,1,8,32,128]{4,0,3,2,1:T(4,128)(2,1)S(1)}, u32[]{:S(2)}, u32[]{:S(2)}) collective-permute-start(bf16[3,1,8,32,128]{4,0,3,2,1:T(4,128)(2,1)S(1)} %copy.55), channel_id=1, source_target_pairs={{0,8},{8,16},{16,24},{1,9},{9,17},{17,25},{2,10},{10,18},{18,26},{... | collective-permute-start | bytes 589832 | tf_op jit(solution)/shard_map/ppermute | solution.py:15
  8.4 4.1 %collective-permute-done = bf16[3,1,8,32,128]{4,0,3,2,1:T(4,128)(2,1)S(1)} collective-permute-done((bf16[3,1,8,32,128]{4,0,3,2,1:T(4,128)(2,1)S(1)}, bf16[3,1,8,32,128]{4,0,3,2,1:T(4,128)(2,1)S(1)}, u32[]{:S(2)}, u32[]{:S(2)}) %collective-permute-start) | collective-permute-done | bytes 196640 | tf_op jit(solution)/shard_map/ppermute | solution.py:15
  12.5 2.9 constant_dynamic-update-slice_fusion.1
  17.2 3.4 %collective-permute-start.2 = (bf16[3,10,1,32,128]{4,0,3,2,1:T(4,128)(2,1)S(1)}, bf16[3,10,1,32,128]{4,0,3,2,1:T(4,128)(2,1)S(1)}, u32[]{:S(2)}, u32[]{:S(2)}) collective-permute-start(bf16[3,10,1,32,128]{4,0,3,2,1:T(4,128)(2,1)S(1)} %get-tuple-element.10), channel_id=1, source_target_pairs={{0,2},{2,4},{4,6},{1,3},{3,5},{5,7},{8,10},{10,12},{12,14},{9,11},... | collective-permute-start | bytes 737288 | tf_op jit(solution)/shard_map/ppermute | solution.py:15
  22.1 4.3 %collective-permute-done.2 = bf16[3,10,1,32,128]{4,0,3,2,1:T(4,128)(2,1)S(1)} collective-permute-done((bf16[3,10,1,32,128]{4,0,3,2,1:T(4,128)(2,1)S(1)}, bf16[3,10,1,32,128]{4,0,3,2,1:T(4,128)(2,1)S(1)}, u32[]{:S(2)}, u32[]{:S(2)}) %collective-permute-start.2) | collective-permute-done | bytes 245792 | tf_op jit(solution)/shard_map/ppermute | solution.py:15
  26.4 9.0 %collective-permute-done.3 = bf16[3,10,1,32,128]{4,0,3,2,1:T(4,128)(2,1)S(1)} collective-permute-done((bf16[3,10,1,32,128]{4,0,3,2,1:T(4,128)(2,1)S(1)}, bf16[3,10,1,32,128]{4,0,3,2,1:T(4,128)(2,1)S(1)}, u32[]{:S(2)}, u32[]{:S(2)}) %collective-permute-start.3) | collective-permute-done | bytes 245792 | tf_op jit(solution)/shard_map/ppermute | solution.py:17
  40.6 15.5 %broadcast_select_fusion.1 = f32[8,8,24,5,128]{4,2,3,1,0:T(8,128)S(1)} fusion(pred[24,5]{0,1:T(8,128)(4,1)S(1)} %copy-done.15, bf16[3,3,3,128,128]{4,3,2,1,0:T(8,128)(2,1)S(1)} %bitcast.63, bf16[10,10,3,7,2,128]{5,3,2,4,1,0:T(8,128)(2,1)S(1)} %slice.69, bf16[10,10,3,8,5,128]{5,3,2,4,1,0:T(8,128)(2,1)S(1)} %copy.21), kind=kOutput, calls=%fused_computation.42 | convolution fusion | flops 6808657920 | bytes 8964216 | tf_op jit(solution)/shard_map/conv_general_dilated | solution.py:27
  62.3 3.5 %collective-permute-start.4 = (bf16[3,1,8,32,128]{4,0,3,2,1:T(4,128)(2,1)S(1)}, bf16[3,1,8,32,128]{4,0,3,2,1:T(4,128)(2,1)S(1)}, u32[]{:S(2)}, u32[]{:S(2)}) collective-permute-start(bf16[3,1,8,32,128]{4,0,3,2,1:T(4,128)(2,1)S(1)} %get-tuple-element.12), channel_id=1, source_target_pairs={{0,8},{8,16},{16,24},{1,9},{9,17},{17,25},{2,10},{10,18},{18,26},{... | collective-permute-start | bytes 589832 | tf_op jit(solution)/shard_map/ppermute | solution.py:15
  69.6 4.4 %collective-permute-done.5 = bf16[3,1,8,32,128]{4,0,3,2,1:T(4,128)(2,1)S(1)} collective-permute-done((bf16[3,1,8,32,128]{4,0,3,2,1:T(4,128)(2,1)S(1)}, bf16[3,1,8,32,128]{4,0,3,2,1:T(4,128)(2,1)S(1)}, u32[]{:S(2)}, u32[]{:S(2)}) %collective-permute-start.5) | collective-permute-done | bytes 196640 | tf_op jit(solution)/shard_map/ppermute | solution.py:17
  75.3 4.1 %collective-permute-start.6 = (bf16[3,10,1,32,128]{4,0,3,2,1:T(4,128)(2,1)}, bf16[3,10,1,32,128]{4,0,3,2,1:T(4,128)(2,1)}, u32[]{:S(2)}, u32[]{:S(2)}) collective-permute-start(bf16[3,10,1,32,128]{4,0,3,2,1:T(4,128)(2,1)} %get-tuple-element.8), channel_id=1, source_target_pairs={{0,2},{2,4},{4,6},{1,3},{3,5},{5,7},{8,10},{10,12},{12,14},{9,11},... | collective-permute-start | bytes 737288 | tf_op jit(solution)/shard_map/ppermute | solution.py:15
  83.6 7.2 %collective-permute-done.7 = bf16[3,10,1,32,128]{4,0,3,2,1:T(4,128)(2,1)} collective-permute-done((bf16[3,10,1,32,128]{4,0,3,2,1:T(4,128)(2,1)}, bf16[3,10,1,32,128]{4,0,3,2,1:T(4,128)(2,1)}, u32[]{:S(2)}, u32[]{:S(2)}) %collective-permute-start.7) | collective-permute-done | bytes 245792 | tf_op jit(solution)/shard_map/ppermute | solution.py:17
  90.8 4.1 %fusion.51 = bf16[10,10,3,32,128]{4,2,3,1,0:T(4,128)(2,1)S(1)} fusion(bf16[3,10,1,32,128]{4,0,3,2,1:T(4,128)(2,1)} %collective-permute-done.7, bf16[3,1,8,32,128]{4,0,3,2,1:T(4,128)(2,1)S(1)} %collective-permute-done.5, bf16[3,8,8,32,128]{4,0,3,2,1:T(4,128)(2,1)S(1)} %multiply_convert_fusion, bf16[3,1,8,32,128]{4,0,3,2,1:T(4,128)(2,1)S(1)} %collective-permute-done.4, ...), kind=kLoop, calls=%fused_computation.117 | loop fusion | flops 4915200 | bytes 4915200 | tf_op jit(solution)/shard_map/concatenate | solution.py:13
  97.5 17.0 %add_multiply_fusion = (f32[8,8,24,5,128]{4,2,3,1,0:T(8,128)S(1)}, bf16[8,8,24,5,128]{4,2,3,1,0:T(8,128)(2,1)}) fusion(pred[24,5]{0,1:T(8,128)(4,1)S(1)} %copy-done.15, bf16[3,3,3,128,128]{4,3,2,1,0:T(8,128)(2,1)S(1)} %bitcast.77, bf16[10,10,3,7,2,128]{5,3,2,4,1,0:T(8,128)(2,1)S(1)} %slice.73, bf16[10,10,3,8,5,128]{5,3,2,4,1,0:T(8,128)(2,1)S(1)} %copy.25), kind=kOutput, calls=%fused_computation.28 | convolution fusion | flops 6817505280 | bytes 10930296 | tf_op jit(solution)/shard_map/conv_general_dilated | solution.py:27
  117.8 4.5 %collective-permute-start.8 = (bf16[3,1,8,32,128]{4,2,3,0,1:T(8,128)(2,1)}, bf16[3,1,8,32,128]{4,2,3,0,1:T(8,128)(2,1)}, u32[]{:S(2)}, u32[]{:S(2)}) collective-permute-start(bf16[3,1,8,32,128]{4,2,3,0,1:T(8,128)(2,1)} %get-tuple-element.20), channel_id=1, source_target_pairs={{0,8},{8,16},{16,24},{1,9},{9,17},{17,25},{2,10},{10,18},{18,26},{... | collective-permute-start | bytes 589832 | tf_op jit(solution)/shard_map/ppermute | solution.py:15
  123.7 24.2 %fusion.27 = f32[3,3,3,128,128]{4,3,2,1,0:T(8,128)S(1)} fusion(bf16[3,8,8,32,128]{4,2,3,0,1:T(8,128)(2,1)S(1)} %fusion.24, bf16[3,10,1,32,128]{4,0,3,2,1:T(4,128)(2,1)} %collective-permute-done.7, bf16[3,1,8,32,128]{4,0,3,2,1:T(4,128)(2,1)S(1)} %collective-permute-done.5, bf16[3,8,8,32,128]{4,0,3,2,1:T(4,128)(2,1)S(1)} %multiply_convert_fusion, ...), kind=kOutput, calls=%fused_computation.38 | convolution fusion | flops 5334859776 | bytes 5799936 | tf_op jit(solution)/shard_map/conv_general_dilated | solution.py:39
  148.0 2.7 pad_maximum_fusion.8
  154.5 5.6 %collective-permute-done.10 = bf16[3,10,1,32,128]{4,2,3,0,1:T(2,128)(2,1)S(1)} collective-permute-done((bf16[3,10,1,32,128]{4,2,3,0,1:T(2,128)(2,1)S(1)}, bf16[3,10,1,32,128]{4,2,3,0,1:T(2,128)(2,1)S(1)}, u32[]{:S(2)}, u32[]{:S(2)}) %collective-permute-start.10) | collective-permute-done | bytes 245792 | tf_op jit(solution)/shard_map/ppermute | solution.py:15
  160.1 11.3 %collective-permute-done.11 = bf16[3,10,1,32,128]{4,2,3,0,1:T(2,128)(2,1)S(1)} collective-permute-done((bf16[3,10,1,32,128]{4,2,3,0,1:T(2,128)(2,1)S(1)}, bf16[3,10,1,32,128]{4,2,3,0,1:T(2,128)(2,1)S(1)}, u32[]{:S(2)}, u32[]{:S(2)}) %collective-permute-start.11) | collective-permute-done | bytes 245792 | tf_op jit(solution)/shard_map/ppermute | solution.py:17
  171.4 3.8 %maximum_bitcast_fusion = bf16[10,10,3,32,128]{4,1,3,2,0:T(8,128)(2,1)S(1)} fusion(bf16[3,10,1,32,128]{4,2,3,0,1:T(2,128)(2,1)S(1)} %collective-permute-done.11, bf16[3,1,8,32,128]{4,2,3,0,1:T(8,128)(2,1)} %collective-permute-done.9, bf16[3,8,8,32,128]{4,2,3,0,1:T(8,128)(2,1)S(1)} %fusion.24, bf16[3,1,8,32,128]{4,2,3,0,1:T(8,128)(2,1)} %collective-permute-done.8, ...), kind=kLoop, calls=%fused_computation.27 | loop fusion | flops 12288000 | bytes 4915200 | tf_op jit(solution)/shard_map/concatenate | solution.py:13
  178.6 2.8 fusion.3
  181.4 20.5 %broadcast_select_fusion = f32[8,8,24,5,128]{4,2,3,1,0:T(8,128)S(1)} fusion(pred[24,5]{0,1:T(8,128)(4,1)S(1)} %copy-done.16, bf16[3,3,3,128,128]{3,4,2,1,0:T(8,128)(2,1)S(1)} %bitcast.78, bf16[10,10,3,8,7,128]{5,4,3,2,1,0:T(8,128)(2,1)S(1)} %fusion.3), kind=kOutput, calls=%fused_computation.41 | convolution fusion | flops 6795755520 | bytes 9117816 | tf_op jit(solution)/shard_map/conv_general_dilated | solution.py:27
  205.1 27.5 %fusion.29 = f32[3,3,3,128,128]{4,3,2,1,0:T(8,128)S(1)} fusion(f32[8,8,3,32,128]{4,1,3,2,0:T(8,128)S(1)} %slice.79, f32[3,8,8,32,128]{4,0,3,2,1:T(4,128)S(1)} %bitcast.66, bf16[3,10,1,32,128]{4,0,3,2,1:T(4,128)(2,1)S(1)} %copy-done.14, bf16[3,10,8,32,128]{4,0,3,2,1:T(4,128)(2,1)S(1)} %copy-done.7, bf16[3,10,1,32,128]{4,0,3,2,1:T(4,128)(2,1)S(1)} %copy-done.12), kind=kOutput, calls=%fused_computation.40 | convolution fusion | flops 5337022464 | bytes 10518528 | tf_op jit(solution)/shard_map/conv_general_dilated | solution.py:39
  235.9 12.3 %collective-permute-done.23 = f32[896,128]{1,0:T(8,128)} collective-permute-done((f32[896,128]{1,0:T(8,128)S(1)}, f32[896,128]{1,0:T(8,128)}, u32[]{:S(2)}, u32[]{:S(2)}) %collective-permute-start.23) | collective-permute-done | bytes 458784 | tf_op jit(solution)/shard_map/ppermute | solution.py:78
  251.0 4.7 %collective-permute-done.24 = f32[448,128]{1,0:T(8,128)S(1)} collective-permute-done((f32[448,128]{1,0:T(8,128)S(1)}, f32[448,128]{1,0:T(8,128)S(1)}, u32[]{:S(2)}, u32[]{:S(2)}) %collective-permute-start.24) | collective-permute-done | bytes 229408 | tf_op jit(solution)/shard_map/ppermute | solution.py:78
  255.8 2.8 collective-permute-start.25
  258.6 3.0 collective-permute-done.25
  273.0 6.5 %collective-permute-done.15 = f32[224,128]{1,0:T(8,128)S(1)} collective-permute-done((f32[224,128]{1,0:T(8,128)S(1)}, f32[224,128]{1,0:T(8,128)S(1)}, u32[]{:S(2)}, u32[]{:S(2)}) %collective-permute-start.15) | collective-permute-done | bytes 114720 | tf_op jit(solution)/shard_map/ppermute | solution.py:78
  280.1 4.2 %collective-permute-done.16 = f32[112,128]{1,0:T(8,128)S(1)} collective-permute-done((f32[112,128]{1,0:T(8,128)S(1)}, f32[112,128]{1,0:T(8,128)S(1)}, u32[]{:S(2)}, u32[]{:S(2)}) %collective-permute-start.16) | collective-permute-done | bytes 57376 | tf_op jit(solution)/shard_map/ppermute | solution.py:78
  284.4 3.5 %collective-permute-done.28 = f32[224,128]{1,0:T(8,128)S(1)} collective-permute-done((f32[224,128]{1,0:T(8,128)S(1)}, f32[224,128]{1,0:T(8,128)S(1)}, u32[]{:S(2)}, u32[]{:S(2)}) %collective-permute-start.28) | collective-permute-done | bytes 114720 | tf_op jit(solution)/shard_map/ppermute | solution.py:82
  289.3 5.7 %collective-permute-done.18 = f32[224,128]{1,0:T(8,128)S(1)} collective-permute-done((f32[224,128]{1,0:T(8,128)S(1)}, f32[224,128]{1,0:T(8,128)S(1)}, u32[]{:S(2)}, u32[]{:S(2)}) %collective-permute-start.18) | collective-permute-done | bytes 114720 | tf_op jit(solution)/shard_map/ppermute | solution.py:82
  296.1 5.1 %collective-permute-done.19 = f32[448,128]{1,0:T(8,128)S(1)} collective-permute-done((f32[448,128]{1,0:T(8,128)S(1)}, f32[448,128]{1,0:T(8,128)S(1)}, u32[]{:S(2)}, u32[]{:S(2)}) %collective-permute-start.19) | collective-permute-done | bytes 229408 | tf_op jit(solution)/shard_map/ppermute | solution.py:82
  302.2 3.8 %collective-permute-done.30 = f32[896,128]{1,0:T(8,128)S(1)} collective-permute-done((f32[896,128]{1,0:T(8,128)S(1)}, f32[896,128]{1,0:T(8,128)S(1)}, u32[]{:S(2)}, u32[]{:S(2)}) %collective-permute-start.30) | collective-permute-done | bytes 458784 | tf_op jit(solution)/shard_map/ppermute | solution.py:82
  (149 shorter events, 75.9 us)
Async XLA Ops:
  2.0 10.5 %collective-permute-start = (bf16[3,1,8,32,128]{4,0,3,2,1:T(4,128)(2,1)S(1)}, bf16[3,1,8,32,128]{4,0,3,2,1:T(4,128)(2,1)S(1)}, u32[]{:S(2)}, u32[]{:S(2)}) collective-permute-start(bf16[3,1,8,32,128]{4,0,3,2,1:T(4,128)(2,1)S(1)} %copy.55), channel_id=1, source_target_pairs={{0,8},{8,16},{16,24},{1,9},{9,17},{17,25},{2,10},{10,18},{18,26},{... | collective-permute-start | bytes 589832 | tf_op jit(solution)/shard_map/ppermute | solution.py:15
  7.1 9.7 %collective-permute-start.1 = (bf16[3,1,8,32,128]{4,0,3,2,1:T(4,128)(2,1)S(1)}, bf16[3,1,8,32,128]{4,0,3,2,1:T(4,128)(2,1)S(1)}, u32[]{:S(2)}, u32[]{:S(2)}) collective-permute-start(bf16[3,1,8,32,128]{4,0,3,2,1:T(4,128)(2,1)S(1)} %copy.56), channel_id=1, source_target_pairs={{8,0},{16,8},{24,16},{9,1},{17,9},{25,17},{10,2},{18,10},{26,18},{... | collective-permute-start | bytes 589832 | tf_op jit(solution)/shard_map/ppermute | solution.py:17
  17.2 9.2 %collective-permute-start.2 = (bf16[3,10,1,32,128]{4,0,3,2,1:T(4,128)(2,1)S(1)}, bf16[3,10,1,32,128]{4,0,3,2,1:T(4,128)(2,1)S(1)}, u32[]{:S(2)}, u32[]{:S(2)}) collective-permute-start(bf16[3,10,1,32,128]{4,0,3,2,1:T(4,128)(2,1)S(1)} %get-tuple-element.10), channel_id=1, source_target_pairs={{0,2},{2,4},{4,6},{1,3},{3,5},{5,7},{8,10},{10,12},{12,14},{9,11},... | collective-permute-start | bytes 737288 | tf_op jit(solution)/shard_map/ppermute | solution.py:15
  20.6 14.7 %collective-permute-start.3 = (bf16[3,10,1,32,128]{4,0,3,2,1:T(4,128)(2,1)S(1)}, bf16[3,10,1,32,128]{4,0,3,2,1:T(4,128)(2,1)S(1)}, u32[]{:S(2)}, u32[]{:S(2)}) collective-permute-start(bf16[3,10,1,32,128]{4,0,3,2,1:T(4,128)(2,1)S(1)} %get-tuple-element.11), channel_id=1, source_target_pairs={{2,0},{4,2},{6,4},{3,1},{5,3},{7,5},{10,8},{12,10},{14,12},{11,9},... | collective-permute-start | bytes 737288 | tf_op jit(solution)/shard_map/ppermute | solution.py:17
  62.3 7.3 %collective-permute-start.4 = (bf16[3,1,8,32,128]{4,0,3,2,1:T(4,128)(2,1)S(1)}, bf16[3,1,8,32,128]{4,0,3,2,1:T(4,128)(2,1)S(1)}, u32[]{:S(2)}, u32[]{:S(2)}) collective-permute-start(bf16[3,1,8,32,128]{4,0,3,2,1:T(4,128)(2,1)S(1)} %get-tuple-element.12), channel_id=1, source_target_pairs={{0,8},{8,16},{16,24},{1,9},{9,17},{17,25},{2,10},{10,18},{18,26},{... | collective-permute-start | bytes 589832 | tf_op jit(solution)/shard_map/ppermute | solution.py:15
  65.7 8.3 %collective-permute-start.5 = (bf16[3,1,8,32,128]{4,0,3,2,1:T(4,128)(2,1)S(1)}, bf16[3,1,8,32,128]{4,0,3,2,1:T(4,128)(2,1)S(1)}, u32[]{:S(2)}, u32[]{:S(2)}) collective-permute-start(bf16[3,1,8,32,128]{4,0,3,2,1:T(4,128)(2,1)S(1)} %get-tuple-element.13), channel_id=1, source_target_pairs={{8,0},{16,8},{24,16},{9,1},{17,9},{25,17},{10,2},{18,10},{26,18},{... | collective-permute-start | bytes 589832 | tf_op jit(solution)/shard_map/ppermute | solution.py:17
  75.3 8.3 %collective-permute-start.6 = (bf16[3,10,1,32,128]{4,0,3,2,1:T(4,128)(2,1)}, bf16[3,10,1,32,128]{4,0,3,2,1:T(4,128)(2,1)}, u32[]{:S(2)}, u32[]{:S(2)}) collective-permute-start(bf16[3,10,1,32,128]{4,0,3,2,1:T(4,128)(2,1)} %get-tuple-element.8), channel_id=1, source_target_pairs={{0,2},{2,4},{4,6},{1,3},{3,5},{5,7},{8,10},{10,12},{12,14},{9,11},... | collective-permute-start | bytes 737288 | tf_op jit(solution)/shard_map/ppermute | solution.py:15
  79.4 11.3 %collective-permute-start.7 = (bf16[3,10,1,32,128]{4,0,3,2,1:T(4,128)(2,1)}, bf16[3,10,1,32,128]{4,0,3,2,1:T(4,128)(2,1)}, u32[]{:S(2)}, u32[]{:S(2)}) collective-permute-start(bf16[3,10,1,32,128]{4,0,3,2,1:T(4,128)(2,1)} %get-tuple-element.9), channel_id=1, source_target_pairs={{2,0},{4,2},{6,4},{3,1},{5,3},{7,5},{10,8},{12,10},{14,12},{11,9},... | collective-permute-start | bytes 737288 | tf_op jit(solution)/shard_map/ppermute | solution.py:17
  117.8 30.2 %collective-permute-start.8 = (bf16[3,1,8,32,128]{4,2,3,0,1:T(8,128)(2,1)}, bf16[3,1,8,32,128]{4,2,3,0,1:T(8,128)(2,1)}, u32[]{:S(2)}, u32[]{:S(2)}) collective-permute-start(bf16[3,1,8,32,128]{4,2,3,0,1:T(8,128)(2,1)} %get-tuple-element.20), channel_id=1, source_target_pairs={{0,8},{8,16},{16,24},{1,9},{9,17},{17,25},{2,10},{10,18},{18,26},{... | collective-permute-start | bytes 589832 | tf_op jit(solution)/shard_map/ppermute | solution.py:15
  122.3 25.8 %collective-permute-start.9 = (bf16[3,1,8,32,128]{4,2,3,0,1:T(8,128)(2,1)}, bf16[3,1,8,32,128]{4,2,3,0,1:T(8,128)(2,1)}, u32[]{:S(2)}, u32[]{:S(2)}) collective-permute-start(bf16[3,1,8,32,128]{4,2,3,0,1:T(8,128)(2,1)} %get-tuple-element.21), channel_id=1, source_target_pairs={{8,0},{16,8},{24,16},{9,1},{17,9},{25,17},{10,2},{18,10},{26,18},{... | collective-permute-start | bytes 589832 | tf_op jit(solution)/shard_map/ppermute | solution.py:17
  150.8 9.3 %collective-permute-start.10 = (bf16[3,10,1,32,128]{4,2,3,0,1:T(2,128)(2,1)S(1)}, bf16[3,10,1,32,128]{4,2,3,0,1:T(2,128)(2,1)S(1)}, u32[]{:S(2)}, u32[]{:S(2)}) collective-permute-start(bf16[3,10,1,32,128]{4,2,3,0,1:T(2,128)(2,1)S(1)} %get-tuple-element.14), channel_id=1, source_target_pairs={{0,2},{2,4},{4,6},{1,3},{3,5},{5,7},{8,10},{10,12},{12,14},{9,11},... | collective-permute-start | bytes 737288 | tf_op jit(solution)/shard_map/ppermute | solution.py:15
  152.2 19.1 %collective-permute-start.11 = (bf16[3,10,1,32,128]{4,2,3,0,1:T(2,128)(2,1)S(1)}, bf16[3,10,1,32,128]{4,2,3,0,1:T(2,128)(2,1)S(1)}, u32[]{:S(2)}, u32[]{:S(2)}) collective-permute-start(bf16[3,10,1,32,128]{4,2,3,0,1:T(2,128)(2,1)S(1)} %get-tuple-element.15), channel_id=1, source_target_pairs={{2,0},{4,2},{6,4},{3,1},{5,3},{7,5},{10,8},{12,10},{14,12},{11,9},... | collective-permute-start | bytes 737288 | tf_op jit(solution)/shard_map/ppermute | solution.py:17
  154.5 79.2 %collective-permute-start.22 = (f32[1792,128]{1,0:T(8,128)}, f32[1792,128]{1,0:T(8,128)}, u32[]{:S(2)}, u32[]{:S(2)}) collective-permute-start(f32[1792,128]{1,0:T(8,128)} %constant_dynamic-slice_fusion.4), channel_id=1, source_target_pairs={{0,1},{1,0},{2,3},{3,2},{4,5},{5,4},{6,7},{7,6},{8,9},{9,8},{10,11... | collective-permute-start | bytes 2752520 | tf_op jit(solution)/shard_map/ppermute | solution.py:78
  233.7 15.7 %collective-permute-start.12 = (f32[1792,128]{1,0:T(8,128)}, f32[1792,128]{1,0:T(8,128)}, u32[]{:S(2)}, u32[]{:S(2)}) collective-permute-start(f32[1792,128]{1,0:T(8,128)} %constant_dynamic-slice_fusion.9), channel_id=1, source_target_pairs={{0,1},{1,0},{2,3},{3,2},{4,5},{5,4},{6,7},{7,6},{8,9},{9,8},{10,11... | collective-permute-start | bytes 2752520 | tf_op jit(solution)/shard_map/ppermute | solution.py:78
  235.8 12.4 %collective-permute-start.23 = (f32[896,128]{1,0:T(8,128)S(1)}, f32[896,128]{1,0:T(8,128)}, u32[]{:S(2)}, u32[]{:S(2)}) collective-permute-start(f32[896,128]{1,0:T(8,128)S(1)} %constant_dynamic-slice_fusion.3), channel_id=1, source_target_pairs={{0,4},{2,6},{4,0},{6,2},{1,5},{3,7},{5,1},{7,3},{8,12},{10,14},{12... | collective-permute-start | bytes 1376264 | tf_op jit(solution)/shard_map/ppermute | solution.py:78
  249.3 6.5 %collective-permute-start.24 = (f32[448,128]{1,0:T(8,128)S(1)}, f32[448,128]{1,0:T(8,128)S(1)}, u32[]{:S(2)}, u32[]{:S(2)}) collective-permute-start(f32[448,128]{1,0:T(8,128)S(1)} %constant_dynamic-slice_fusion.2), channel_id=1, source_target_pairs={{0,2},{2,0},{4,6},{6,4},{1,3},{3,1},{5,7},{7,5},{8,10},{10,8},{12,... | collective-permute-start | bytes 688136 | tf_op jit(solution)/shard_map/ppermute | solution.py:78
  250.7 13.4 %collective-permute-start.13 = (f32[896,128]{1,0:T(8,128)S(1)}, f32[896,128]{1,0:T(8,128)S(1)}, u32[]{:S(2)}, u32[]{:S(2)}) collective-permute-start(f32[896,128]{1,0:T(8,128)S(1)} %constant_dynamic-slice_fusion.8), channel_id=1, source_target_pairs={{0,4},{2,6},{4,0},{6,2},{1,5},{3,7},{5,1},{7,3},{8,12},{10,14},{12... | collective-permute-start | bytes 1376264 | tf_op jit(solution)/shard_map/ppermute | solution.py:78
  255.8 5.8 %collective-permute-start.25 = (f32[224,128]{1,0:T(8,128)S(1)}, f32[224,128]{1,0:T(8,128)S(1)}, u32[]{:S(2)}, u32[]{:S(2)}) collective-permute-start(f32[224,128]{1,0:T(8,128)S(1)} %constant_dynamic-slice_fusion.1), channel_id=1, source_target_pairs={{0,16},{8,24},{16,0},{24,8},{1,17},{9,25},{17,1},{25,9},{2,18},{10... | collective-permute-start | bytes 344072 | tf_op jit(solution)/shard_map/ppermute | solution.py:78
  261.7 4.7 %collective-permute-start.26 = (f32[112,128]{1,0:T(8,128)S(1)}, f32[112,128]{1,0:T(8,128)S(1)}, u32[]{:S(2)}, u32[]{:S(2)}) collective-permute-start(f32[112,128]{1,0:T(8,128)S(1)} %constant_dynamic-slice_fusion), channel_id=1, source_target_pairs={{0,8},{8,0},{16,24},{24,16},{1,9},{9,1},{17,25},{25,17},{2,10},{10... | collective-permute-start | bytes 172040 | tf_op jit(solution)/shard_map/ppermute | solution.py:78
  264.1 6.1 %collective-permute-start.14 = (f32[448,128]{1,0:T(8,128)S(1)}, f32[448,128]{1,0:T(8,128)S(1)}, u32[]{:S(2)}, u32[]{:S(2)}) collective-permute-start(f32[448,128]{1,0:T(8,128)S(1)} %constant_dynamic-slice_fusion.7), channel_id=1, source_target_pairs={{0,2},{2,0},{4,6},{6,4},{1,3},{3,1},{5,7},{7,5},{8,10},{10,8},{12,... | collective-permute-start | bytes 688136 | tf_op jit(solution)/shard_map/ppermute | solution.py:78
  266.4 6.5 %collective-permute-start.27 = (f32[112,128]{1,0:T(8,128)S(1)}, f32[112,128]{1,0:T(8,128)S(1)}, u32[]{:S(2)}, u32[]{:S(2)}) collective-permute-start(f32[112,128]{1,0:T(8,128)S(1)} %dynamic-slice_add_fusion.8), channel_id=1, source_target_pairs={{0,8},{8,0},{16,24},{24,16},{1,9},{9,1},{17,25},{25,17},{2,10},{10... | collective-permute-start | bytes 172040 | tf_op jit(solution)/shard_map/ppermute | solution.py:82
  270.3 9.2 %collective-permute-start.15 = (f32[224,128]{1,0:T(8,128)S(1)}, f32[224,128]{1,0:T(8,128)S(1)}, u32[]{:S(2)}, u32[]{:S(2)}) collective-permute-start(f32[224,128]{1,0:T(8,128)S(1)} %constant_dynamic-slice_fusion.6), channel_id=1, source_target_pairs={{0,16},{8,24},{16,0},{24,8},{1,17},{9,25},{17,1},{25,9},{2,18},{10... | collective-permute-start | bytes 344072 | tf_op jit(solution)/shard_map/ppermute | solution.py:78
  279.5 4.8 %collective-permute-start.16 = (f32[112,128]{1,0:T(8,128)S(1)}, f32[112,128]{1,0:T(8,128)S(1)}, u32[]{:S(2)}, u32[]{:S(2)}) collective-permute-start(f32[112,128]{1,0:T(8,128)S(1)} %constant_dynamic-slice_fusion.5), channel_id=1, source_target_pairs={{0,8},{8,0},{16,24},{24,16},{1,9},{9,1},{17,25},{25,17},{2,10},{10... | collective-permute-start | bytes 172040 | tf_op jit(solution)/shard_map/ppermute | solution.py:78
  279.6 8.2 %collective-permute-start.28 = (f32[224,128]{1,0:T(8,128)S(1)}, f32[224,128]{1,0:T(8,128)S(1)}, u32[]{:S(2)}, u32[]{:S(2)}) collective-permute-start(f32[224,128]{1,0:T(8,128)S(1)} %pad_maximum_fusion.17), channel_id=1, source_target_pairs={{0,16},{8,24},{16,0},{24,8},{1,17},{9,25},{17,1},{25,9},{2,18},{10... | collective-permute-start | bytes 344072 | tf_op jit(solution)/shard_map/ppermute | solution.py:82
  284.3 4.2 %collective-permute-start.17 = (f32[112,128]{1,0:T(8,128)S(1)}, f32[112,128]{1,0:T(8,128)S(1)}, u32[]{:S(2)}, u32[]{:S(2)}) collective-permute-start(f32[112,128]{1,0:T(8,128)S(1)} %dynamic-slice_add_fusion.9), channel_id=1, source_target_pairs={{0,8},{8,0},{16,24},{24,16},{1,9},{9,1},{17,25},{25,17},{2,10},{10... | collective-permute-start | bytes 172040 | tf_op jit(solution)/shard_map/ppermute | solution.py:82
  288.6 6.4 %collective-permute-start.18 = (f32[224,128]{1,0:T(8,128)S(1)}, f32[224,128]{1,0:T(8,128)S(1)}, u32[]{:S(2)}, u32[]{:S(2)}) collective-permute-start(f32[224,128]{1,0:T(8,128)S(1)} %pad_maximum_fusion.16), channel_id=1, source_target_pairs={{0,16},{8,24},{16,0},{24,8},{1,17},{9,25},{17,1},{25,9},{2,18},{10... | collective-permute-start | bytes 344072 | tf_op jit(solution)/shard_map/ppermute | solution.py:82
  289.2 6.1 %collective-permute-start.29 = (f32[448,128]{1,0:T(8,128)S(1)}, f32[448,128]{1,0:T(8,128)S(1)}, u32[]{:S(2)}, u32[]{:S(2)}) collective-permute-start(f32[448,128]{1,0:T(8,128)S(1)} %pad_maximum_fusion.15), channel_id=1, source_target_pairs={{0,2},{2,0},{4,6},{6,4},{1,3},{3,1},{5,7},{7,5},{8,10},{10,8},{12,... | collective-permute-start | bytes 688136 | tf_op jit(solution)/shard_map/ppermute | solution.py:82
  295.1 6.1 %collective-permute-start.19 = (f32[448,128]{1,0:T(8,128)S(1)}, f32[448,128]{1,0:T(8,128)S(1)}, u32[]{:S(2)}, u32[]{:S(2)}) collective-permute-start(f32[448,128]{1,0:T(8,128)S(1)} %pad_maximum_fusion.14), channel_id=1, source_target_pairs={{0,2},{2,0},{4,6},{6,4},{1,3},{3,1},{5,7},{7,5},{8,10},{10,8},{12,... | collective-permute-start | bytes 688136 | tf_op jit(solution)/shard_map/ppermute | solution.py:82
  295.3 10.6 %collective-permute-start.30 = (f32[896,128]{1,0:T(8,128)S(1)}, f32[896,128]{1,0:T(8,128)S(1)}, u32[]{:S(2)}, u32[]{:S(2)}) collective-permute-start(f32[896,128]{1,0:T(8,128)S(1)} %pad_maximum_fusion.10), channel_id=1, source_target_pairs={{0,4},{2,6},{4,0},{6,2},{1,5},{3,7},{5,1},{7,3},{8,12},{10,14},{12... | collective-permute-start | bytes 1376264 | tf_op jit(solution)/shard_map/ppermute | solution.py:82
  302.0 9.0 %collective-permute-start.20 = (f32[896,128]{1,0:T(8,128)}, f32[896,128]{1,0:T(8,128)}, u32[]{:S(2)}, u32[]{:S(2)}) collective-permute-start(f32[896,128]{1,0:T(8,128)} %pad_maximum_fusion.9), channel_id=1, source_target_pairs={{0,4},{2,6},{4,0},{6,2},{1,5},{3,7},{5,1},{7,3},{8,12},{10,14},{12... | collective-permute-start | bytes 1376264 | tf_op jit(solution)/shard_map/ppermute | solution.py:82
  306.1 6.1 %collective-permute-start.31 = (f32[1792,128]{1,0:T(8,128)S(1)}, f32[1792,128]{1,0:T(8,128)S(1)}, u32[]{:S(2)}, u32[]{:S(2)}) collective-permute-start(f32[1792,128]{1,0:T(8,128)S(1)} %pad_maximum_fusion.5), channel_id=1, source_target_pairs={{0,1},{1,0},{2,3},{3,2},{4,5},{5,4},{6,7},{7,6},{8,9},{9,8},{10,11... | collective-permute-start | bytes 2752520 | tf_op jit(solution)/shard_map/ppermute | solution.py:82
  312.1 2.5 collective-permute-start.21
  (17 other events, 150.9 us)

commit v2 on v1

--- a/solution.py
+++ b/solution.py
@@ -4,21 +4,49 @@
 from jax.sharding import PartitionSpec as P
 
 
-def extended(cells, sides, width):
-    for axis, dim in sides:
-        count = lax.axis_size(axis)
-        ends = count - 1
-        head = lax.slice_in_dim(cells, 0, width, axis=dim)
-        tail = lax.slice_in_dim(cells, cells.shape[dim] - width, cells.shape[dim], axis=dim)
-        cells = jnp.concatenate(
-            [
-                lax.ppermute(tail, axis, [(i, (i + 1) % count) for i in range(ends)]),
-                cells,
-                lax.ppermute(head, axis, [((i + 1) % count, i) for i in range(ends)]),
-            ],
-            axis=dim,
-        )
-    return cells
+def neighbour_piece(cells, dx, dy):
+    rows = cells.shape[1]
+    cols = cells.shape[2]
+    piece = cells
+    if dx:
+        start = rows - 1 if dx < 0 else 0
+        piece = lax.slice_in_dim(piece, start, start + 1, axis=1)
+    if dy:
+        start = cols - 1 if dy < 0 else 0
+        piece = lax.slice_in_dim(piece, start, start + 1, axis=2)
+    nx = lax.axis_size("gx")
+    ny = lax.axis_size("gy")
+    pairs = []
+    for i in range(nx):
+        for j in range(ny):
+            si, sj = i + dx, j + dy
+            if 0 <= si < nx and 0 <= sj < ny:
+                if dx and dy:
+                    pairs.append((si * ny + sj, i * ny + j))
+                elif dx:
+                    if j == 0:
+                        pairs.append((si, i))
+                else:
+                    if i == 0:
+                        pairs.append((sj, j))
+    if dx and dy:
+        axis = ("gx", "gy")
+    elif dx:
+        axis = "gx"
+    else:
+        axis = "gy"
+    return lax.ppermute(piece, axis, pairs)
+
+
+def extended(cells):
+    got = {}
+    for dx in (-1, 0, 1):
+        for dy in (-1, 0, 1):
+            if dx or dy:
+                got[dx, dy] = neighbour_piece(cells, dx, dy)
+    got[0, 0] = cells
+    bands = [jnp.concatenate([got[dx, dy] for dy in (-1, 0, 1)], axis=2) for dx in (-1, 0, 1)]
+    return jnp.concatenate(bands, axis=1)
 
 
 def conv_block(padded, kernel):
@@ -95,15 +123,15 @@
     layout = volumes.shape
     depth = layout[4]
     flipped = jnp.transpose(weight_two[::-1], (0, 2, 1))
-    rim_input = extended(volumes, (("gx", 1), ("gy", 2)), 1)
+    rim_input = extended(volumes)
     act_one = lax.optimization_barrier(conv_block(rim_input, weight_one))
     hidden = jax.nn.silu(act_one).astype(jnp.bfloat16)
-    rim_hidden = extended(hidden, (("gx", 1), ("gy", 2)), 1)
+    rim_hidden = extended(hidden)
     act_two = conv_block(rim_hidden, weight_two)
     features = jax.nn.silu(act_two).astype(jnp.bfloat16)
     delta_two = (cotangent.astype(jnp.float32) * swish_slope(act_two)).astype(jnp.bfloat16)
     grad_two = weight_grad(rim_hidden, delta_two)
-    rim_delta = extended(delta_two, (("gx", 1), ("gy", 2)), 1)
+    rim_delta = extended(delta_two)
     back_grad = conv_block(rim_delta, flipped)
     delta_one = (back_grad * swish_slope(act_one)).astype(jnp.bfloat16)
     grad_one = weight_grad(rim_input, delta_one)

time: 320 us -> 354 us (1.11)
  starting transfers between devices: 43 us -> 84.9 us
  waiting for transfers between devices: 107 us -> 101 us
  matrix products: 105 us -> 100 us
  local copies, waits for them, and re-layouts: 29.8 us -> 34.4 us
    ppermute x12 -> x24, starting transfers between devices: 30 us -> 68.8 us  [neighbour_piece(): return lax.ppermute(piece, axis, pairs)]
    ppermute x12 -> x24, waiting for transfers between devices: 51.4 us -> 44.8 us  [neighbour_piece(): return lax.ppermute(piece, axis, pairs)]
    conv_general_dilated x2, matrix products: 51.6 us -> 47.1 us  [kernel_grad(): lax.conv_general_dilated(padded, delta_field, (1, 1, 1), ((0, 0), (0, 0),...]
    conv_general_dilated x0 -> x1, other arithmetic: none -> 4.08 us  [kernel_grad(): lax.conv_general_dilated(padded, delta_field, (1, 1, 1), ((0, 0), (0, 0),...]
    slice x2 -> x0, other arithmetic: 4.02 us -> none  [extended(): lax.slice_in_dim(cells, cells.shape[dim] - width, cells.shape[dim], axis=...]
    unnamed x40 -> x77, local copies, waits for them, and re-layouts: 10.7 us -> 12 us
  transfers between devices with their start and end apart: 32 -> 44, of which waited for: 25 -> 21; matrix products, arithmetic and copies ran while one was open for 32% -> 20% of each run, Pallas kernels for 0% -> 0%
where the time goes in v2:
time: 354 us; the launch traced here: 350 us
  waiting for transfers between devices  101 us (29%)
  matrix products  100 us (28%)
  starting transfers between devices  84.9 us (24%)
  local copies, waits for them, and re-layouts  34.4 us (10%)
  other arithmetic  28 us (8%)
    ppermute x24, starting transfers between devices, neighbour_piece(): return lax.ppermute(piece, axis, pairs)  68.8 us
    conv_general_dilated x3, matrix products, conv_block(): lax.conv_general_dilated(padded, cube_kernel, (1, 1, 1), ((0, 0), (0, 0),...  53.1 us
    conv_general_dilated x2, matrix products, kernel_grad(): lax.conv_general_dilated(padded, delta_field, (1, 1, 1), ((0, 0), (0, 0),...  47.1 us
    ppermute x24, waiting for transfers between devices, neighbour_piece(): return lax.ppermute(piece, axis, pairs)  44.8 us
    ppermute x10, waiting for transfers between devices, tree_sum(): rows = keep + lax.ppermute(send, axis, pairs)  34 us
    ppermute x10, waiting for transfers between devices, tree_sum(): other = lax.ppermute(rows, axis, pairs)  21.8 us
    unnamed x77, local copies, waits for them, and re-layouts  12 us
    concatenate x3, other arithmetic, extended(): return jnp.concatenate(bands, axis=1)  9.7 us
  transfers between devices with their start and end apart: 44, of which 21 were waited for; matrix products, arithmetic and copies ran while one was open for 20% of the time, Pallas kernels for 0%

profile of v2, /device:TPU:0, one launch (start us, length us, event | category | flops | bytes accessed | tf_op | source)
XLA Modules:
  0.0 350.1 jit_solution(6205346425965929931)
XLA Ops:
  0.6 2.8 copy.23
  3.7 4.9 %collective-permute-start.1 = (bf16[3,1,8,32,128]{4,0,3,2,1:T(4,128)(2,1)S(1)}, bf16[3,1,8,32,128]{4,0,3,2,1:T(4,128)(2,1)S(1)}, u32[]{:S(2)}, u32[]{:S(2)}) collective-permute-start(bf16[3,1,8,32,128]{4,0,3,2,1:T(4,128)(2,1)S(1)} %get-tuple-element.20), channel_id=1, source_target_pairs={{0,8},{8,16},{16,24},{1,9},{9,17},{17,25},{2,10},{10,18},{18,26},{... | collective-permute-start | bytes 589832 | tf_op jit(solution)/shard_map/ppermute | solution.py:38
  8.9 3.4 collective-permute-start.3
  14.9 6.6 %collective-permute-start = (bf16[3,1,1,32,128]{4,0,3,2,1:T(4,128)(2,1)S(1)}, bf16[3,1,1,32,128]{4,0,3,2,1:T(4,128)(2,1)S(1)}, u32[]{:S(2)}, u32[]{:S(2)}) collective-permute-start(bf16[3,1,1,32,128]{4,0,3,2,1:T(4,128)(2,1)S(1)} %get-tuple-element.16), channel_id=1, source_target_pairs={{0,10},{2,12},{4,14},{8,18},{10,20},{12,22},{16,26},{18,28},{20,30... | collective-permute-start | bytes 73736 | tf_op jit(solution)/shard_map/ppermute | solution.py:38
  26.3 18.3 %collective-permute-done.7 = bf16[3,1,1,32,128]{4,0,3,2,1:T(4,128)(2,1)S(1)} collective-permute-done((bf16[3,1,1,32,128]{4,0,3,2,1:T(4,128)(2,1)S(1)}, bf16[3,1,1,32,128]{4,0,3,2,1:T(4,128)(2,1)S(1)}, u32[]{:S(2)}, u32[]{:S(2)}) %collective-permute-start.7) | collective-permute-done | bytes 24608 | tf_op jit(solution)/shard_map/ppermute | solution.py:38
  46.3 2.8 fusion.57
  51.8 15.5 %broadcast_select_fusion.1 = f32[8,8,24,5,128]{4,2,3,1,0:T(8,128)S(1)} fusion(pred[24,5]{0,1:T(8,128)(4,1)S(1)} %copy-done.35, bf16[3,3,3,128,128]{4,3,2,1,0:T(8,128)(2,1)S(1)} %bitcast.72, bf16[10,10,3,7,2,128]{5,3,2,4,1,0:T(8,128)(2,1)S(1)} %slice.145, bf16[10,10,3,8,5,128]{5,3,2,4,1,0:T(8,128)(2,1)S(1)} %copy.33), kind=kOutput, calls=%fused_computation.42 | convolution fusion | flops 6808657920 | bytes 8964216 | tf_op jit(solution)/shard_map/conv_general_dilated | solution.py:55
  75.1 5.1 %collective-permute-start.11 = (bf16[3,8,1,32,128]{4,0,3,2,1:T(4,128)(2,1)}, bf16[3,8,1,32,128]{4,0,3,2,1:T(4,128)(2,1)S(1)}, u32[]{:S(2)}, u32[]{:S(2)}) collective-permute-start(bf16[3,8,1,32,128]{4,0,3,2,1:T(4,128)(2,1)} %get-tuple-element.14), channel_id=1, source_target_pairs={{0,2},{2,4},{4,6},{1,3},{3,5},{5,7},{8,10},{10,12},{12,14},{9,11},... | collective-permute-start | bytes 589832 | tf_op jit(solution)/shard_map/ppermute | solution.py:38
  82.8 5.3 %collective-permute-start.9 = (bf16[3,1,8,32,128]{4,0,3,2,1:T(4,128)(2,1)}, bf16[3,1,8,32,128]{4,0,3,2,1:T(4,128)(2,1)}, u32[]{:S(2)}, u32[]{:S(2)}) collective-permute-start(bf16[3,1,8,32,128]{4,0,3,2,1:T(4,128)(2,1)} %get-tuple-element.12), channel_id=1, source_target_pairs={{0,8},{8,16},{16,24},{1,9},{9,17},{17,25},{2,10},{10,18},{18,26},{... | collective-permute-start | bytes 589832 | tf_op jit(solution)/shard_map/ppermute | solution.py:38
  92.0 18.0 %collective-permute-done.15 = bf16[3,1,1,32,128]{4,0,3,2,1:T(4,128)(2,1)} collective-permute-done((bf16[3,1,1,32,128]{4,0,3,2,1:T(4,128)(2,1)S(1)}, bf16[3,1,1,32,128]{4,0,3,2,1:T(4,128)(2,1)}, u32[]{:S(2)}, u32[]{:S(2)}) %collective-permute-start.15) | collective-permute-done | bytes 24608 | tf_op jit(solution)/shard_map/ppermute | solution.py:38
  110.0 7.0 %collective-permute-start.8 = (bf16[3,1,1,32,128]{4,0,3,2,1:T(4,128)(2,1)}, bf16[3,1,1,32,128]{4,0,3,2,1:T(4,128)(2,1)}, u32[]{:S(2)}, u32[]{:S(2)}) collective-permute-start(bf16[3,1,1,32,128]{4,0,3,2,1:T(4,128)(2,1)} %get-tuple-element.8), channel_id=1, source_target_pairs={{0,10},{2,12},{4,14},{8,18},{10,20},{12,22},{16,26},{18,28},{20,30... | collective-permute-start | bytes 73736 | tf_op jit(solution)/shard_map/ppermute | solution.py:38
  118.3 4.0 %fusion.56 = bf16[10,10,3,32,128]{4,2,3,1,0:T(4,128)(2,1)S(1)} fusion(bf16[3,1,1,32,128]{4,0,3,2,1:T(4,128)(2,1)} %collective-permute-done.15, bf16[3,1,8,32,128]{4,0,3,2,1:T(4,128)(2,1)} %collective-permute-done.14, bf16[3,1,1,32,128]{4,0,3,2,1:T(4,128)(2,1)} %collective-permute-done.13, bf16[3,8,1,32,128]{4,0,3,2,1:T(4,128)(2,1)S(1)} %collective-permute-done.12, ...), kind=kLoop, calls=%fused_computation.112 | loop fusion | flops 9830400 | bytes 4915200 | tf_op jit(solution)/shard_map/concatenate | solution.py:49
  124.9 17.2 %add_multiply_fusion = (f32[8,8,24,5,128]{4,2,3,1,0:T(8,128)S(1)}, bf16[8,8,24,5,128]{4,2,3,1,0:T(8,128)(2,1)}) fusion(pred[24,5]{0,1:T(8,128)(4,1)S(1)} %copy-done.35, bf16[3,3,3,128,128]{4,3,2,1,0:T(8,128)(2,1)S(1)} %bitcast.86, bf16[10,10,3,7,2,128]{5,3,2,4,1,0:T(8,128)(2,1)S(1)} %slice.155, bf16[10,10,3,8,5,128]{5,3,2,4,1,0:T(8,128)(2,1)S(1)} %copy.37), kind=kOutput, calls=%fused_computation.28 | convolution fusion | flops 6817505280 | bytes 10930296 | tf_op jit(solution)/shard_map/conv_general_dilated | solution.py:55
  147.1 24.4 %fusion.27 = f32[3,3,3,128,128]{4,3,2,1,0:T(8,128)S(1)} fusion(bf16[3,8,8,32,128]{4,2,3,0,1:T(8,128)(2,1)S(1)} %fusion.24, bf16[3,1,1,32,128]{4,0,3,2,1:T(4,128)(2,1)} %collective-permute-done.15, bf16[3,1,8,32,128]{4,0,3,2,1:T(4,128)(2,1)} %collective-permute-done.14, bf16[3,1,1,32,128]{4,0,3,2,1:T(4,128)(2,1)} %collective-permute-done.13, ...), kind=kOutput, calls=%fused_computation.38 | convolution fusion | flops 5344690176 | bytes 5799936 | tf_op jit(solution)/shard_map/conv_general_dilated | solution.py:67
  171.7 5.3 %collective-permute-start.16 = (bf16[3,1,1,32,128]{4,2,3,0,1:T(2,128)(2,1)S(1)}, bf16[3,1,1,32,128]{4,2,3,0,1:T(2,128)(2,1)S(1)}, u32[]{:S(2)}, u32[]{:S(2)}) collective-permute-start(bf16[3,1,1,32,128]{4,2,3,0,1:T(2,128)(2,1)S(1)} %copy-done.26), channel_id=1, source_target_pairs={{0,10},{2,12},{4,14},{8,18},{10,20},{12,22},{16,26},{18,28},{20,30... | collective-permute-start | bytes 73736 | tf_op jit(solution)/shard_map/ppermute | solution.py:38
  178.4 6.7 %collective-permute-start.19 = (bf16[3,8,1,32,128]{4,2,3,0,1:T(2,128)(2,1)S(1)}, bf16[3,8,1,32,128]{4,2,3,0,1:T(2,128)(2,1)S(1)}, u32[]{:S(2)}, u32[]{:S(2)}) collective-permute-start(bf16[3,8,1,32,128]{4,2,3,0,1:T(2,128)(2,1)S(1)} %copy-done.14), channel_id=1, source_target_pairs={{0,2},{2,4},{4,6},{1,3},{3,5},{5,7},{8,10},{10,12},{12,14},{9,11},... | collective-permute-start | bytes 589832 | tf_op jit(solution)/shard_map/ppermute | solution.py:38
  186.5 7.8 %collective-permute-start.17 = (bf16[3,1,8,32,128]{4,2,3,0,1:T(8,128)(2,1)S(1)}, bf16[3,1,8,32,128]{4,2,3,0,1:T(8,128)(2,1)S(1)}, u32[]{:S(2)}, u32[]{:S(2)}) collective-permute-start(bf16[3,1,8,32,128]{4,2,3,0,1:T(8,128)(2,1)S(1)} %get-tuple-element.32), channel_id=1, source_target_pairs={{0,8},{8,16},{16,24},{1,9},{9,17},{17,25},{2,10},{10,18},{18,26},{... | collective-permute-start | bytes 589832 | tf_op jit(solution)/shard_map/ppermute | solution.py:38
  197.9 6.6 %collective-permute-done.23 = bf16[3,1,1,32,128]{4,2,3,0,1:T(2,128)(2,1)S(1)} collective-permute-done((bf16[3,1,1,32,128]{4,2,3,0,1:T(2,128)(2,1)S(1)}, bf16[3,1,1,32,128]{4,2,3,0,1:T(2,128)(2,1)S(1)}, u32[]{:S(2)}, u32[]{:S(2)}) %collective-permute-start.23) | collective-permute-done | bytes 24608 | tf_op jit(solution)/shard_map/ppermute | solution.py:38
  204.5 2.9 maximum_bitcast_fusion
  210.8 2.8 fusion.3
  213.6 20.3 %broadcast_select_fusion = f32[8,8,24,5,128]{4,2,3,1,0:T(8,128)S(1)} fusion(pred[24,5]{0,1:T(8,128)(4,1)S(1)} %copy-done.36, bf16[3,3,3,128,128]{3,4,2,1,0:T(8,128)(2,1)S(1)} %bitcast.87, bf16[10,10,3,8,7,128]{5,4,3,2,1,0:T(8,128)(2,1)S(1)} %fusion.3), kind=kOutput, calls=%fused_computation.41 | convolution fusion | flops 6795755520 | bytes 9117816 | tf_op jit(solution)/shard_map/conv_general_dilated | solution.py:55
  236.9 4.1 %fusion.64 = bf16[3,8,8,32,128]{4,0,3,2,1:T(4,128)(2,1)S(1)} fusion(f32[8,8,3,32,128]{4,1,3,2,0:T(8,128)S(1)} %slice.167, f32[3,8,8,32,128]{4,0,3,2,1:T(4,128)S(1)} %bitcast.74), kind=kLoop, calls=%fused_computation.23.clone.clone.2 | loop fusion | flops 7077888 | bytes 7864320 | tf_op jit(solution)/shard_map/conv_general_dilated | solution.py:67
  241.0 22.7 %fusion.29 = f32[3,3,3,128,128]{4,3,2,1,0:T(8,128)S(1)} fusion(bf16[3,1,1,32,128]{4,0,3,2,1:T(4,128)(2,1)S(1)} %copy-done.34, bf16[3,1,8,32,128]{4,0,3,2,1:T(4,128)(2,1)S(1)} %copy-done.22, bf16[3,1,1,32,128]{4,0,3,2,1:T(4,128)(2,1)S(1)} %copy-done.32, bf16[3,8,1,32,128]{4,0,3,2,1:T(4,128)(2,1)S(1)} %copy-done.20, ...), kind=kOutput, calls=%fused_computation.40 | convolution fusion | flops 5344690176 | bytes 5799936 | tf_op jit(solution)/shard_map/conv_general_dilated | solution.py:67
  270.3 10.3 %collective-permute-done.35 = f32[896,128]{1,0:T(8,128)S(1)} collective-permute-done((f32[896,128]{1,0:T(8,128)S(1)}, f32[896,128]{1,0:T(8,128)S(1)}, u32[]{:S(2)}, u32[]{:S(2)}) %collective-permute-start.35) | collective-permute-done | bytes 458784 | tf_op jit(solution)/shard_map/ppermute | solution.py:106
  282.6 4.7 %collective-permute-done.36 = f32[448,128]{1,0:T(8,128)S(1)} collective-permute-done((f32[448,128]{1,0:T(8,128)S(1)}, f32[448,128]{1,0:T(8,128)S(1)}, u32[]{:S(2)}, u32[]{:S(2)}) %collective-permute-start.36) | collective-permute-done | bytes 229408 | tf_op jit(solution)/shard_map/ppermute | solution.py:106
  289.4 4.3 %collective-permute-done.25 = f32[896,128]{1,0:T(8,128)S(1)} collective-permute-done((f32[896,128]{1,0:T(8,128)S(1)}, f32[896,128]{1,0:T(8,128)S(1)}, u32[]{:S(2)}, u32[]{:S(2)}) %collective-permute-start.25) | collective-permute-done | bytes 458784 | tf_op jit(solution)/shard_map/ppermute | solution.py:106
  303.5 7.5 %collective-permute-done.27 = f32[224,128]{1,0:T(8,128)S(1)} collective-permute-done((f32[224,128]{1,0:T(8,128)S(1)}, f32[224,128]{1,0:T(8,128)S(1)}, u32[]{:S(2)}, u32[]{:S(2)}) %collective-permute-start.27) | collective-permute-done | bytes 114720 | tf_op jit(solution)/shard_map/ppermute | solution.py:106
  311.4 3.9 %collective-permute-done.28 = f32[112,128]{1,0:T(8,128)S(1)} collective-permute-done((f32[112,128]{1,0:T(8,128)S(1)}, f32[112,128]{1,0:T(8,128)S(1)}, u32[]{:S(2)}, u32[]{:S(2)}) %collective-permute-start.28) | collective-permute-done | bytes 57376 | tf_op jit(solution)/shard_map/ppermute | solution.py:106
  315.7 4.5 %collective-permute-done.40 = f32[224,128]{1,0:T(8,128)S(1)} collective-permute-done((f32[224,128]{1,0:T(8,128)S(1)}, f32[224,128]{1,0:T(8,128)S(1)}, u32[]{:S(2)}, u32[]{:S(2)}) %collective-permute-start.40) | collective-permute-done | bytes 114720 | tf_op jit(solution)/shard_map/ppermute | solution.py:110
  322.2 4.5 %collective-permute-done.30 = f32[224,128]{1,0:T(8,128)S(1)} collective-permute-done((f32[224,128]{1,0:T(8,128)S(1)}, f32[224,128]{1,0:T(8,128)S(1)}, u32[]{:S(2)}, u32[]{:S(2)}) %collective-permute-start.30) | collective-permute-done | bytes 114720 | tf_op jit(solution)/shard_map/ppermute | solution.py:110
  328.9 3.9 %collective-permute-done.31 = f32[448,128]{1,0:T(8,128)S(1)} collective-permute-done((f32[448,128]{1,0:T(8,128)S(1)}, f32[448,128]{1,0:T(8,128)S(1)}, u32[]{:S(2)}, u32[]{:S(2)}) %collective-permute-start.31) | collective-permute-done | bytes 229408 | tf_op jit(solution)/shard_map/ppermute | solution.py:110
  333.7 6.1 %collective-permute-done.42 = f32[896,128]{1,0:T(8,128)S(1)} collective-permute-done((f32[896,128]{1,0:T(8,128)S(1)}, f32[896,128]{1,0:T(8,128)S(1)}, u32[]{:S(2)}, u32[]{:S(2)}) %collective-permute-start.42) | collective-permute-done | bytes 458784 | tf_op jit(solution)/shard_map/ppermute | solution.py:110
  (213 shorter events, 83.9 us)
Async XLA Ops:
  3.7 40.9 %collective-permute-start.1 = (bf16[3,1,8,32,128]{4,0,3,2,1:T(4,128)(2,1)S(1)}, bf16[3,1,8,32,128]{4,0,3,2,1:T(4,128)(2,1)S(1)}, u32[]{:S(2)}, u32[]{:S(2)}) collective-permute-start(bf16[3,1,8,32,128]{4,0,3,2,1:T(4,128)(2,1)S(1)} %get-tuple-element.20), channel_id=1, source_target_pairs={{0,8},{8,16},{16,24},{1,9},{9,17},{17,25},{2,10},{10,18},{18,26},{... | collective-permute-start | bytes 589832 | tf_op jit(solution)/shard_map/ppermute | solution.py:38
  8.9 35.8 %collective-permute-start.3 = (bf16[3,8,1,32,128]{4,0,3,2,1:T(4,128)(2,1)S(1)}, bf16[3,8,1,32,128]{4,0,3,2,1:T(4,128)(2,1)S(1)}, u32[]{:S(2)}, u32[]{:S(2)}) collective-permute-start(bf16[3,8,1,32,128]{4,0,3,2,1:T(4,128)(2,1)S(1)} %get-tuple-element.22), channel_id=1, source_target_pairs={{0,2},{2,4},{4,6},{1,3},{3,5},{5,7},{8,10},{10,12},{12,14},{9,11},... | collective-permute-start | bytes 589832 | tf_op jit(solution)/shard_map/ppermute | solution.py:38
  12.3 32.4 %collective-permute-start.4 = (bf16[3,8,1,32,128]{4,0,3,2,1:T(4,128)(2,1)S(1)}, bf16[3,8,1,32,128]{4,0,3,2,1:T(4,128)(2,1)S(1)}, u32[]{:S(2)}, u32[]{:S(2)}) collective-permute-start(bf16[3,8,1,32,128]{4,0,3,2,1:T(4,128)(2,1)S(1)} %get-tuple-element.23), channel_id=1, source_target_pairs={{2,0},{4,2},{6,4},{3,1},{5,3},{7,5},{10,8},{12,10},{14,12},{11,9},... | collective-permute-start | bytes 589832 | tf_op jit(solution)/shard_map/ppermute | solution.py:38
  13.6 31.1 %collective-permute-start.6 = (bf16[3,1,8,32,128]{4,0,3,2,1:T(4,128)(2,1)S(1)}, bf16[3,1,8,32,128]{4,0,3,2,1:T(4,128)(2,1)S(1)}, u32[]{:S(2)}, u32[]{:S(2)}) collective-permute-start(bf16[3,1,8,32,128]{4,0,3,2,1:T(4,128)(2,1)S(1)} %get-tuple-element.21), channel_id=1, source_target_pairs={{8,0},{16,8},{24,16},{9,1},{17,9},{25,17},{10,2},{18,10},{26,18},{... | collective-permute-start | bytes 589832 | tf_op jit(solution)/shard_map/ppermute | solution.py:38
  14.9 8.2 %collective-permute-start = (bf16[3,1,1,32,128]{4,0,3,2,1:T(4,128)(2,1)S(1)}, bf16[3,1,1,32,128]{4,0,3,2,1:T(4,128)(2,1)S(1)}, u32[]{:S(2)}, u32[]{:S(2)}) collective-permute-start(bf16[3,1,1,32,128]{4,0,3,2,1:T(4,128)(2,1)S(1)} %get-tuple-element.16), channel_id=1, source_target_pairs={{0,10},{2,12},{4,14},{8,18},{10,20},{12,22},{16,26},{18,28},{20,30... | collective-permute-start | bytes 73736 | tf_op jit(solution)/shard_map/ppermute | solution.py:38
  24.5 20.1 %collective-permute-start.7 = (bf16[3,1,1,32,128]{4,0,3,2,1:T(4,128)(2,1)S(1)}, bf16[3,1,1,32,128]{4,0,3,2,1:T(4,128)(2,1)S(1)}, u32[]{:S(2)}, u32[]{:S(2)}) collective-permute-start(bf16[3,1,1,32,128]{4,0,3,2,1:T(4,128)(2,1)S(1)} %get-tuple-element.17), channel_id=1, source_target_pairs={{10,0},{12,2},{14,4},{18,8},{20,10},{22,12},{26,16},{28,18},{30,20... | collective-permute-start | bytes 73736 | tf_op jit(solution)/shard_map/ppermute | solution.py:38
  75.1 43.2 %collective-permute-start.11 = (bf16[3,8,1,32,128]{4,0,3,2,1:T(4,128)(2,1)}, bf16[3,8,1,32,128]{4,0,3,2,1:T(4,128)(2,1)S(1)}, u32[]{:S(2)}, u32[]{:S(2)}) collective-permute-start(bf16[3,8,1,32,128]{4,0,3,2,1:T(4,128)(2,1)} %get-tuple-element.14), channel_id=1, source_target_pairs={{0,2},{2,4},{4,6},{1,3},{3,5},{5,7},{8,10},{10,12},{12,14},{9,11},... | collective-permute-start | bytes 589832 | tf_op jit(solution)/shard_map/ppermute | solution.py:38
  80.2 38.1 %collective-permute-start.12 = (bf16[3,8,1,32,128]{4,0,3,2,1:T(4,128)(2,1)}, bf16[3,8,1,32,128]{4,0,3,2,1:T(4,128)(2,1)S(1)}, u32[]{:S(2)}, u32[]{:S(2)}) collective-permute-start(bf16[3,8,1,32,128]{4,0,3,2,1:T(4,128)(2,1)} %get-tuple-element.15), channel_id=1, source_target_pairs={{2,0},{4,2},{6,4},{3,1},{5,3},{7,5},{10,8},{12,10},{14,12},{11,9},... | collective-permute-start | bytes 589832 | tf_op jit(solution)/shard_map/ppermute | solution.py:38
  81.5 36.8 %collective-permute-start.14 = (bf16[3,1,8,32,128]{4,0,3,2,1:T(4,128)(2,1)}, bf16[3,1,8,32,128]{4,0,3,2,1:T(4,128)(2,1)}, u32[]{:S(2)}, u32[]{:S(2)}) collective-permute-start(bf16[3,1,8,32,128]{4,0,3,2,1:T(4,128)(2,1)} %get-tuple-element.13), channel_id=1, source_target_pairs={{8,0},{16,8},{24,16},{9,1},{17,9},{25,17},{10,2},{18,10},{26,18},{... | collective-permute-start | bytes 589832 | tf_op jit(solution)/shard_map/ppermute | solution.py:38
  82.8 35.5 %collective-permute-start.9 = (bf16[3,1,8,32,128]{4,0,3,2,1:T(4,128)(2,1)}, bf16[3,1,8,32,128]{4,0,3,2,1:T(4,128)(2,1)}, u32[]{:S(2)}, u32[]{:S(2)}) collective-permute-start(bf16[3,1,8,32,128]{4,0,3,2,1:T(4,128)(2,1)} %get-tuple-element.12), channel_id=1, source_target_pairs={{0,8},{8,16},{16,24},{1,9},{9,17},{17,25},{2,10},{10,18},{18,26},{... | collective-permute-start | bytes 589832 | tf_op jit(solution)/shard_map/ppermute | solution.py:38
  90.7 19.3 %collective-permute-start.15 = (bf16[3,1,1,32,128]{4,0,3,2,1:T(4,128)(2,1)S(1)}, bf16[3,1,1,32,128]{4,0,3,2,1:T(4,128)(2,1)}, u32[]{:S(2)}, u32[]{:S(2)}) collective-permute-start(bf16[3,1,1,32,128]{4,0,3,2,1:T(4,128)(2,1)S(1)} %get-tuple-element.9), channel_id=1, source_target_pairs={{10,0},{12,2},{14,4},{18,8},{20,10},{22,12},{26,16},{28,18},{30,20... | collective-permute-start | bytes 73736 | tf_op jit(solution)/shard_map/ppermute | solution.py:38
  110.0 8.3 %collective-permute-start.8 = (bf16[3,1,1,32,128]{4,0,3,2,1:T(4,128)(2,1)}, bf16[3,1,1,32,128]{4,0,3,2,1:T(4,128)(2,1)}, u32[]{:S(2)}, u32[]{:S(2)}) collective-permute-start(bf16[3,1,1,32,128]{4,0,3,2,1:T(4,128)(2,1)} %get-tuple-element.8), channel_id=1, source_target_pairs={{0,10},{2,12},{4,14},{8,18},{10,20},{12,22},{16,26},{18,28},{20,30... | collective-permute-start | bytes 73736 | tf_op jit(solution)/shard_map/ppermute | solution.py:38
  171.7 14.7 %collective-permute-start.16 = (bf16[3,1,1,32,128]{4,2,3,0,1:T(2,128)(2,1)S(1)}, bf16[3,1,1,32,128]{4,2,3,0,1:T(2,128)(2,1)S(1)}, u32[]{:S(2)}, u32[]{:S(2)}) collective-permute-start(bf16[3,1,1,32,128]{4,2,3,0,1:T(2,128)(2,1)S(1)} %copy-done.26), channel_id=1, source_target_pairs={{0,10},{2,12},{4,14},{8,18},{10,20},{12,22},{16,26},{18,28},{20,30... | collective-permute-start | bytes 73736 | tf_op jit(solution)/shard_map/ppermute | solution.py:38
  177.0 17.3 %collective-permute-start.18 = (bf16[3,1,1,32,128]{4,2,3,0,1:T(2,128)(2,1)S(1)}, bf16[3,1,1,32,128]{4,2,3,0,1:T(2,128)(2,1)S(1)}, u32[]{:S(2)}, u32[]{:S(2)}) collective-permute-start(bf16[3,1,1,32,128]{4,2,3,0,1:T(2,128)(2,1)S(1)} %copy-done.25), channel_id=1, source_target_pairs={{2,8},{4,10},{6,12},{10,16},{12,18},{14,20},{18,24},{20,26},{22,28... | collective-permute-start | bytes 73736 | tf_op jit(solution)/shard_map/ppermute | solution.py:38
  177.7 17.9 %collective-permute-start.21 = (bf16[3,1,1,32,128]{4,2,3,0,1:T(2,128)(2,1)S(1)}, bf16[3,1,1,32,128]{4,2,3,0,1:T(2,128)(2,1)S(1)}, u32[]{:S(2)}, u32[]{:S(2)}) collective-permute-start(bf16[3,1,1,32,128]{4,2,3,0,1:T(2,128)(2,1)S(1)} %copy-done.24), channel_id=1, source_target_pairs={{8,2},{10,4},{12,6},{16,10},{18,12},{20,14},{24,18},{26,20},{28,22... | collective-permute-start | bytes 73736 | tf_op jit(solution)/shard_map/ppermute | solution.py:38
  178.4 26.1 %collective-permute-start.19 = (bf16[3,8,1,32,128]{4,2,3,0,1:T(2,128)(2,1)S(1)}, bf16[3,8,1,32,128]{4,2,3,0,1:T(2,128)(2,1)S(1)}, u32[]{:S(2)}, u32[]{:S(2)}) collective-permute-start(bf16[3,8,1,32,128]{4,2,3,0,1:T(2,128)(2,1)S(1)} %copy-done.14), channel_id=1, source_target_pairs={{0,2},{2,4},{4,6},{1,3},{3,5},{5,7},{8,10},{10,12},{12,14},{9,11},... | collective-permute-start | bytes 589832 | tf_op jit(solution)/shard_map/ppermute | solution.py:38
  185.2 19.3 %collective-permute-start.20 = (bf16[3,8,1,32,128]{4,2,3,0,1:T(2,128)(2,1)S(1)}, bf16[3,8,1,32,128]{4,2,3,0,1:T(2,128)(2,1)S(1)}, u32[]{:S(2)}, u32[]{:S(2)}) collective-permute-start(bf16[3,8,1,32,128]{4,2,3,0,1:T(2,128)(2,1)S(1)} %copy-done.13), channel_id=1, source_target_pairs={{2,0},{4,2},{6,4},{3,1},{5,3},{7,5},{10,8},{12,10},{14,12},{11,9},... | collective-permute-start | bytes 589832 | tf_op jit(solution)/shard_map/ppermute | solution.py:38
  186.5 18.0 %collective-permute-start.17 = (bf16[3,1,8,32,128]{4,2,3,0,1:T(8,128)(2,1)S(1)}, bf16[3,1,8,32,128]{4,2,3,0,1:T(8,128)(2,1)S(1)}, u32[]{:S(2)}, u32[]{:S(2)}) collective-permute-start(bf16[3,1,8,32,128]{4,2,3,0,1:T(8,128)(2,1)S(1)} %get-tuple-element.32), channel_id=1, source_target_pairs={{0,8},{8,16},{16,24},{1,9},{9,17},{17,25},{2,10},{10,18},{18,26},{... | collective-permute-start | bytes 589832 | tf_op jit(solution)/shard_map/ppermute | solution.py:38
  194.3 10.2 %collective-permute-start.22 = (bf16[3,1,8,32,128]{4,2,3,0,1:T(8,128)(2,1)S(1)}, bf16[3,1,8,32,128]{4,2,3,0,1:T(8,128)(2,1)S(1)}, u32[]{:S(2)}, u32[]{:S(2)}) collective-permute-start(bf16[3,1,8,32,128]{4,2,3,0,1:T(8,128)(2,1)S(1)} %get-tuple-element.33), channel_id=1, source_target_pairs={{8,0},{16,8},{24,16},{9,1},{17,9},{25,17},{10,2},{18,10},{26,18},{... | collective-permute-start | bytes 589832 | tf_op jit(solution)/shard_map/ppermute | solution.py:38
  195.6 8.8 %collective-permute-start.23 = (bf16[3,1,1,32,128]{4,2,3,0,1:T(2,128)(2,1)S(1)}, bf16[3,1,1,32,128]{4,2,3,0,1:T(2,128)(2,1)S(1)}, u32[]{:S(2)}, u32[]{:S(2)}) collective-permute-start(bf16[3,1,1,32,128]{4,2,3,0,1:T(2,128)(2,1)S(1)} %copy-done.23), channel_id=1, source_target_pairs={{10,0},{12,2},{14,4},{18,8},{20,10},{22,12},{26,16},{28,18},{30,20... | collective-permute-start | bytes 73736 | tf_op jit(solution)/shard_map/ppermute | solution.py:38
  204.5 62.1 %collective-permute-start.34 = (f32[1792,128]{1,0:T(8,128)}, f32[1792,128]{1,0:T(8,128)}, u32[]{:S(2)}, u32[]{:S(2)}) collective-permute-start(f32[1792,128]{1,0:T(8,128)} %constant_dynamic-slice_fusion.4), channel_id=1, source_target_pairs={{0,1},{1,0},{2,3},{3,2},{4,5},{5,4},{6,7},{7,6},{8,9},{9,8},{10,11... | collective-permute-start | bytes 2752520 | tf_op jit(solution)/shard_map/ppermute | solution.py:106
  268.0 12.5 %collective-permute-start.35 = (f32[896,128]{1,0:T(8,128)S(1)}, f32[896,128]{1,0:T(8,128)S(1)}, u32[]{:S(2)}, u32[]{:S(2)}) collective-permute-start(f32[896,128]{1,0:T(8,128)S(1)} %constant_dynamic-slice_fusion.3), channel_id=1, source_target_pairs={{0,4},{2,6},{4,0},{6,2},{1,5},{3,7},{5,1},{7,3},{8,12},{10,14},{12... | collective-permute-start | bytes 1376264 | tf_op jit(solution)/shard_map/ppermute | solution.py:106
  280.6 6.7 %collective-permute-start.36 = (f32[448,128]{1,0:T(8,128)S(1)}, f32[448,128]{1,0:T(8,128)S(1)}, u32[]{:S(2)}, u32[]{:S(2)}) collective-permute-start(f32[448,128]{1,0:T(8,128)S(1)} %constant_dynamic-slice_fusion.2), channel_id=1, source_target_pairs={{0,2},{2,0},{4,6},{6,4},{1,3},{3,1},{5,7},{7,5},{8,10},{10,8},{12,... | collective-permute-start | bytes 688136 | tf_op jit(solution)/shard_map/ppermute | solution.py:106
  282.3 11.4 %collective-permute-start.25 = (f32[896,128]{1,0:T(8,128)S(1)}, f32[896,128]{1,0:T(8,128)S(1)}, u32[]{:S(2)}, u32[]{:S(2)}) collective-permute-start(f32[896,128]{1,0:T(8,128)S(1)} %constant_dynamic-slice_fusion.8), channel_id=1, source_target_pairs={{0,4},{2,6},{4,0},{6,2},{1,5},{3,7},{5,1},{7,3},{8,12},{10,14},{12... | collective-permute-start | bytes 1376264 | tf_op jit(solution)/shard_map/ppermute | solution.py:106
  287.4 6.5 %collective-permute-start.37 = (f32[224,128]{1,0:T(8,128)S(1)}, f32[224,128]{1,0:T(8,128)S(1)}, u32[]{:S(2)}, u32[]{:S(2)}) collective-permute-start(f32[224,128]{1,0:T(8,128)S(1)} %constant_dynamic-slice_fusion.1), channel_id=1, source_target_pairs={{0,16},{8,24},{16,0},{24,8},{1,17},{9,25},{17,1},{25,9},{2,18},{10... | collective-permute-start | bytes 344072 | tf_op jit(solution)/shard_map/ppermute | solution.py:106
  296.5 6.1 %collective-permute-start.26 = (f32[448,128]{1,0:T(8,128)S(1)}, f32[448,128]{1,0:T(8,128)S(1)}, u32[]{:S(2)}, u32[]{:S(2)}) collective-permute-start(f32[448,128]{1,0:T(8,128)S(1)} %constant_dynamic-slice_fusion.7), channel_id=1, source_target_pairs={{0,2},{2,0},{4,6},{6,4},{1,3},{3,1},{5,7},{7,5},{8,10},{10,8},{12,... | collective-permute-start | bytes 688136 | tf_op jit(solution)/shard_map/ppermute | solution.py:106
  302.7 8.4 %collective-permute-start.27 = (f32[224,128]{1,0:T(8,128)S(1)}, f32[224,128]{1,0:T(8,128)S(1)}, u32[]{:S(2)}, u32[]{:S(2)}) collective-permute-start(f32[224,128]{1,0:T(8,128)S(1)} %constant_dynamic-slice_fusion.6), channel_id=1, source_target_pairs={{0,16},{8,24},{16,0},{24,8},{1,17},{9,25},{17,1},{25,9},{2,18},{10... | collective-permute-start | bytes 344072 | tf_op jit(solution)/shard_map/ppermute | solution.py:106
  311.2 9.0 %collective-permute-start.40 = (f32[224,128]{1,0:T(8,128)S(1)}, f32[224,128]{1,0:T(8,128)S(1)}, u32[]{:S(2)}, u32[]{:S(2)}) collective-permute-start(f32[224,128]{1,0:T(8,128)S(1)} %pad_maximum_fusion.9), channel_id=1, source_target_pairs={{0,16},{8,24},{16,0},{24,8},{1,17},{9,25},{17,1},{25,9},{2,18},{10... | collective-permute-start | bytes 344072 | tf_op jit(solution)/shard_map/ppermute | solution.py:110
  320.8 7.8 %collective-permute-start.41 = (f32[448,128]{1,0:T(8,128)S(1)}, f32[448,128]{1,0:T(8,128)S(1)}, u32[]{:S(2)}, u32[]{:S(2)}) collective-permute-start(f32[448,128]{1,0:T(8,128)S(1)} %pad_maximum_fusion.7), channel_id=1, source_target_pairs={{0,2},{2,0},{4,6},{6,4},{1,3},{3,1},{5,7},{7,5},{8,10},{10,8},{12,... | collective-permute-start | bytes 688136 | tf_op jit(solution)/shard_map/ppermute | solution.py:110
  328.8 11.0 %collective-permute-start.42 = (f32[896,128]{1,0:T(8,128)S(1)}, f32[896,128]{1,0:T(8,128)S(1)}, u32[]{:S(2)}, u32[]{:S(2)}) collective-permute-start(f32[896,128]{1,0:T(8,128)S(1)} %pad_maximum_fusion.5), channel_id=1, source_target_pairs={{0,4},{2,6},{4,0},{6,2},{1,5},{3,7},{5,1},{7,3},{8,12},{10,14},{12... | collective-permute-start | bytes 1376264 | tf_op jit(solution)/shard_map/ppermute | solution.py:110
  333.7 11.1 %collective-permute-start.32 = (f32[896,128]{1,0:T(8,128)}, f32[896,128]{1,0:T(8,128)}, u32[]{:S(2)}, u32[]{:S(2)}) collective-permute-start(f32[896,128]{1,0:T(8,128)} %pad_maximum_fusion.4), channel_id=1, source_target_pairs={{0,4},{2,6},{4,0},{6,2},{1,5},{3,7},{5,1},{7,3},{8,12},{10,14},{12... | collective-permute-start | bytes 1376264 | tf_op jit(solution)/shard_map/ppermute | solution.py:110
  339.9 6.1 %collective-permute-start.43 = (f32[1792,128]{1,0:T(8,128)S(1)}, f32[1792,128]{1,0:T(8,128)S(1)}, u32[]{:S(2)}, u32[]{:S(2)}) collective-permute-start(f32[1792,128]{1,0:T(8,128)S(1)} %pad_maximum_fusion.3), channel_id=1, source_target_pairs={{0,1},{1,0},{2,3},{3,2},{4,5},{5,4},{6,7},{7,6},{8,9},{9,8},{10,11... | collective-permute-start | bytes 2752520 | tf_op jit(solution)/shard_map/ppermute | solution.py:110
  (49 other events, 470.0 us)

commit v3 on v1

--- a/solution.py
+++ b/solution.py
@@ -86,9 +86,11 @@
     return rows.reshape(-1)[:size].reshape(value.shape)
 
 
-def weight_grad(padded, delta_field):
+def weight_grad(padded, delta_field, after=None):
     local_grad = kernel_grad(padded, delta_field)
-    return tree_sum(local_grad, ("dp", "gy", "gx"))
+    if after is not None:
+        after, local_grad = lax.optimization_barrier((after, local_grad))
+    return after, tree_sum(local_grad, ("dp", "gy", "gx"))
 
 
 def per_device(volumes, weight_one, weight_two, cotangent):
@@ -102,11 +104,11 @@
     act_two = conv_block(rim_hidden, weight_two)
     features = jax.nn.silu(act_two).astype(jnp.bfloat16)
     delta_two = (cotangent.astype(jnp.float32) * swish_slope(act_two)).astype(jnp.bfloat16)
-    grad_two = weight_grad(rim_hidden, delta_two)
+    _, grad_two = weight_grad(rim_hidden, delta_two)
     rim_delta = extended(delta_two, (("gx", 1), ("gy", 2)), 1)
     back_grad = conv_block(rim_delta, flipped)
     delta_one = (back_grad * swish_slope(act_one)).astype(jnp.bfloat16)
-    grad_one = weight_grad(rim_input, delta_one)
+    grad_two, grad_one = weight_grad(rim_input, delta_one, grad_two)
     return (features, grad_one.reshape(27, depth, depth), grad_two.reshape(27, depth, depth))
 
 

time: 320 us -> 345 us (1.078)
  starting transfers between devices: 43 us -> 78.6 us
  waiting for transfers between devices: 107 us -> 102 us
  other arithmetic: 29.9 us -> 26.2 us
    ppermute x10, starting transfers between devices: 4.26 us -> 20.9 us  [tree_sum(): other = lax.ppermute(rows, axis, pairs)]
    ppermute x10, waiting for transfers between devices: 34.5 us -> 50.6 us  [tree_sum(): rows = keep + lax.ppermute(send, axis, pairs)]
    ppermute x6, waiting for transfers between devices: 18.3 us -> 6.82 us  [extended(): lax.ppermute(tail, axis, [(i, (i + 1) % count) for i in range(ends)])]
    ppermute x6, waiting for transfers between devices: 33.1 us -> 22.1 us  [extended(): lax.ppermute(head, axis, [((i + 1) % count, i) for i in range(ends)])]
    ppermute x10, starting transfers between devices: 8.75 us -> 19.5 us  [tree_sum(): rows = keep + lax.ppermute(send, axis, pairs)]
    ppermute x6, starting transfers between devices: 21.9 us -> 30.4 us  [extended(): lax.ppermute(tail, axis, [(i, (i + 1) % count) for i in range(ends)])]
    unnamed x40 -> x48, local copies, waits for them, and re-layouts: 10.7 us -> 10.5 us
  transfers between devices with their start and end apart: 32 -> 32, of which waited for: 25 -> 23; matrix products, arithmetic and copies ran while one was open for 32% -> 19% of each run, Pallas kernels for 0% -> 0%
where the time goes in v3:
time: 345 us; the launch traced here: 341 us
  matrix products  104 us (30%)
  waiting for transfers between devices  102 us (30%)
  starting transfers between devices  78.6 us (23%)
  local copies, waits for them, and re-layouts  27.8 us (8%)
  other arithmetic  26.2 us (8%)
    conv_general_dilated x3, matrix products, conv_block(): lax.conv_general_dilated(padded, cube_kernel, (1, 1, 1), ((0, 0), (0, 0),...  53.3 us
    conv_general_dilated x2, matrix products, kernel_grad(): lax.conv_general_dilated(padded, delta_field, (1, 1, 1), ((0, 0), (0, 0),...  51.1 us
    ppermute x10, waiting for transfers between devices, tree_sum(): rows = keep + lax.ppermute(send, axis, pairs)  50.6 us
    ppermute x6, starting transfers between devices, extended(): lax.ppermute(tail, axis, [(i, (i + 1) % count) for i in range(ends)])  30.4 us
    ppermute x10, waiting for transfers between devices, tree_sum(): other = lax.ppermute(rows, axis, pairs)  22.8 us
    ppermute x6, waiting for transfers between devices, extended(): lax.ppermute(head, axis, [((i + 1) % count, i) for i in range(ends)])  22.1 us
    ppermute x10, starting transfers between devices, tree_sum(): other = lax.ppermute(rows, axis, pairs)  20.9 us
    ppermute x10, starting transfers between devices, tree_sum(): rows = keep + lax.ppermute(send, axis, pairs)  19.5 us
  transfers between devices with their start and end apart: 32, of which 23 were waited for; matrix products, arithmetic and copies ran while one was open for 19% of the time, Pallas kernels for 0%

profile of v3, /device:TPU:0, one launch (start us, length us, event | category | flops | bytes accessed | tf_op | source)
XLA Modules:
  0.0 341.1 jit_solution(8035132977588116824)
XLA Ops:
  2.0 4.9 %collective-permute-start = (bf16[3,1,8,32,128]{4,0,3,2,1:T(4,128)(2,1)S(1)}, bf16[3,1,8,32,128]{4,0,3,2,1:T(4,128)(2,1)S(1)}, u32[]{:S(2)}, u32[]{:S(2)}) collective-permute-start(bf16[3,1,8,32,128]{4,0,3,2,1:T(4,128)(2,1)S(1)} %copy.55), channel_id=1, source_target_pairs={{0,8},{8,16},{16,24},{1,9},{9,17},{17,25},{2,10},{10,18},{18,26},{... | collective-permute-start | bytes 589832 | tf_op jit(solution)/shard_map/ppermute | solution.py:15
  8.4 4.1 %collective-permute-done = bf16[3,1,8,32,128]{4,0,3,2,1:T(4,128)(2,1)S(1)} collective-permute-done((bf16[3,1,8,32,128]{4,0,3,2,1:T(4,128)(2,1)S(1)}, bf16[3,1,8,32,128]{4,0,3,2,1:T(4,128)(2,1)S(1)}, u32[]{:S(2)}, u32[]{:S(2)}) %collective-permute-start) | collective-permute-done | bytes 196640 | tf_op jit(solution)/shard_map/ppermute | solution.py:15
  18.5 5.1 %collective-permute-start.2 = (bf16[3,10,1,32,128]{4,0,3,2,1:T(4,128)(2,1)S(1)}, bf16[3,10,1,32,128]{4,0,3,2,1:T(4,128)(2,1)S(1)}, u32[]{:S(2)}, u32[]{:S(2)}) collective-permute-start(bf16[3,10,1,32,128]{4,0,3,2,1:T(4,128)(2,1)S(1)} %get-tuple-element.14), channel_id=1, source_target_pairs={{0,2},{2,4},{4,6},{1,3},{3,5},{5,7},{8,10},{10,12},{12,14},{9,11},... | collective-permute-start | bytes 737288 | tf_op jit(solution)/shard_map/ppermute | solution.py:15
  23.6 6.1 %collective-permute-done.3 = bf16[3,10,1,32,128]{4,0,3,2,1:T(4,128)(2,1)S(1)} collective-permute-done((bf16[3,10,1,32,128]{4,0,3,2,1:T(4,128)(2,1)S(1)}, bf16[3,10,1,32,128]{4,0,3,2,1:T(4,128)(2,1)S(1)}, u32[]{:S(2)}, u32[]{:S(2)}) %collective-permute-start.3) | collective-permute-done | bytes 245792 | tf_op jit(solution)/shard_map/ppermute | solution.py:17
  35.1 15.5 %broadcast_select_fusion.1 = f32[8,8,24,5,128]{4,2,3,1,0:T(8,128)S(1)} fusion(pred[24,5]{0,1:T(8,128)(4,1)S(1)} %copy-done.19, bf16[3,3,3,128,128]{4,3,2,1,0:T(8,128)(2,1)S(1)} %bitcast.64, bf16[10,10,3,7,2,128]{5,3,2,4,1,0:T(8,128)(2,1)S(1)} %slice.69, bf16[10,10,3,8,5,128]{5,3,2,4,1,0:T(8,128)(2,1)S(1)} %copy.21), kind=kOutput, calls=%fused_computation.42 | convolution fusion | flops 6808657920 | bytes 8964216 | tf_op jit(solution)/shard_map/conv_general_dilated | solution.py:27
  57.7 4.6 %collective-permute-start.4 = (bf16[3,1,8,32,128]{4,0,3,2,1:T(4,128)(2,1)S(1)}, bf16[3,1,8,32,128]{4,0,3,2,1:T(4,128)(2,1)S(1)}, u32[]{:S(2)}, u32[]{:S(2)}) collective-permute-start(bf16[3,1,8,32,128]{4,0,3,2,1:T(4,128)(2,1)S(1)} %get-tuple-element.16), channel_id=1, source_target_pairs={{0,8},{8,16},{16,24},{1,9},{9,17},{17,25},{2,10},{10,18},{18,26},{... | collective-permute-start | bytes 589832 | tf_op jit(solution)/shard_map/ppermute | solution.py:15
  68.8 6.7 %collective-permute-start.6 = (bf16[3,10,1,32,128]{4,0,3,2,1:T(4,128)(2,1)}, bf16[3,10,1,32,128]{4,0,3,2,1:T(4,128)(2,1)S(1)}, u32[]{:S(2)}, u32[]{:S(2)}) collective-permute-start(bf16[3,10,1,32,128]{4,0,3,2,1:T(4,128)(2,1)} %get-tuple-element.12), channel_id=1, source_target_pairs={{0,2},{2,4},{4,6},{1,3},{3,5},{5,7},{8,10},{10,12},{12,14},{9,11},... | collective-permute-start | bytes 737288 | tf_op jit(solution)/shard_map/ppermute | solution.py:15
  75.5 5.9 %collective-permute-done.7 = bf16[3,10,1,32,128]{4,0,3,2,1:T(4,128)(2,1)S(1)} collective-permute-done((bf16[3,10,1,32,128]{4,0,3,2,1:T(4,128)(2,1)}, bf16[3,10,1,32,128]{4,0,3,2,1:T(4,128)(2,1)S(1)}, u32[]{:S(2)}, u32[]{:S(2)}) %collective-permute-start.7) | collective-permute-done | bytes 245792 | tf_op jit(solution)/shard_map/ppermute | solution.py:17
  87.4 17.2 %add_multiply_fusion = (f32[8,8,24,5,128]{4,2,3,1,0:T(8,128)S(1)}, bf16[8,8,24,5,128]{4,2,3,1,0:T(8,128)(2,1)}) fusion(pred[24,5]{0,1:T(8,128)(4,1)S(1)} %copy-done.19, bf16[3,3,3,128,128]{4,3,2,1,0:T(8,128)(2,1)S(1)} %bitcast.78, bf16[10,10,3,7,2,128]{5,3,2,4,1,0:T(8,128)(2,1)S(1)} %slice.73, bf16[10,10,3,8,5,128]{5,3,2,4,1,0:T(8,128)(2,1)S(1)} %copy.25), kind=kOutput, calls=%fused_computation.28 | convolution fusion | flops 6817505280 | bytes 10930296 | tf_op jit(solution)/shard_map/conv_general_dilated | solution.py:27
  107.2 23.6 %fusion.27 = f32[3,3,3,128,128]{4,3,2,1,0:T(8,128)S(1)} fusion(bf16[3,8,8,32,128]{4,2,3,0,1:T(8,128)(2,1)S(1)} %fusion.24, bf16[3,10,1,32,128]{4,0,3,2,1:T(4,128)(2,1)S(1)} %collective-permute-done.7, bf16[3,1,8,32,128]{4,0,3,2,1:T(4,128)(2,1)S(1)} %collective-permute-done.5, bf16[3,8,8,32,128]{4,0,3,2,1:T(4,128)(2,1)S(1)} %multiply_convert_fusion, ...), kind=kOutput, calls=%fused_computation.38 | convolution fusion | flops 5334859776 | bytes 5799936 | tf_op jit(solution)/shard_map/conv_general_dilated | solution.py:39
  138.0 5.9 %collective-permute-start.9 = (f32[896,128]{1,0:T(8,128)S(1)}, f32[896,128]{1,0:T(8,128)S(1)}, u32[]{:S(2)}, u32[]{:S(2)}) collective-permute-start(f32[896,128]{1,0:T(8,128)S(1)} %constant_dynamic-slice_fusion.8), channel_id=1, source_target_pairs={{0,4},{2,6},{4,0},{6,2},{1,5},{3,7},{5,1},{7,3},{8,12},{10,14},{12... | collective-permute-start | bytes 1376264 | tf_op jit(solution)/shard_map/ppermute | solution.py:78
  143.9 10.8 %collective-permute-done.9 = f32[896,128]{1,0:T(8,128)S(1)} collective-permute-done((f32[896,128]{1,0:T(8,128)S(1)}, f32[896,128]{1,0:T(8,128)S(1)}, u32[]{:S(2)}, u32[]{:S(2)}) %collective-permute-start.9) | collective-permute-done | bytes 458784 | tf_op jit(solution)/shard_map/ppermute | solution.py:78
  157.8 5.4 %collective-permute-done.10 = f32[448,128]{1,0:T(8,128)S(1)} collective-permute-done((f32[448,128]{1,0:T(8,128)S(1)}, f32[448,128]{1,0:T(8,128)S(1)}, u32[]{:S(2)}, u32[]{:S(2)}) %collective-permute-start.10) | collective-permute-done | bytes 229408 | tf_op jit(solution)/shard_map/ppermute | solution.py:78
  163.2 3.5 %collective-permute-start.11 = (f32[224,128]{1,0:T(8,128)S(1)}, f32[224,128]{1,0:T(8,128)S(1)}, u32[]{:S(2)}, u32[]{:S(2)}) collective-permute-start(f32[224,128]{1,0:T(8,128)S(1)} %constant_dynamic-slice_fusion.6), channel_id=1, source_target_pairs={{0,16},{8,24},{16,0},{24,8},{1,17},{9,25},{17,1},{25,9},{2,18},{10... | collective-permute-start | bytes 344072 | tf_op jit(solution)/shard_map/ppermute | solution.py:78
  168.0 3.4 %collective-permute-done.11 = f32[224,128]{1,0:T(8,128)S(1)} collective-permute-done((f32[224,128]{1,0:T(8,128)S(1)}, f32[224,128]{1,0:T(8,128)S(1)}, u32[]{:S(2)}, u32[]{:S(2)}) %collective-permute-start.11) | collective-permute-done | bytes 114720 | tf_op jit(solution)/shard_map/ppermute | solution.py:78
  173.4 4.6 %collective-permute-start.18 = (bf16[3,1,8,32,128]{4,2,3,0,1:T(8,128)(2,1)S(1)}, bf16[3,1,8,32,128]{4,2,3,0,1:T(8,128)(2,1)S(1)}, u32[]{:S(2)}, u32[]{:S(2)}) collective-permute-start(bf16[3,1,8,32,128]{4,2,3,0,1:T(8,128)(2,1)S(1)} %get-tuple-element.24), channel_id=1, source_target_pairs={{0,8},{8,16},{16,24},{1,9},{9,17},{17,25},{2,10},{10,18},{18,26},{... | collective-permute-start | bytes 589832 | tf_op jit(solution)/shard_map/ppermute | solution.py:15
  183.7 4.6 %collective-permute-start.20 = (bf16[3,10,1,32,128]{4,2,3,0,1:T(2,128)(2,1)S(1)}, bf16[3,10,1,32,128]{4,2,3,0,1:T(2,128)(2,1)S(1)}, u32[]{:S(2)}, u32[]{:S(2)}) collective-permute-start(bf16[3,10,1,32,128]{4,2,3,0,1:T(2,128)(2,1)S(1)} %get-tuple-element.18), channel_id=1, source_target_pairs={{0,2},{2,4},{4,6},{1,3},{3,5},{5,7},{8,10},{10,12},{12,14},{9,11},... | collective-permute-start | bytes 737288 | tf_op jit(solution)/shard_map/ppermute | solution.py:15
  188.4 3.7 %collective-permute-start.14 = (f32[224,128]{1,0:T(8,128)S(1)}, f32[224,128]{1,0:T(8,128)S(1)}, u32[]{:S(2)}, u32[]{:S(2)}) collective-permute-start(f32[224,128]{1,0:T(8,128)S(1)} %pad_maximum_fusion.16), channel_id=1, source_target_pairs={{0,16},{8,24},{16,0},{24,8},{1,17},{9,25},{17,1},{25,9},{2,18},{10... | collective-permute-start | bytes 344072 | tf_op jit(solution)/shard_map/ppermute | solution.py:82
  192.1 6.4 %collective-permute-done.21 = bf16[3,10,1,32,128]{4,2,3,0,1:T(2,128)(2,1)S(1)} collective-permute-done((bf16[3,10,1,32,128]{4,2,3,0,1:T(2,128)(2,1)S(1)}, bf16[3,10,1,32,128]{4,2,3,0,1:T(2,128)(2,1)S(1)}, u32[]{:S(2)}, u32[]{:S(2)}) %collective-permute-start.21) | collective-permute-done | bytes 245792 | tf_op jit(solution)/shard_map/ppermute | solution.py:17
  205.0 6.0 %collective-permute-start.15 = (f32[448,128]{1,0:T(8,128)S(1)}, f32[448,128]{1,0:T(8,128)S(1)}, u32[]{:S(2)}, u32[]{:S(2)}) collective-permute-start(f32[448,128]{1,0:T(8,128)S(1)} %pad_maximum_fusion.14), channel_id=1, source_target_pairs={{0,2},{2,0},{4,6},{6,4},{1,3},{3,1},{5,7},{7,5},{8,10},{10,8},{12,... | collective-permute-start | bytes 688136 | tf_op jit(solution)/shard_map/ppermute | solution.py:82
  215.0 4.0 %collective-permute-start.16 = (f32[896,128]{1,0:T(8,128)S(1)}, f32[896,128]{1,0:T(8,128)S(1)}, u32[]{:S(2)}, u32[]{:S(2)}) collective-permute-start(f32[896,128]{1,0:T(8,128)S(1)} %pad_maximum_fusion.9), channel_id=1, source_target_pairs={{0,4},{2,6},{4,0},{6,2},{1,5},{3,7},{5,1},{7,3},{8,12},{10,14},{12... | collective-permute-start | bytes 1376264 | tf_op jit(solution)/shard_map/ppermute | solution.py:82
  219.0 20.5 %broadcast_select_fusion = f32[8,8,24,5,128]{4,2,3,1,0:T(8,128)S(1)} fusion(pred[24,5]{0,1:T(8,128)(4,1)S(1)} %copy-done.20, bf16[3,3,3,128,128]{3,4,2,1,0:T(8,128)(2,1)S(1)} %bitcast.79, bf16[10,10,3,8,7,128]{5,4,3,2,1,0:T(8,128)(2,1)S(1)} %fusion.3), kind=kOutput, calls=%fused_computation.41 | convolution fusion | flops 6795755520 | bytes 9117816 | tf_op jit(solution)/shard_map/conv_general_dilated | solution.py:27
  244.0 27.6 %fusion.29 = f32[3,3,3,128,128]{4,3,2,1,0:T(8,128)S(1)} fusion(f32[8,8,3,32,128]{4,1,3,2,0:T(8,128)S(1)} %slice.79, f32[3,8,8,32,128]{4,0,3,2,1:T(4,128)S(1)} %bitcast.67, bf16[3,10,1,32,128]{4,0,3,2,1:T(4,128)(2,1)S(1)} %copy-done.16, bf16[3,10,8,32,128]{4,0,3,2,1:T(4,128)(2,1)S(1)} %copy-done.7, bf16[3,10,1,32,128]{4,0,3,2,1:T(4,128)(2,1)S(1)} %copy-done.18), kind=kOutput, calls=%fused_computation.40 | convolution fusion | flops 5337022464 | bytes 10518528 | tf_op jit(solution)/shard_map/conv_general_dilated | solution.py:39
  277.2 12.5 %collective-permute-done.23 = f32[896,128]{1,0:T(8,128)S(1)} collective-permute-done((f32[896,128]{1,0:T(8,128)S(1)}, f32[896,128]{1,0:T(8,128)S(1)}, u32[]{:S(2)}, u32[]{:S(2)}) %collective-permute-start.23) | collective-permute-done | bytes 458784 | tf_op jit(solution)/shard_map/ppermute | solution.py:78
  291.5 5.2 %collective-permute-done.24 = f32[448,128]{1,0:T(8,128)S(1)} collective-permute-done((f32[448,128]{1,0:T(8,128)S(1)}, f32[448,128]{1,0:T(8,128)S(1)}, u32[]{:S(2)}, u32[]{:S(2)}) %collective-permute-start.24) | collective-permute-done | bytes 229408 | tf_op jit(solution)/shard_map/ppermute | solution.py:78
  296.8 4.7 %collective-permute-start.25 = (f32[224,128]{1,0:T(8,128)S(1)}, f32[224,128]{1,0:T(8,128)S(1)}, u32[]{:S(2)}, u32[]{:S(2)}) collective-permute-start(f32[224,128]{1,0:T(8,128)S(1)} %constant_dynamic-slice_fusion.1), channel_id=1, source_target_pairs={{0,16},{8,24},{16,0},{24,8},{1,17},{9,25},{17,1},{25,9},{2,18},{10... | collective-permute-start | bytes 344072 | tf_op jit(solution)/shard_map/ppermute | solution.py:78
  301.5 4.2 %collective-permute-done.25 = f32[224,128]{1,0:T(8,128)S(1)} collective-permute-done((f32[224,128]{1,0:T(8,128)S(1)}, f32[224,128]{1,0:T(8,128)S(1)}, u32[]{:S(2)}, u32[]{:S(2)}) %collective-permute-start.25) | collective-permute-done | bytes 114720 | tf_op jit(solution)/shard_map/ppermute | solution.py:78
  306.6 3.8 %collective-permute-done.26 = f32[112,128]{1,0:T(8,128)S(1)} collective-permute-done((f32[112,128]{1,0:T(8,128)S(1)}, f32[112,128]{1,0:T(8,128)S(1)}, u32[]{:S(2)}, u32[]{:S(2)}) %collective-permute-start.26) | collective-permute-done | bytes 57376 | tf_op jit(solution)/shard_map/ppermute | solution.py:78
  311.2 3.8 %collective-permute-done.27 = f32[112,128]{1,0:T(8,128)S(1)} collective-permute-done((f32[112,128]{1,0:T(8,128)S(1)}, f32[112,128]{1,0:T(8,128)S(1)}, u32[]{:S(2)}, u32[]{:S(2)}) %collective-permute-start.27) | collective-permute-done | bytes 57376 | tf_op jit(solution)/shard_map/ppermute | solution.py:82
  316.8 5.2 %collective-permute-done.28 = f32[224,128]{1,0:T(8,128)S(1)} collective-permute-done((f32[224,128]{1,0:T(8,128)S(1)}, f32[224,128]{1,0:T(8,128)S(1)}, u32[]{:S(2)}, u32[]{:S(2)}) %collective-permute-start.28) | collective-permute-done | bytes 114720 | tf_op jit(solution)/shard_map/ppermute | solution.py:82
  323.7 4.4 %collective-permute-done.29 = f32[448,128]{1,0:T(8,128)S(1)} collective-permute-done((f32[448,128]{1,0:T(8,128)S(1)}, f32[448,128]{1,0:T(8,128)S(1)}, u32[]{:S(2)}, u32[]{:S(2)}) %collective-permute-start.29) | collective-permute-done | bytes 229408 | tf_op jit(solution)/shard_map/ppermute | solution.py:82
  329.2 7.6 %collective-permute-done.30 = f32[896,128]{1,0:T(8,128)S(1)} collective-permute-done((f32[896,128]{1,0:T(8,128)S(1)}, f32[896,128]{1,0:T(8,128)S(1)}, u32[]{:S(2)}, u32[]{:S(2)}) %collective-permute-start.30) | collective-permute-done | bytes 458784 | tf_op jit(solution)/shard_map/ppermute | solution.py:82
  (157 shorter events, 87.7 us)
Async XLA Ops:
  2.0 10.5 %collective-permute-start = (bf16[3,1,8,32,128]{4,0,3,2,1:T(4,128)(2,1)S(1)}, bf16[3,1,8,32,128]{4,0,3,2,1:T(4,128)(2,1)S(1)}, u32[]{:S(2)}, u32[]{:S(2)}) collective-permute-start(bf16[3,1,8,32,128]{4,0,3,2,1:T(4,128)(2,1)S(1)} %copy.55), channel_id=1, source_target_pairs={{0,8},{8,16},{16,24},{1,9},{9,17},{17,25},{2,10},{10,18},{18,26},{... | collective-permute-start | bytes 589832 | tf_op jit(solution)/shard_map/ppermute | solution.py:15
  7.1 9.7 %collective-permute-start.1 = (bf16[3,1,8,32,128]{4,0,3,2,1:T(4,128)(2,1)S(1)}, bf16[3,1,8,32,128]{4,0,3,2,1:T(4,128)(2,1)S(1)}, u32[]{:S(2)}, u32[]{:S(2)}) collective-permute-start(bf16[3,1,8,32,128]{4,0,3,2,1:T(4,128)(2,1)S(1)} %copy.56), channel_id=1, source_target_pairs={{8,0},{16,8},{24,16},{9,1},{17,9},{25,17},{10,2},{18,10},{26,18},{... | collective-permute-start | bytes 589832 | tf_op jit(solution)/shard_map/ppermute | solution.py:17
  17.2 12.5 %collective-permute-start.3 = (bf16[3,10,1,32,128]{4,0,3,2,1:T(4,128)(2,1)S(1)}, bf16[3,10,1,32,128]{4,0,3,2,1:T(4,128)(2,1)S(1)}, u32[]{:S(2)}, u32[]{:S(2)}) collective-permute-start(bf16[3,10,1,32,128]{4,0,3,2,1:T(4,128)(2,1)S(1)} %get-tuple-element.15), channel_id=1, source_target_pairs={{2,0},{4,2},{6,4},{3,1},{5,3},{7,5},{10,8},{12,10},{14,12},{11,9},... | collective-permute-start | bytes 737288 | tf_op jit(solution)/shard_map/ppermute | solution.py:17
  18.5 11.2 %collective-permute-start.2 = (bf16[3,10,1,32,128]{4,0,3,2,1:T(4,128)(2,1)S(1)}, bf16[3,10,1,32,128]{4,0,3,2,1:T(4,128)(2,1)S(1)}, u32[]{:S(2)}, u32[]{:S(2)}) collective-permute-start(bf16[3,10,1,32,128]{4,0,3,2,1:T(4,128)(2,1)S(1)} %get-tuple-element.14), channel_id=1, source_target_pairs={{0,2},{2,4},{4,6},{1,3},{3,5},{5,7},{8,10},{10,12},{12,14},{9,11},... | collective-permute-start | bytes 737288 | tf_op jit(solution)/shard_map/ppermute | solution.py:15
  56.4 8.3 %collective-permute-start.5 = (bf16[3,1,8,32,128]{4,0,3,2,1:T(4,128)(2,1)S(1)}, bf16[3,1,8,32,128]{4,0,3,2,1:T(4,128)(2,1)S(1)}, u32[]{:S(2)}, u32[]{:S(2)}) collective-permute-start(bf16[3,1,8,32,128]{4,0,3,2,1:T(4,128)(2,1)S(1)} %get-tuple-element.17), channel_id=1, source_target_pairs={{8,0},{16,8},{24,16},{9,1},{17,9},{25,17},{10,2},{18,10},{26,18},{... | collective-permute-start | bytes 589832 | tf_op jit(solution)/shard_map/ppermute | solution.py:17
  57.7 8.4 %collective-permute-start.4 = (bf16[3,1,8,32,128]{4,0,3,2,1:T(4,128)(2,1)S(1)}, bf16[3,1,8,32,128]{4,0,3,2,1:T(4,128)(2,1)S(1)}, u32[]{:S(2)}, u32[]{:S(2)}) collective-permute-start(bf16[3,1,8,32,128]{4,0,3,2,1:T(4,128)(2,1)S(1)} %get-tuple-element.16), channel_id=1, source_target_pairs={{0,8},{8,16},{16,24},{1,9},{9,17},{17,25},{2,10},{10,18},{18,26},{... | collective-permute-start | bytes 589832 | tf_op jit(solution)/shard_map/ppermute | solution.py:15
  67.5 13.9 %collective-permute-start.7 = (bf16[3,10,1,32,128]{4,0,3,2,1:T(4,128)(2,1)}, bf16[3,10,1,32,128]{4,0,3,2,1:T(4,128)(2,1)S(1)}, u32[]{:S(2)}, u32[]{:S(2)}) collective-permute-start(bf16[3,10,1,32,128]{4,0,3,2,1:T(4,128)(2,1)} %get-tuple-element.13), channel_id=1, source_target_pairs={{2,0},{4,2},{6,4},{3,1},{5,3},{7,5},{10,8},{12,10},{14,12},{11,9},... | collective-permute-start | bytes 737288 | tf_op jit(solution)/shard_map/ppermute | solution.py:17
  68.8 12.6 %collective-permute-start.6 = (bf16[3,10,1,32,128]{4,0,3,2,1:T(4,128)(2,1)}, bf16[3,10,1,32,128]{4,0,3,2,1:T(4,128)(2,1)S(1)}, u32[]{:S(2)}, u32[]{:S(2)}) collective-permute-start(bf16[3,10,1,32,128]{4,0,3,2,1:T(4,128)(2,1)} %get-tuple-element.12), channel_id=1, source_target_pairs={{0,2},{2,4},{4,6},{1,3},{3,5},{5,7},{8,10},{10,12},{12,14},{9,11},... | collective-permute-start | bytes 737288 | tf_op jit(solution)/shard_map/ppermute | solution.py:15
  131.9 2.8 collective-permute-start.8
  138.0 16.8 %collective-permute-start.9 = (f32[896,128]{1,0:T(8,128)S(1)}, f32[896,128]{1,0:T(8,128)S(1)}, u32[]{:S(2)}, u32[]{:S(2)}) collective-permute-start(f32[896,128]{1,0:T(8,128)S(1)} %constant_dynamic-slice_fusion.8), channel_id=1, source_target_pairs={{0,4},{2,6},{4,0},{6,2},{1,5},{3,7},{5,1},{7,3},{8,12},{10,14},{12... | collective-permute-start | bytes 1376264 | tf_op jit(solution)/shard_map/ppermute | solution.py:78
  155.8 7.4 %collective-permute-start.10 = (f32[448,128]{1,0:T(8,128)S(1)}, f32[448,128]{1,0:T(8,128)S(1)}, u32[]{:S(2)}, u32[]{:S(2)}) collective-permute-start(f32[448,128]{1,0:T(8,128)S(1)} %constant_dynamic-slice_fusion.7), channel_id=1, source_target_pairs={{0,2},{2,0},{4,6},{6,4},{1,3},{3,1},{5,7},{7,5},{8,10},{10,8},{12,... | collective-permute-start | bytes 688136 | tf_op jit(solution)/shard_map/ppermute | solution.py:78
  163.2 8.2 %collective-permute-start.11 = (f32[224,128]{1,0:T(8,128)S(1)}, f32[224,128]{1,0:T(8,128)S(1)}, u32[]{:S(2)}, u32[]{:S(2)}) collective-permute-start(f32[224,128]{1,0:T(8,128)S(1)} %constant_dynamic-slice_fusion.6), channel_id=1, source_target_pairs={{0,16},{8,24},{16,0},{24,8},{1,17},{9,25},{17,1},{25,9},{2,18},{10... | collective-permute-start | bytes 344072 | tf_op jit(solution)/shard_map/ppermute | solution.py:78
  171.5 6.5 %collective-permute-start.12 = (f32[112,128]{1,0:T(8,128)S(1)}, f32[112,128]{1,0:T(8,128)S(1)}, u32[]{:S(2)}, u32[]{:S(2)}) collective-permute-start(f32[112,128]{1,0:T(8,128)S(1)} %constant_dynamic-slice_fusion.5), channel_id=1, source_target_pairs={{0,8},{8,0},{16,24},{24,16},{1,9},{9,1},{17,25},{25,17},{2,10},{10... | collective-permute-start | bytes 172040 | tf_op jit(solution)/shard_map/ppermute | solution.py:78
  172.1 7.9 %collective-permute-start.19 = (bf16[3,1,8,32,128]{4,2,3,0,1:T(8,128)(2,1)S(1)}, bf16[3,1,8,32,128]{4,2,3,0,1:T(8,128)(2,1)S(1)}, u32[]{:S(2)}, u32[]{:S(2)}) collective-permute-start(bf16[3,1,8,32,128]{4,2,3,0,1:T(8,128)(2,1)S(1)} %get-tuple-element.25), channel_id=1, source_target_pairs={{8,0},{16,8},{24,16},{9,1},{17,9},{25,17},{10,2},{18,10},{26,18},{... | collective-permute-start | bytes 589832 | tf_op jit(solution)/shard_map/ppermute | solution.py:17
  173.4 7.9 %collective-permute-start.18 = (bf16[3,1,8,32,128]{4,2,3,0,1:T(8,128)(2,1)S(1)}, bf16[3,1,8,32,128]{4,2,3,0,1:T(8,128)(2,1)S(1)}, u32[]{:S(2)}, u32[]{:S(2)}) collective-permute-start(bf16[3,1,8,32,128]{4,2,3,0,1:T(8,128)(2,1)S(1)} %get-tuple-element.24), channel_id=1, source_target_pairs={{0,8},{8,16},{16,24},{1,9},{9,17},{17,25},{2,10},{10,18},{18,26},{... | collective-permute-start | bytes 589832 | tf_op jit(solution)/shard_map/ppermute | solution.py:15
  178.0 10.3 %collective-permute-start.13 = (f32[112,128]{1,0:T(8,128)S(1)}, f32[112,128]{1,0:T(8,128)S(1)}, u32[]{:S(2)}, u32[]{:S(2)}) collective-permute-start(f32[112,128]{1,0:T(8,128)S(1)} %dynamic-slice_add_fusion.9), channel_id=1, source_target_pairs={{0,8},{8,0},{16,24},{24,16},{1,9},{9,1},{17,25},{25,17},{2,10},{10... | collective-permute-start | bytes 172040 | tf_op jit(solution)/shard_map/ppermute | solution.py:82
  182.4 16.1 %collective-permute-start.21 = (bf16[3,10,1,32,128]{4,2,3,0,1:T(2,128)(2,1)S(1)}, bf16[3,10,1,32,128]{4,2,3,0,1:T(2,128)(2,1)S(1)}, u32[]{:S(2)}, u32[]{:S(2)}) collective-permute-start(bf16[3,10,1,32,128]{4,2,3,0,1:T(2,128)(2,1)S(1)} %get-tuple-element.19), channel_id=1, source_target_pairs={{2,0},{4,2},{6,4},{3,1},{5,3},{7,5},{10,8},{12,10},{14,12},{11,9},... | collective-permute-start | bytes 737288 | tf_op jit(solution)/shard_map/ppermute | solution.py:17
  183.7 14.8 %collective-permute-start.20 = (bf16[3,10,1,32,128]{4,2,3,0,1:T(2,128)(2,1)S(1)}, bf16[3,10,1,32,128]{4,2,3,0,1:T(2,128)(2,1)S(1)}, u32[]{:S(2)}, u32[]{:S(2)}) collective-permute-start(bf16[3,10,1,32,128]{4,2,3,0,1:T(2,128)(2,1)S(1)} %get-tuple-element.18), channel_id=1, source_target_pairs={{0,2},{2,4},{4,6},{1,3},{3,5},{5,7},{8,10},{10,12},{12,14},{9,11},... | collective-permute-start | bytes 737288 | tf_op jit(solution)/shard_map/ppermute | solution.py:15
  188.4 16.5 %collective-permute-start.14 = (f32[224,128]{1,0:T(8,128)S(1)}, f32[224,128]{1,0:T(8,128)S(1)}, u32[]{:S(2)}, u32[]{:S(2)}) collective-permute-start(f32[224,128]{1,0:T(8,128)S(1)} %pad_maximum_fusion.16), channel_id=1, source_target_pairs={{0,16},{8,24},{16,0},{24,8},{1,17},{9,25},{17,1},{25,9},{2,18},{10... | collective-permute-start | bytes 344072 | tf_op jit(solution)/shard_map/ppermute | solution.py:82
  205.0 10.0 %collective-permute-start.15 = (f32[448,128]{1,0:T(8,128)S(1)}, f32[448,128]{1,0:T(8,128)S(1)}, u32[]{:S(2)}, u32[]{:S(2)}) collective-permute-start(f32[448,128]{1,0:T(8,128)S(1)} %pad_maximum_fusion.14), channel_id=1, source_target_pairs={{0,2},{2,0},{4,6},{6,4},{1,3},{3,1},{5,7},{7,5},{8,10},{10,8},{12,... | collective-permute-start | bytes 688136 | tf_op jit(solution)/shard_map/ppermute | solution.py:82
  215.0 25.5 %collective-permute-start.16 = (f32[896,128]{1,0:T(8,128)S(1)}, f32[896,128]{1,0:T(8,128)S(1)}, u32[]{:S(2)}, u32[]{:S(2)}) collective-permute-start(f32[896,128]{1,0:T(8,128)S(1)} %pad_maximum_fusion.9), channel_id=1, source_target_pairs={{0,4},{2,6},{4,0},{6,2},{1,5},{3,7},{5,1},{7,3},{8,12},{10,14},{12... | collective-permute-start | bytes 1376264 | tf_op jit(solution)/shard_map/ppermute | solution.py:82
  242.3 29.2 %collective-permute-start.17 = (f32[1792,128]{1,0:T(8,128)}, f32[1792,128]{1,0:T(8,128)}, u32[]{:S(2)}, u32[]{:S(2)}) collective-permute-start(f32[1792,128]{1,0:T(8,128)} %pad_maximum_fusion.4), channel_id=1, source_target_pairs={{0,1},{1,0},{2,3},{3,2},{4,5},{5,4},{6,7},{7,6},{8,9},{9,8},{10,11... | collective-permute-start | bytes 2752520 | tf_op jit(solution)/shard_map/ppermute | solution.py:82
  274.4 2.5 collective-permute-start.22
  277.1 12.6 %collective-permute-start.23 = (f32[896,128]{1,0:T(8,128)S(1)}, f32[896,128]{1,0:T(8,128)S(1)}, u32[]{:S(2)}, u32[]{:S(2)}) collective-permute-start(f32[896,128]{1,0:T(8,128)S(1)} %constant_dynamic-slice_fusion.3), channel_id=1, source_target_pairs={{0,4},{2,6},{4,0},{6,2},{1,5},{3,7},{5,1},{7,3},{8,12},{10,14},{12... | collective-permute-start | bytes 1376264 | tf_op jit(solution)/shard_map/ppermute | solution.py:78
  289.8 6.9 %collective-permute-start.24 = (f32[448,128]{1,0:T(8,128)S(1)}, f32[448,128]{1,0:T(8,128)S(1)}, u32[]{:S(2)}, u32[]{:S(2)}) collective-permute-start(f32[448,128]{1,0:T(8,128)S(1)} %constant_dynamic-slice_fusion.2), channel_id=1, source_target_pairs={{0,2},{2,0},{4,6},{6,4},{1,3},{3,1},{5,7},{7,5},{8,10},{10,8},{12,... | collective-permute-start | bytes 688136 | tf_op jit(solution)/shard_map/ppermute | solution.py:78
  296.8 8.9 %collective-permute-start.25 = (f32[224,128]{1,0:T(8,128)S(1)}, f32[224,128]{1,0:T(8,128)S(1)}, u32[]{:S(2)}, u32[]{:S(2)}) collective-permute-start(f32[224,128]{1,0:T(8,128)S(1)} %constant_dynamic-slice_fusion.1), channel_id=1, source_target_pairs={{0,16},{8,24},{16,0},{24,8},{1,17},{9,25},{17,1},{25,9},{2,18},{10... | collective-permute-start | bytes 344072 | tf_op jit(solution)/shard_map/ppermute | solution.py:78
  305.7 4.7 %collective-permute-start.26 = (f32[112,128]{1,0:T(8,128)S(1)}, f32[112,128]{1,0:T(8,128)S(1)}, u32[]{:S(2)}, u32[]{:S(2)}) collective-permute-start(f32[112,128]{1,0:T(8,128)S(1)} %constant_dynamic-slice_fusion), channel_id=1, source_target_pairs={{0,8},{8,0},{16,24},{24,16},{1,9},{9,1},{17,25},{25,17},{2,10},{10... | collective-permute-start | bytes 172040 | tf_op jit(solution)/shard_map/ppermute | solution.py:78
  310.5 4.5 %collective-permute-start.27 = (f32[112,128]{1,0:T(8,128)S(1)}, f32[112,128]{1,0:T(8,128)S(1)}, u32[]{:S(2)}, u32[]{:S(2)}) collective-permute-start(f32[112,128]{1,0:T(8,128)S(1)} %dynamic-slice_add_fusion.8), channel_id=1, source_target_pairs={{0,8},{8,0},{16,24},{24,16},{1,9},{9,1},{17,25},{25,17},{2,10},{10... | collective-permute-start | bytes 172040 | tf_op jit(solution)/shard_map/ppermute | solution.py:82
  315.0 7.0 %collective-permute-start.28 = (f32[224,128]{1,0:T(8,128)S(1)}, f32[224,128]{1,0:T(8,128)S(1)}, u32[]{:S(2)}, u32[]{:S(2)}) collective-permute-start(f32[224,128]{1,0:T(8,128)S(1)} %pad_maximum_fusion.17), channel_id=1, source_target_pairs={{0,16},{8,24},{16,0},{24,8},{1,17},{9,25},{17,1},{25,9},{2,18},{10... | collective-permute-start | bytes 344072 | tf_op jit(solution)/shard_map/ppermute | solution.py:82
  322.1 6.1 %collective-permute-start.29 = (f32[448,128]{1,0:T(8,128)S(1)}, f32[448,128]{1,0:T(8,128)S(1)}, u32[]{:S(2)}, u32[]{:S(2)}) collective-permute-start(f32[448,128]{1,0:T(8,128)S(1)} %pad_maximum_fusion.15), channel_id=1, source_target_pairs={{0,2},{2,0},{4,6},{6,4},{1,3},{3,1},{5,7},{7,5},{8,10},{10,8},{12,... | collective-permute-start | bytes 688136 | tf_op jit(solution)/shard_map/ppermute | solution.py:82
  328.2 8.5 %collective-permute-start.30 = (f32[896,128]{1,0:T(8,128)S(1)}, f32[896,128]{1,0:T(8,128)S(1)}, u32[]{:S(2)}, u32[]{:S(2)}) collective-permute-start(f32[896,128]{1,0:T(8,128)S(1)} %pad_maximum_fusion.10), channel_id=1, source_target_pairs={{0,4},{2,6},{4,0},{6,2},{1,5},{3,7},{5,1},{7,3},{8,12},{10,14},{12... | collective-permute-start | bytes 1376264 | tf_op jit(solution)/shard_map/ppermute | solution.py:82
  336.9 2.5 collective-permute-start.31
  (21 other events, 269.1 us)

commit v4 on v1

--- a/solution.py
+++ b/solution.py
@@ -77,13 +77,14 @@
         send = lax.dynamic_slice_in_dim(rows, (1 - side) * half, half, 0)
         rows = keep + lax.ppermute(send, axis, pairs)
         sides.append(side)
+    rows = rows.astype(jnp.bfloat16)
     for (axis, n, bit), side in zip(reversed(steps), reversed(sides)):
         pairs = [(i, i ^ bit) for i in range(n)]
         other = lax.ppermute(rows, axis, pairs)
         low = jnp.where(side == 0, rows, other)
         high = jnp.where(side == 0, other, rows)
         rows = jnp.concatenate([low, high], 0)
-    return rows.reshape(-1)[:size].reshape(value.shape)
+    return rows.reshape(-1)[:size].reshape(value.shape).astype(value.dtype)
 
 
 def weight_grad(padded, delta_field):

time: 320 us -> 314 us (0.981)
  waiting for transfers between devices: 107 us -> 97.7 us
  starting transfers between devices: 43 us -> 48.3 us
    ppermute x10, waiting for transfers between devices: 34.5 us -> 28.3 us  [tree_sum(): rows = keep + lax.ppermute(send, axis, pairs)]
    ppermute x10, starting transfers between devices: 4.26 us -> 9.22 us  [tree_sum(): other = lax.ppermute(rows, axis, pairs)]
    concatenate x10, other arithmetic: 3.65 us -> 0.25 us  [tree_sum(): rows = jnp.concatenate([low, high], 0)]
  transfers between devices with their start and end apart: 32 -> 32, of which waited for: 25 -> 27; matrix products, arithmetic and copies ran while one was open for 32% -> 32% of each run, Pallas kernels for 0% -> 0%
where the time goes in v4:
time: 314 us; the launch traced here: 311 us
  matrix products  105 us (33%)
  waiting for transfers between devices  97.7 us (31%)
  starting transfers between devices  48.3 us (15%)
  local copies, waits for them, and re-layouts  29.8 us (9%)
  other arithmetic  28.6 us (9%)
    conv_general_dilated x3, matrix products, conv_block(): lax.conv_general_dilated(padded, cube_kernel, (1, 1, 1), ((0, 0), (0, 0),...  53.1 us
    conv_general_dilated x2, matrix products, kernel_grad(): lax.conv_general_dilated(padded, delta_field, (1, 1, 1), ((0, 0), (0, 0),...  51.6 us
    ppermute x6, waiting for transfers between devices, extended(): lax.ppermute(head, axis, [((i + 1) % count, i) for i in range(ends)])  33.1 us
    ppermute x10, waiting for transfers between devices, tree_sum(): rows = keep + lax.ppermute(send, axis, pairs)  28.3 us
    ppermute x6, starting transfers between devices, extended(): lax.ppermute(tail, axis, [(i, (i + 1) % count) for i in range(ends)])  21.9 us
    ppermute x6, waiting for transfers between devices, extended(): lax.ppermute(tail, axis, [(i, (i + 1) % count) for i in range(ends)])  18.3 us
    ppermute x10, waiting for transfers between devices, tree_sum(): other = lax.ppermute(rows, axis, pairs)  18 us
    unnamed x40, local copies, waits for them, and re-layouts  10.7 us
  transfers between devices with their start and end apart: 32, of which 27 were waited for; matrix products, arithmetic and copies ran while one was open for 32% of the time, Pallas kernels for 0%

profile of v4, /device:TPU:0, one launch (start us, length us, event | category | flops | bytes accessed | tf_op | source)
XLA Modules:
  0.0 310.9 jit_solution(16376343199115199773)
XLA Ops:
  2.0 4.9 %collective-permute-start = (bf16[3,1,8,32,128]{4,0,3,2,1:T(4,128)(2,1)S(1)}, bf16[3,1,8,32,128]{4,0,3,2,1:T(4,128)(2,1)S(1)}, u32[]{:S(2)}, u32[]{:S(2)}) collective-permute-start(bf16[3,1,8,32,128]{4,0,3,2,1:T(4,128)(2,1)S(1)} %copy.55), channel_id=1, source_target_pairs={{0,8},{8,16},{16,24},{1,9},{9,17},{17,25},{2,10},{10,18},{18,26},{... | collective-permute-start | bytes 589832 | tf_op jit(solution)/shard_map/ppermute | solution.py:15
  8.4 4.1 %collective-permute-done = bf16[3,1,8,32,128]{4,0,3,2,1:T(4,128)(2,1)S(1)} collective-permute-done((bf16[3,1,8,32,128]{4,0,3,2,1:T(4,128)(2,1)S(1)}, bf16[3,1,8,32,128]{4,0,3,2,1:T(4,128)(2,1)S(1)}, u32[]{:S(2)}, u32[]{:S(2)}) %collective-permute-start) | collective-permute-done | bytes 196640 | tf_op jit(solution)/shard_map/ppermute | solution.py:15
  12.5 2.9 constant_dynamic-update-slice_fusion.1
  17.2 3.4 %collective-permute-start.2 = (bf16[3,10,1,32,128]{4,0,3,2,1:T(4,128)(2,1)S(1)}, bf16[3,10,1,32,128]{4,0,3,2,1:T(4,128)(2,1)S(1)}, u32[]{:S(2)}, u32[]{:S(2)}) collective-permute-start(bf16[3,10,1,32,128]{4,0,3,2,1:T(4,128)(2,1)S(1)} %get-tuple-element.10), channel_id=1, source_target_pairs={{0,2},{2,4},{4,6},{1,3},{3,5},{5,7},{8,10},{10,12},{12,14},{9,11},... | collective-permute-start | bytes 737288 | tf_op jit(solution)/shard_map/ppermute | solution.py:15
  22.1 4.3 %collective-permute-done.2 = bf16[3,10,1,32,128]{4,0,3,2,1:T(4,128)(2,1)S(1)} collective-permute-done((bf16[3,10,1,32,128]{4,0,3,2,1:T(4,128)(2,1)S(1)}, bf16[3,10,1,32,128]{4,0,3,2,1:T(4,128)(2,1)S(1)}, u32[]{:S(2)}, u32[]{:S(2)}) %collective-permute-start.2) | collective-permute-done | bytes 245792 | tf_op jit(solution)/shard_map/ppermute | solution.py:15
  26.4 9.0 %collective-permute-done.3 = bf16[3,10,1,32,128]{4,0,3,2,1:T(4,128)(2,1)S(1)} collective-permute-done((bf16[3,10,1,32,128]{4,0,3,2,1:T(4,128)(2,1)S(1)}, bf16[3,10,1,32,128]{4,0,3,2,1:T(4,128)(2,1)S(1)}, u32[]{:S(2)}, u32[]{:S(2)}) %collective-permute-start.3) | collective-permute-done | bytes 245792 | tf_op jit(solution)/shard_map/ppermute | solution.py:17
  40.6 15.5 %broadcast_select_fusion.1 = f32[8,8,24,5,128]{4,2,3,1,0:T(8,128)S(1)} fusion(pred[24,5]{0,1:T(8,128)(4,1)S(1)} %copy-done.15, bf16[3,3,3,128,128]{4,3,2,1,0:T(8,128)(2,1)S(1)} %bitcast.65, bf16[10,10,3,7,2,128]{5,3,2,4,1,0:T(8,128)(2,1)S(1)} %slice.69, bf16[10,10,3,8,5,128]{5,3,2,4,1,0:T(8,128)(2,1)S(1)} %copy.21), kind=kOutput, calls=%fused_computation.42 | convolution fusion | flops 6808657920 | bytes 8964216 | tf_op jit(solution)/shard_map/conv_general_dilated | solution.py:27
  59.4 2.6 multiply_convert_fusion
  62.3 3.5 %collective-permute-start.4 = (bf16[3,1,8,32,128]{4,0,3,2,1:T(4,128)(2,1)S(1)}, bf16[3,1,8,32,128]{4,0,3,2,1:T(4,128)(2,1)S(1)}, u32[]{:S(2)}, u32[]{:S(2)}) collective-permute-start(bf16[3,1,8,32,128]{4,0,3,2,1:T(4,128)(2,1)S(1)} %get-tuple-element.12), channel_id=1, source_target_pairs={{0,8},{8,16},{16,24},{1,9},{9,17},{17,25},{2,10},{10,18},{18,26},{... | collective-permute-start | bytes 589832 | tf_op jit(solution)/shard_map/ppermute | solution.py:15
  69.6 4.4 %collective-permute-done.5 = bf16[3,1,8,32,128]{4,0,3,2,1:T(4,128)(2,1)S(1)} collective-permute-done((bf16[3,1,8,32,128]{4,0,3,2,1:T(4,128)(2,1)S(1)}, bf16[3,1,8,32,128]{4,0,3,2,1:T(4,128)(2,1)S(1)}, u32[]{:S(2)}, u32[]{:S(2)}) %collective-permute-start.5) | collective-permute-done | bytes 196640 | tf_op jit(solution)/shard_map/ppermute | solution.py:17
  75.3 4.1 %collective-permute-start.6 = (bf16[3,10,1,32,128]{4,0,3,2,1:T(4,128)(2,1)}, bf16[3,10,1,32,128]{4,0,3,2,1:T(4,128)(2,1)}, u32[]{:S(2)}, u32[]{:S(2)}) collective-permute-start(bf16[3,10,1,32,128]{4,0,3,2,1:T(4,128)(2,1)} %get-tuple-element.8), channel_id=1, source_target_pairs={{0,2},{2,4},{4,6},{1,3},{3,5},{5,7},{8,10},{10,12},{12,14},{9,11},... | collective-permute-start | bytes 737288 | tf_op jit(solution)/shard_map/ppermute | solution.py:15
  83.6 7.2 %collective-permute-done.7 = bf16[3,10,1,32,128]{4,0,3,2,1:T(4,128)(2,1)} collective-permute-done((bf16[3,10,1,32,128]{4,0,3,2,1:T(4,128)(2,1)}, bf16[3,10,1,32,128]{4,0,3,2,1:T(4,128)(2,1)}, u32[]{:S(2)}, u32[]{:S(2)}) %collective-permute-start.7) | collective-permute-done | bytes 245792 | tf_op jit(solution)/shard_map/ppermute | solution.py:17
  90.8 4.1 %fusion.51 = bf16[10,10,3,32,128]{4,2,3,1,0:T(4,128)(2,1)S(1)} fusion(bf16[3,10,1,32,128]{4,0,3,2,1:T(4,128)(2,1)} %collective-permute-done.7, bf16[3,1,8,32,128]{4,0,3,2,1:T(4,128)(2,1)S(1)} %collective-permute-done.5, bf16[3,8,8,32,128]{4,0,3,2,1:T(4,128)(2,1)S(1)} %multiply_convert_fusion, bf16[3,1,8,32,128]{4,0,3,2,1:T(4,128)(2,1)S(1)} %collective-permute-done.4, ...), kind=kLoop, calls=%fused_computation.117 | loop fusion | flops 4915200 | bytes 4915200 | tf_op jit(solution)/shard_map/concatenate | solution.py:13
  97.5 17.0 %add_multiply_fusion = (f32[8,8,24,5,128]{4,2,3,1,0:T(8,128)S(1)}, bf16[8,8,24,5,128]{4,2,3,1,0:T(8,128)(2,1)}) fusion(pred[24,5]{0,1:T(8,128)(4,1)S(1)} %copy-done.15, bf16[3,3,3,128,128]{4,3,2,1,0:T(8,128)(2,1)S(1)} %bitcast.79, bf16[10,10,3,7,2,128]{5,3,2,4,1,0:T(8,128)(2,1)S(1)} %slice.73, bf16[10,10,3,8,5,128]{5,3,2,4,1,0:T(8,128)(2,1)S(1)} %copy.25), kind=kOutput, calls=%fused_computation.28 | convolution fusion | flops 6817505280 | bytes 10930296 | tf_op jit(solution)/shard_map/conv_general_dilated | solution.py:27
  117.8 4.5 %collective-permute-start.8 = (bf16[3,1,8,32,128]{4,2,3,0,1:T(8,128)(2,1)}, bf16[3,1,8,32,128]{4,2,3,0,1:T(8,128)(2,1)}, u32[]{:S(2)}, u32[]{:S(2)}) collective-permute-start(bf16[3,1,8,32,128]{4,2,3,0,1:T(8,128)(2,1)} %get-tuple-element.16), channel_id=1, source_target_pairs={{0,8},{8,16},{16,24},{1,9},{9,17},{17,25},{2,10},{10,18},{18,26},{... | collective-permute-start | bytes 589832 | tf_op jit(solution)/shard_map/ppermute | solution.py:15
  123.7 24.2 %fusion.27 = f32[3,3,3,128,128]{4,3,2,1,0:T(8,128)S(1)} fusion(bf16[3,8,8,32,128]{4,2,3,0,1:T(8,128)(2,1)S(1)} %fusion.24, bf16[3,10,1,32,128]{4,0,3,2,1:T(4,128)(2,1)} %collective-permute-done.7, bf16[3,1,8,32,128]{4,0,3,2,1:T(4,128)(2,1)S(1)} %collective-permute-done.5, bf16[3,8,8,32,128]{4,0,3,2,1:T(4,128)(2,1)S(1)} %multiply_convert_fusion, ...), kind=kOutput, calls=%fused_computation.38 | convolution fusion | flops 5334859776 | bytes 5799936 | tf_op jit(solution)/shard_map/conv_general_dilated | solution.py:39
  148.0 2.7 pad_maximum_fusion.6
  154.5 5.6 %collective-permute-done.10 = bf16[3,10,1,32,128]{4,2,3,0,1:T(2,128)(2,1)S(1)} collective-permute-done((bf16[3,10,1,32,128]{4,2,3,0,1:T(2,128)(2,1)S(1)}, bf16[3,10,1,32,128]{4,2,3,0,1:T(2,128)(2,1)S(1)}, u32[]{:S(2)}, u32[]{:S(2)}) %collective-permute-start.10) | collective-permute-done | bytes 245792 | tf_op jit(solution)/shard_map/ppermute | solution.py:15
  160.1 11.3 %collective-permute-done.11 = bf16[3,10,1,32,128]{4,2,3,0,1:T(2,128)(2,1)S(1)} collective-permute-done((bf16[3,10,1,32,128]{4,2,3,0,1:T(2,128)(2,1)S(1)}, bf16[3,10,1,32,128]{4,2,3,0,1:T(2,128)(2,1)S(1)}, u32[]{:S(2)}, u32[]{:S(2)}) %collective-permute-start.11) | collective-permute-done | bytes 245792 | tf_op jit(solution)/shard_map/ppermute | solution.py:17
  171.4 3.8 %maximum_bitcast_fusion = bf16[10,10,3,32,128]{4,1,3,2,0:T(8,128)(2,1)S(1)} fusion(bf16[3,10,1,32,128]{4,2,3,0,1:T(2,128)(2,1)S(1)} %collective-permute-done.11, bf16[3,1,8,32,128]{4,2,3,0,1:T(8,128)(2,1)} %collective-permute-done.9, bf16[3,8,8,32,128]{4,2,3,0,1:T(8,128)(2,1)S(1)} %fusion.24, bf16[3,1,8,32,128]{4,2,3,0,1:T(8,128)(2,1)} %collective-permute-done.8, ...), kind=kLoop, calls=%fused_computation.27 | loop fusion | flops 12288000 | bytes 4915200 | tf_op jit(solution)/shard_map/concatenate | solution.py:13
  178.6 2.8 fusion.3
  181.4 20.5 %broadcast_select_fusion = f32[8,8,24,5,128]{4,2,3,1,0:T(8,128)S(1)} fusion(pred[24,5]{0,1:T(8,128)(4,1)S(1)} %copy-done.16, bf16[3,3,3,128,128]{3,4,2,1,0:T(8,128)(2,1)S(1)} %bitcast.80, bf16[10,10,3,8,7,128]{5,4,3,2,1,0:T(8,128)(2,1)S(1)} %fusion.3), kind=kOutput, calls=%fused_computation.41 | convolution fusion | flops 6795755520 | bytes 9117816 | tf_op jit(solution)/shard_map/conv_general_dilated | solution.py:27
  205.1 27.5 %fusion.29 = f32[3,3,3,128,128]{4,3,2,1,0:T(8,128)S(1)} fusion(f32[8,8,3,32,128]{4,1,3,2,0:T(8,128)S(1)} %slice.79, f32[3,8,8,32,128]{4,0,3,2,1:T(4,128)S(1)} %bitcast.68, bf16[3,10,1,32,128]{4,0,3,2,1:T(4,128)(2,1)S(1)} %copy-done.14, bf16[3,10,8,32,128]{4,0,3,2,1:T(4,128)(2,1)S(1)} %copy-done.7, bf16[3,10,1,32,128]{4,0,3,2,1:T(4,128)(2,1)S(1)} %copy-done.12), kind=kOutput, calls=%fused_computation.40 | convolution fusion | flops 5337022464 | bytes 10518528 | tf_op jit(solution)/shard_map/conv_general_dilated | solution.py:39
  237.8 10.4 %collective-permute-done.23 = f32[896,128]{1,0:T(8,128)} collective-permute-done((f32[896,128]{1,0:T(8,128)S(1)}, f32[896,128]{1,0:T(8,128)}, u32[]{:S(2)}, u32[]{:S(2)}) %collective-permute-start.23) | collective-permute-done | bytes 458784 | tf_op jit(solution)/shard_map/ppermute | solution.py:78
  250.6 5.1 %collective-permute-done.24 = f32[448,128]{1,0:T(8,128)S(1)} collective-permute-done((f32[448,128]{1,0:T(8,128)S(1)}, f32[448,128]{1,0:T(8,128)S(1)}, u32[]{:S(2)}, u32[]{:S(2)}) %collective-permute-start.24) | collective-permute-done | bytes 229408 | tf_op jit(solution)/shard_map/ppermute | solution.py:78
  255.8 2.8 collective-permute-start.25
  277.9 4.2 %collective-permute-done.15 = f32[224,128]{1,0:T(8,128)S(1)} collective-permute-done((f32[224,128]{1,0:T(8,128)S(1)}, f32[224,128]{1,0:T(8,128)S(1)}, u32[]{:S(2)}, u32[]{:S(2)}) %collective-permute-start.15) | collective-permute-done | bytes 114720 | tf_op jit(solution)/shard_map/ppermute | solution.py:78
  283.1 3.2 %collective-permute-done.16 = f32[112,128]{1,0:T(8,128)S(1)} collective-permute-done((f32[112,128]{1,0:T(8,128)S(1)}, f32[112,128]{1,0:T(8,128)S(1)}, u32[]{:S(2)}, u32[]{:S(2)}) %collective-permute-start.16) | collective-permute-done | bytes 57376 | tf_op jit(solution)/shard_map/ppermute | solution.py:78
  287.5 2.9 collective-permute-done.17
  292.5 3.4 %collective-permute-done.18 = bf16[224,128]{1,0:T(8,128)(2,1)S(1)} collective-permute-done((bf16[224,128]{1,0:T(8,128)(2,1)S(1)}, bf16[224,128]{1,0:T(8,128)(2,1)S(1)}, u32[]{:S(2)}, u32[]{:S(2)}) %collective-permute-start.18) | collective-permute-done | bytes 57376 | tf_op jit(solution)/shard_map/ppermute | solution.py:83
  296.5 3.7 %collective-permute-done.30 = bf16[896,128]{1,0:T(8,128)(2,1)S(1)} collective-permute-done((bf16[896,128]{1,0:T(8,128)(2,1)S(1)}, bf16[896,128]{1,0:T(8,128)(2,1)S(1)}, u32[]{:S(2)}, u32[]{:S(2)}) %collective-permute-start.30) | collective-permute-done | bytes 229408 | tf_op jit(solution)/shard_map/ppermute | solution.py:83
  302.0 5.0 %collective-permute-done.20 = bf16[896,128]{1,0:T(8,128)(2,1)S(1)} collective-permute-done((bf16[896,128]{1,0:T(8,128)(2,1)S(1)}, bf16[896,128]{1,0:T(8,128)(2,1)S(1)}, u32[]{:S(2)}, u32[]{:S(2)}) %collective-permute-start.20) | collective-permute-done | bytes 229408 | tf_op jit(solution)/shard_map/ppermute | solution.py:83
  (151 shorter events, 78.7 us)
Async XLA Ops:
  2.0 10.5 %collective-permute-start = (bf16[3,1,8,32,128]{4,0,3,2,1:T(4,128)(2,1)S(1)}, bf16[3,1,8,32,128]{4,0,3,2,1:T(4,128)(2,1)S(1)}, u32[]{:S(2)}, u32[]{:S(2)}) collective-permute-start(bf16[3,1,8,32,128]{4,0,3,2,1:T(4,128)(2,1)S(1)} %copy.55), channel_id=1, source_target_pairs={{0,8},{8,16},{16,24},{1,9},{9,17},{17,25},{2,10},{10,18},{18,26},{... | collective-permute-start | bytes 589832 | tf_op jit(solution)/shard_map/ppermute | solution.py:15
  7.1 9.7 %collective-permute-start.1 = (bf16[3,1,8,32,128]{4,0,3,2,1:T(4,128)(2,1)S(1)}, bf16[3,1,8,32,128]{4,0,3,2,1:T(4,128)(2,1)S(1)}, u32[]{:S(2)}, u32[]{:S(2)}) collective-permute-start(bf16[3,1,8,32,128]{4,0,3,2,1:T(4,128)(2,1)S(1)} %copy.56), channel_id=1, source_target_pairs={{8,0},{16,8},{24,16},{9,1},{17,9},{25,17},{10,2},{18,10},{26,18},{... | collective-permute-start | bytes 589832 | tf_op jit(solution)/shard_map/ppermute | solution.py:17
  17.2 9.2 %collective-permute-start.2 = (bf16[3,10,1,32,128]{4,0,3,2,1:T(4,128)(2,1)S(1)}, bf16[3,10,1,32,128]{4,0,3,2,1:T(4,128)(2,1)S(1)}, u32[]{:S(2)}, u32[]{:S(2)}) collective-permute-start(bf16[3,10,1,32,128]{4,0,3,2,1:T(4,128)(2,1)S(1)} %get-tuple-element.10), channel_id=1, source_target_pairs={{0,2},{2,4},{4,6},{1,3},{3,5},{5,7},{8,10},{10,12},{12,14},{9,11},... | collective-permute-start | bytes 737288 | tf_op jit(solution)/shard_map/ppermute | solution.py:15
  20.6 14.7 %collective-permute-start.3 = (bf16[3,10,1,32,128]{4,0,3,2,1:T(4,128)(2,1)S(1)}, bf16[3,10,1,32,128]{4,0,3,2,1:T(4,128)(2,1)S(1)}, u32[]{:S(2)}, u32[]{:S(2)}) collective-permute-start(bf16[3,10,1,32,128]{4,0,3,2,1:T(4,128)(2,1)S(1)} %get-tuple-element.11), channel_id=1, source_target_pairs={{2,0},{4,2},{6,4},{3,1},{5,3},{7,5},{10,8},{12,10},{14,12},{11,9},... | collective-permute-start | bytes 737288 | tf_op jit(solution)/shard_map/ppermute | solution.py:17
  62.3 7.3 %collective-permute-start.4 = (bf16[3,1,8,32,128]{4,0,3,2,1:T(4,128)(2,1)S(1)}, bf16[3,1,8,32,128]{4,0,3,2,1:T(4,128)(2,1)S(1)}, u32[]{:S(2)}, u32[]{:S(2)}) collective-permute-start(bf16[3,1,8,32,128]{4,0,3,2,1:T(4,128)(2,1)S(1)} %get-tuple-element.12), channel_id=1, source_target_pairs={{0,8},{8,16},{16,24},{1,9},{9,17},{17,25},{2,10},{10,18},{18,26},{... | collective-permute-start | bytes 589832 | tf_op jit(solution)/shard_map/ppermute | solution.py:15
  65.7 8.3 %collective-permute-start.5 = (bf16[3,1,8,32,128]{4,0,3,2,1:T(4,128)(2,1)S(1)}, bf16[3,1,8,32,128]{4,0,3,2,1:T(4,128)(2,1)S(1)}, u32[]{:S(2)}, u32[]{:S(2)}) collective-permute-start(bf16[3,1,8,32,128]{4,0,3,2,1:T(4,128)(2,1)S(1)} %get-tuple-element.13), channel_id=1, source_target_pairs={{8,0},{16,8},{24,16},{9,1},{17,9},{25,17},{10,2},{18,10},{26,18},{... | collective-permute-start | bytes 589832 | tf_op jit(solution)/shard_map/ppermute | solution.py:17
  75.3 8.3 %collective-permute-start.6 = (bf16[3,10,1,32,128]{4,0,3,2,1:T(4,128)(2,1)}, bf16[3,10,1,32,128]{4,0,3,2,1:T(4,128)(2,1)}, u32[]{:S(2)}, u32[]{:S(2)}) collective-permute-start(bf16[3,10,1,32,128]{4,0,3,2,1:T(4,128)(2,1)} %get-tuple-element.8), channel_id=1, source_target_pairs={{0,2},{2,4},{4,6},{1,3},{3,5},{5,7},{8,10},{10,12},{12,14},{9,11},... | collective-permute-start | bytes 737288 | tf_op jit(solution)/shard_map/ppermute | solution.py:15
  79.4 11.3 %collective-permute-start.7 = (bf16[3,10,1,32,128]{4,0,3,2,1:T(4,128)(2,1)}, bf16[3,10,1,32,128]{4,0,3,2,1:T(4,128)(2,1)}, u32[]{:S(2)}, u32[]{:S(2)}) collective-permute-start(bf16[3,10,1,32,128]{4,0,3,2,1:T(4,128)(2,1)} %get-tuple-element.9), channel_id=1, source_target_pairs={{2,0},{4,2},{6,4},{3,1},{5,3},{7,5},{10,8},{12,10},{14,12},{11,9},... | collective-permute-start | bytes 737288 | tf_op jit(solution)/shard_map/ppermute | solution.py:17
  117.8 30.2 %collective-permute-start.8 = (bf16[3,1,8,32,128]{4,2,3,0,1:T(8,128)(2,1)}, bf16[3,1,8,32,128]{4,2,3,0,1:T(8,128)(2,1)}, u32[]{:S(2)}, u32[]{:S(2)}) collective-permute-start(bf16[3,1,8,32,128]{4,2,3,0,1:T(8,128)(2,1)} %get-tuple-element.16), channel_id=1, source_target_pairs={{0,8},{8,16},{16,24},{1,9},{9,17},{17,25},{2,10},{10,18},{18,26},{... | collective-permute-start | bytes 589832 | tf_op jit(solution)/shard_map/ppermute | solution.py:15
  122.3 25.8 %collective-permute-start.9 = (bf16[3,1,8,32,128]{4,2,3,0,1:T(8,128)(2,1)}, bf16[3,1,8,32,128]{4,2,3,0,1:T(8,128)(2,1)}, u32[]{:S(2)}, u32[]{:S(2)}) collective-permute-start(bf16[3,1,8,32,128]{4,2,3,0,1:T(8,128)(2,1)} %get-tuple-element.17), channel_id=1, source_target_pairs={{8,0},{16,8},{24,16},{9,1},{17,9},{25,17},{10,2},{18,10},{26,18},{... | collective-permute-start | bytes 589832 | tf_op jit(solution)/shard_map/ppermute | solution.py:17
  150.8 9.3 %collective-permute-start.10 = (bf16[3,10,1,32,128]{4,2,3,0,1:T(2,128)(2,1)S(1)}, bf16[3,10,1,32,128]{4,2,3,0,1:T(2,128)(2,1)S(1)}, u32[]{:S(2)}, u32[]{:S(2)}) collective-permute-start(bf16[3,10,1,32,128]{4,2,3,0,1:T(2,128)(2,1)S(1)} %get-tuple-element.14), channel_id=1, source_target_pairs={{0,2},{2,4},{4,6},{1,3},{3,5},{5,7},{8,10},{10,12},{12,14},{9,11},... | collective-permute-start | bytes 737288 | tf_op jit(solution)/shard_map/ppermute | solution.py:15
  152.2 19.1 %collective-permute-start.11 = (bf16[3,10,1,32,128]{4,2,3,0,1:T(2,128)(2,1)S(1)}, bf16[3,10,1,32,128]{4,2,3,0,1:T(2,128)(2,1)S(1)}, u32[]{:S(2)}, u32[]{:S(2)}) collective-permute-start(bf16[3,10,1,32,128]{4,2,3,0,1:T(2,128)(2,1)S(1)} %get-tuple-element.15), channel_id=1, source_target_pairs={{2,0},{4,2},{6,4},{3,1},{5,3},{7,5},{10,8},{12,10},{14,12},{11,9},... | collective-permute-start | bytes 737288 | tf_op jit(solution)/shard_map/ppermute | solution.py:17
  154.5 79.2 %collective-permute-start.22 = (f32[1792,128]{1,0:T(8,128)}, f32[1792,128]{1,0:T(8,128)}, u32[]{:S(2)}, u32[]{:S(2)}) collective-permute-start(f32[1792,128]{1,0:T(8,128)} %constant_dynamic-slice_fusion.4), channel_id=1, source_target_pairs={{0,1},{1,0},{2,3},{3,2},{4,5},{5,4},{6,7},{7,6},{8,9},{9,8},{10,11... | collective-permute-start | bytes 2752520 | tf_op jit(solution)/shard_map/ppermute | solution.py:78
  233.7 15.7 %collective-permute-start.12 = (f32[1792,128]{1,0:T(8,128)}, f32[1792,128]{1,0:T(8,128)}, u32[]{:S(2)}, u32[]{:S(2)}) collective-permute-start(f32[1792,128]{1,0:T(8,128)} %constant_dynamic-slice_fusion.9), channel_id=1, source_target_pairs={{0,1},{1,0},{2,3},{3,2},{4,5},{5,4},{6,7},{7,6},{8,9},{9,8},{10,11... | collective-permute-start | bytes 2752520 | tf_op jit(solution)/shard_map/ppermute | solution.py:78
  235.8 12.4 %collective-permute-start.23 = (f32[896,128]{1,0:T(8,128)S(1)}, f32[896,128]{1,0:T(8,128)}, u32[]{:S(2)}, u32[]{:S(2)}) collective-permute-start(f32[896,128]{1,0:T(8,128)S(1)} %constant_dynamic-slice_fusion.3), channel_id=1, source_target_pairs={{0,4},{2,6},{4,0},{6,2},{1,5},{3,7},{5,1},{7,3},{8,12},{10,14},{12... | collective-permute-start | bytes 1376264 | tf_op jit(solution)/shard_map/ppermute | solution.py:78
  249.3 6.5 %collective-permute-start.24 = (f32[448,128]{1,0:T(8,128)S(1)}, f32[448,128]{1,0:T(8,128)S(1)}, u32[]{:S(2)}, u32[]{:S(2)}) collective-permute-start(f32[448,128]{1,0:T(8,128)S(1)} %constant_dynamic-slice_fusion.2), channel_id=1, source_target_pairs={{0,2},{2,0},{4,6},{6,4},{1,3},{3,1},{5,7},{7,5},{8,10},{10,8},{12,... | collective-permute-start | bytes 688136 | tf_op jit(solution)/shard_map/ppermute | solution.py:78
  255.8 5.8 %collective-permute-start.25 = (f32[224,128]{1,0:T(8,128)S(1)}, f32[224,128]{1,0:T(8,128)S(1)}, u32[]{:S(2)}, u32[]{:S(2)}) collective-permute-start(f32[224,128]{1,0:T(8,128)S(1)} %constant_dynamic-slice_fusion.1), channel_id=1, source_target_pairs={{0,16},{8,24},{16,0},{24,8},{1,17},{9,25},{17,1},{25,9},{2,18},{10... | collective-permute-start | bytes 344072 | tf_op jit(solution)/shard_map/ppermute | solution.py:78
  258.7 10.2 %collective-permute-start.13 = (f32[896,128]{1,0:T(8,128)S(1)}, f32[896,128]{1,0:T(8,128)S(1)}, u32[]{:S(2)}, u32[]{:S(2)}) collective-permute-start(f32[896,128]{1,0:T(8,128)S(1)} %constant_dynamic-slice_fusion.8), channel_id=1, source_target_pairs={{0,4},{2,6},{4,0},{6,2},{1,5},{3,7},{5,1},{7,3},{8,12},{10,14},{12... | collective-permute-start | bytes 1376264 | tf_op jit(solution)/shard_map/ppermute | solution.py:78
  261.7 4.5 %collective-permute-start.26 = (f32[112,128]{1,0:T(8,128)S(1)}, f32[112,128]{1,0:T(8,128)S(1)}, u32[]{:S(2)}, u32[]{:S(2)}) collective-permute-start(f32[112,128]{1,0:T(8,128)S(1)} %constant_dynamic-slice_fusion), channel_id=1, source_target_pairs={{0,8},{8,0},{16,24},{24,16},{1,9},{9,1},{17,25},{25,17},{2,10},{10... | collective-permute-start | bytes 172040 | tf_op jit(solution)/shard_map/ppermute | solution.py:78
  266.2 4.6 %collective-permute-start.27 = (bf16[112,128]{1,0:T(8,128)(2,1)S(1)}, bf16[112,128]{1,0:T(8,128)(2,1)S(1)}, u32[]{:S(2)}, u32[]{:S(2)}) collective-permute-start(bf16[112,128]{1,0:T(8,128)(2,1)S(1)} %add_convert_fusion), channel_id=1, source_target_pairs={{0,8},{8,0},{16,24},{24,16},{1,9},{9,1},{17,25},{25,17},{2,10},{10... | collective-permute-start | bytes 86024 | tf_op jit(solution)/shard_map/ppermute | solution.py:83
  269.0 6.1 %collective-permute-start.14 = (f32[448,128]{1,0:T(8,128)S(1)}, f32[448,128]{1,0:T(8,128)S(1)}, u32[]{:S(2)}, u32[]{:S(2)}) collective-permute-start(f32[448,128]{1,0:T(8,128)S(1)} %constant_dynamic-slice_fusion.7), channel_id=1, source_target_pairs={{0,2},{2,0},{4,6},{6,4},{1,3},{3,1},{5,7},{7,5},{8,10},{10,8},{12,... | collective-permute-start | bytes 688136 | tf_op jit(solution)/shard_map/ppermute | solution.py:78
  270.8 7.1 %collective-permute-start.28 = (bf16[224,128]{1,0:T(8,128)(2,1)S(1)}, bf16[224,128]{1,0:T(8,128)(2,1)S(1)}, u32[]{:S(2)}, u32[]{:S(2)}) collective-permute-start(bf16[224,128]{1,0:T(8,128)(2,1)S(1)} %pad_maximum_fusion.17), channel_id=1, source_target_pairs={{0,16},{8,24},{16,0},{24,8},{1,17},{9,25},{17,1},{25,9},{2,18},{10... | collective-permute-start | bytes 172040 | tf_op jit(solution)/shard_map/ppermute | solution.py:83
  275.1 7.0 %collective-permute-start.15 = (f32[224,128]{1,0:T(8,128)S(1)}, f32[224,128]{1,0:T(8,128)S(1)}, u32[]{:S(2)}, u32[]{:S(2)}) collective-permute-start(f32[224,128]{1,0:T(8,128)S(1)} %constant_dynamic-slice_fusion.6), channel_id=1, source_target_pairs={{0,16},{8,24},{16,0},{24,8},{1,17},{9,25},{17,1},{25,9},{2,18},{10... | collective-permute-start | bytes 344072 | tf_op jit(solution)/shard_map/ppermute | solution.py:78
  282.1 4.2 %collective-permute-start.16 = (f32[112,128]{1,0:T(8,128)S(1)}, f32[112,128]{1,0:T(8,128)S(1)}, u32[]{:S(2)}, u32[]{:S(2)}) collective-permute-start(f32[112,128]{1,0:T(8,128)S(1)} %constant_dynamic-slice_fusion.5), channel_id=1, source_target_pairs={{0,8},{8,0},{16,24},{24,16},{1,9},{9,1},{17,25},{25,17},{2,10},{10... | collective-permute-start | bytes 172040 | tf_op jit(solution)/shard_map/ppermute | solution.py:78
  282.6 4.9 %collective-permute-start.29 = (bf16[448,128]{1,0:T(8,128)(2,1)S(1)}, bf16[448,128]{1,0:T(8,128)(2,1)S(1)}, u32[]{:S(2)}, u32[]{:S(2)}) collective-permute-start(bf16[448,128]{1,0:T(8,128)(2,1)S(1)} %pad_maximum_fusion.15), channel_id=1, source_target_pairs={{0,2},{2,0},{4,6},{6,4},{1,3},{3,1},{5,7},{7,5},{8,10},{10,8},{12,... | collective-permute-start | bytes 344072 | tf_op jit(solution)/shard_map/ppermute | solution.py:83
  286.4 3.9 %collective-permute-start.17 = (bf16[112,128]{1,0:T(8,128)(2,1)S(1)}, bf16[112,128]{1,0:T(8,128)(2,1)S(1)}, u32[]{:S(2)}, u32[]{:S(2)}) collective-permute-start(bf16[112,128]{1,0:T(8,128)(2,1)S(1)} %add_convert_fusion.1), channel_id=1, source_target_pairs={{0,8},{8,0},{16,24},{24,16},{1,9},{9,1},{17,25},{25,17},{2,10},{10... | collective-permute-start | bytes 86024 | tf_op jit(solution)/shard_map/ppermute | solution.py:83
  290.4 5.5 %collective-permute-start.18 = (bf16[224,128]{1,0:T(8,128)(2,1)S(1)}, bf16[224,128]{1,0:T(8,128)(2,1)S(1)}, u32[]{:S(2)}, u32[]{:S(2)}) collective-permute-start(bf16[224,128]{1,0:T(8,128)(2,1)S(1)} %pad_maximum_fusion.16), channel_id=1, source_target_pairs={{0,16},{8,24},{16,0},{24,8},{1,17},{9,25},{17,1},{25,9},{2,18},{10... | collective-permute-start | bytes 172040 | tf_op jit(solution)/shard_map/ppermute | solution.py:83
  291.9 8.3 %collective-permute-start.30 = (bf16[896,128]{1,0:T(8,128)(2,1)S(1)}, bf16[896,128]{1,0:T(8,128)(2,1)S(1)}, u32[]{:S(2)}, u32[]{:S(2)}) collective-permute-start(bf16[896,128]{1,0:T(8,128)(2,1)S(1)} %pad_maximum_fusion.13), channel_id=1, source_target_pairs={{0,4},{2,6},{4,0},{6,2},{1,5},{3,7},{5,1},{7,3},{8,12},{10,14},{12... | collective-permute-start | bytes 688136 | tf_op jit(solution)/shard_map/ppermute | solution.py:83
  295.9 4.9 %collective-permute-start.19 = (bf16[448,128]{1,0:T(8,128)(2,1)S(1)}, bf16[448,128]{1,0:T(8,128)(2,1)S(1)}, u32[]{:S(2)}, u32[]{:S(2)}) collective-permute-start(bf16[448,128]{1,0:T(8,128)(2,1)S(1)} %pad_maximum_fusion.14), channel_id=1, source_target_pairs={{0,2},{2,0},{4,6},{6,4},{1,3},{3,1},{5,7},{7,5},{8,10},{10,8},{12,... | collective-permute-start | bytes 344072 | tf_op jit(solution)/shard_map/ppermute | solution.py:83
  300.9 6.1 %collective-permute-start.20 = (bf16[896,128]{1,0:T(8,128)(2,1)S(1)}, bf16[896,128]{1,0:T(8,128)(2,1)S(1)}, u32[]{:S(2)}, u32[]{:S(2)}) collective-permute-start(bf16[896,128]{1,0:T(8,128)(2,1)S(1)} %pad_maximum_fusion.12), channel_id=1, source_target_pairs={{0,4},{2,6},{4,0},{6,2},{1,5},{3,7},{5,1},{7,3},{8,12},{10,14},{12... | collective-permute-start | bytes 688136 | tf_op jit(solution)/shard_map/ppermute | solution.py:83
  301.9 5.3 %collective-permute-start.31 = (bf16[1792,128]{1,0:T(8,128)(2,1)S(1)}, bf16[1792,128]{1,0:T(8,128)(2,1)S(1)}, u32[]{:S(2)}, u32[]{:S(2)}) collective-permute-start(bf16[1792,128]{1,0:T(8,128)(2,1)S(1)} %pad_maximum_fusion.8), channel_id=1, source_target_pairs={{0,1},{1,0},{2,3},{3,2},{4,5},{5,4},{6,7},{7,6},{8,9},{9,8},{10,11... | collective-permute-start | bytes 1376264 | tf_op jit(solution)/shard_map/ppermute | solution.py:83
  307.1 1.9 collective-permute-start.21
  (17 other events, 150.3 us)

commit v5 on v4

--- a/solution.py
+++ b/solution.py
@@ -59,10 +59,10 @@
     steps = []
     total = 1
     for axis, n in zip(axes, sizes):
-        bit = n // 2
-        while bit >= 1:
+        bit = 1
+        while bit < n:
             steps.append((axis, n, bit))
-            bit //= 2
+            bit *= 2
         total *= n
     flat = value.reshape(-1)
     unit = total * 8 * 128

time: 314 us -> 313 us (level)
  transfers between devices with their start and end apart: 32 -> 32, of which waited for: 27 -> 24; matrix products, arithmetic and copies ran while one was open for 32% -> 32% of each run, Pallas kernels for 0% -> 0%
where the time goes in v5:
time: 313 us; the launch traced here: 310 us
  matrix products  105 us (34%)
  waiting for transfers between devices  95.5 us (31%)
  starting transfers between devices  49.4 us (16%)
  local copies, waits for them, and re-layouts  29.8 us (10%)
  other arithmetic  28.6 us (9%)
    conv_general_dilated x3, matrix products, conv_block(): lax.conv_general_dilated(padded, cube_kernel, (1, 1, 1), ((0, 0), (0, 0),...  53.1 us
    conv_general_dilated x2, matrix products, kernel_grad(): lax.conv_general_dilated(padded, delta_field, (1, 1, 1), ((0, 0), (0, 0),...  51.6 us
    ppermute x6, waiting for transfers between devices, extended(): lax.ppermute(head, axis, [((i + 1) % count, i) for i in range(ends)])  33.1 us
    ppermute x10, waiting for transfers between devices, tree_sum(): rows = keep + lax.ppermute(send, axis, pairs)  28.1 us
    ppermute x6, starting transfers between devices, extended(): lax.ppermute(tail, axis, [(i, (i + 1) % count) for i in range(ends)])  21.9 us
    ppermute x6, waiting for transfers between devices, extended(): lax.ppermute(tail, axis, [(i, (i + 1) % count) for i in range(ends)])  18.3 us
    ppermute x10, waiting for transfers between devices, tree_sum(): other = lax.ppermute(rows, axis, pairs)  16 us
    ppermute x10, starting transfers between devices, tree_sum(): other = lax.ppermute(rows, axis, pairs)  11 us
  transfers between devices with their start and end apart: 32, of which 24 were waited for; matrix products, arithmetic and copies ran while one was open for 32% of the time, Pallas kernels for 0%

profile of v5, /device:TPU:0, one launch (start us, length us, event | category | flops | bytes accessed | tf_op | source)
XLA Modules:
  0.0 309.8 jit_solution(4734879750368045925)
XLA Ops:
  2.0 4.9 %collective-permute-start = (bf16[3,1,8,32,128]{4,0,3,2,1:T(4,128)(2,1)S(1)}, bf16[3,1,8,32,128]{4,0,3,2,1:T(4,128)(2,1)S(1)}, u32[]{:S(2)}, u32[]{:S(2)}) collective-permute-start(bf16[3,1,8,32,128]{4,0,3,2,1:T(4,128)(2,1)S(1)} %copy.55), channel_id=1, source_target_pairs={{0,8},{8,16},{16,24},{1,9},{9,17},{17,25},{2,10},{10,18},{18,26},{... | collective-permute-start | bytes 589832 | tf_op jit(solution)/shard_map/ppermute | solution.py:15
  8.4 4.1 %collective-permute-done = bf16[3,1,8,32,128]{4,0,3,2,1:T(4,128)(2,1)S(1)} collective-permute-done((bf16[3,1,8,32,128]{4,0,3,2,1:T(4,128)(2,1)S(1)}, bf16[3,1,8,32,128]{4,0,3,2,1:T(4,128)(2,1)S(1)}, u32[]{:S(2)}, u32[]{:S(2)}) %collective-permute-start) | collective-permute-done | bytes 196640 | tf_op jit(solution)/shard_map/ppermute | solution.py:15
  12.5 2.9 constant_dynamic-update-slice_fusion.1
  17.2 3.4 %collective-permute-start.2 = (bf16[3,10,1,32,128]{4,0,3,2,1:T(4,128)(2,1)S(1)}, bf16[3,10,1,32,128]{4,0,3,2,1:T(4,128)(2,1)S(1)}, u32[]{:S(2)}, u32[]{:S(2)}) collective-permute-start(bf16[3,10,1,32,128]{4,0,3,2,1:T(4,128)(2,1)S(1)} %get-tuple-element.10), channel_id=1, source_target_pairs={{0,2},{2,4},{4,6},{1,3},{3,5},{5,7},{8,10},{10,12},{12,14},{9,11},... | collective-permute-start | bytes 737288 | tf_op jit(solution)/shard_map/ppermute | solution.py:15
  22.1 4.3 %collective-permute-done.2 = bf16[3,10,1,32,128]{4,0,3,2,1:T(4,128)(2,1)S(1)} collective-permute-done((bf16[3,10,1,32,128]{4,0,3,2,1:T(4,128)(2,1)S(1)}, bf16[3,10,1,32,128]{4,0,3,2,1:T(4,128)(2,1)S(1)}, u32[]{:S(2)}, u32[]{:S(2)}) %collective-permute-start.2) | collective-permute-done | bytes 245792 | tf_op jit(solution)/shard_map/ppermute | solution.py:15
  26.4 9.0 %collective-permute-done.3 = bf16[3,10,1,32,128]{4,0,3,2,1:T(4,128)(2,1)S(1)} collective-permute-done((bf16[3,10,1,32,128]{4,0,3,2,1:T(4,128)(2,1)S(1)}, bf16[3,10,1,32,128]{4,0,3,2,1:T(4,128)(2,1)S(1)}, u32[]{:S(2)}, u32[]{:S(2)}) %collective-permute-start.3) | collective-permute-done | bytes 245792 | tf_op jit(solution)/shard_map/ppermute | solution.py:17
  35.3 2.6 fusion.42
  40.6 15.5 %broadcast_select_fusion.1 = f32[8,8,24,5,128]{4,2,3,1,0:T(8,128)S(1)} fusion(pred[24,5]{0,1:T(8,128)(4,1)S(1)} %copy-done.15, bf16[3,3,3,128,128]{4,3,2,1,0:T(8,128)(2,1)S(1)} %bitcast.65, bf16[10,10,3,7,2,128]{5,3,2,4,1,0:T(8,128)(2,1)S(1)} %slice.69, bf16[10,10,3,8,5,128]{5,3,2,4,1,0:T(8,128)(2,1)S(1)} %copy.21), kind=kOutput, calls=%fused_computation.42 | convolution fusion | flops 6808657920 | bytes 8964216 | tf_op jit(solution)/shard_map/conv_general_dilated | solution.py:27
  59.4 2.6 multiply_convert_fusion
  62.3 3.5 %collective-permute-start.4 = (bf16[3,1,8,32,128]{4,0,3,2,1:T(4,128)(2,1)S(1)}, bf16[3,1,8,32,128]{4,0,3,2,1:T(4,128)(2,1)S(1)}, u32[]{:S(2)}, u32[]{:S(2)}) collective-permute-start(bf16[3,1,8,32,128]{4,0,3,2,1:T(4,128)(2,1)S(1)} %get-tuple-element.12), channel_id=1, source_target_pairs={{0,8},{8,16},{16,24},{1,9},{9,17},{17,25},{2,10},{10,18},{18,26},{... | collective-permute-start | bytes 589832 | tf_op jit(solution)/shard_map/ppermute | solution.py:15
  67.0 2.6 collective-permute-done.4
  69.6 4.4 %collective-permute-done.5 = bf16[3,1,8,32,128]{4,0,3,2,1:T(4,128)(2,1)S(1)} collective-permute-done((bf16[3,1,8,32,128]{4,0,3,2,1:T(4,128)(2,1)S(1)}, bf16[3,1,8,32,128]{4,0,3,2,1:T(4,128)(2,1)S(1)}, u32[]{:S(2)}, u32[]{:S(2)}) %collective-permute-start.5) | collective-permute-done | bytes 196640 | tf_op jit(solution)/shard_map/ppermute | solution.py:17
  75.3 4.1 %collective-permute-start.6 = (bf16[3,10,1,32,128]{4,0,3,2,1:T(4,128)(2,1)}, bf16[3,10,1,32,128]{4,0,3,2,1:T(4,128)(2,1)}, u32[]{:S(2)}, u32[]{:S(2)}) collective-permute-start(bf16[3,10,1,32,128]{4,0,3,2,1:T(4,128)(2,1)} %get-tuple-element.8), channel_id=1, source_target_pairs={{0,2},{2,4},{4,6},{1,3},{3,5},{5,7},{8,10},{10,12},{12,14},{9,11},... | collective-permute-start | bytes 737288 | tf_op jit(solution)/shard_map/ppermute | solution.py:15
  83.6 7.2 %collective-permute-done.7 = bf16[3,10,1,32,128]{4,0,3,2,1:T(4,128)(2,1)} collective-permute-done((bf16[3,10,1,32,128]{4,0,3,2,1:T(4,128)(2,1)}, bf16[3,10,1,32,128]{4,0,3,2,1:T(4,128)(2,1)}, u32[]{:S(2)}, u32[]{:S(2)}) %collective-permute-start.7) | collective-permute-done | bytes 245792 | tf_op jit(solution)/shard_map/ppermute | solution.py:17
  90.8 4.1 %fusion.51 = bf16[10,10,3,32,128]{4,2,3,1,0:T(4,128)(2,1)S(1)} fusion(bf16[3,10,1,32,128]{4,0,3,2,1:T(4,128)(2,1)} %collective-permute-done.7, bf16[3,1,8,32,128]{4,0,3,2,1:T(4,128)(2,1)S(1)} %collective-permute-done.5, bf16[3,8,8,32,128]{4,0,3,2,1:T(4,128)(2,1)S(1)} %multiply_convert_fusion, bf16[3,1,8,32,128]{4,0,3,2,1:T(4,128)(2,1)S(1)} %collective-permute-done.4, ...), kind=kLoop, calls=%fused_computation.117 | loop fusion | flops 4915200 | bytes 4915200 | tf_op jit(solution)/shard_map/concatenate | solution.py:13
  97.5 17.0 %add_multiply_fusion = (f32[8,8,24,5,128]{4,2,3,1,0:T(8,128)S(1)}, bf16[8,8,24,5,128]{4,2,3,1,0:T(8,128)(2,1)}) fusion(pred[24,5]{0,1:T(8,128)(4,1)S(1)} %copy-done.15, bf16[3,3,3,128,128]{4,3,2,1,0:T(8,128)(2,1)S(1)} %bitcast.79, bf16[10,10,3,7,2,128]{5,3,2,4,1,0:T(8,128)(2,1)S(1)} %slice.73, bf16[10,10,3,8,5,128]{5,3,2,4,1,0:T(8,128)(2,1)S(1)} %copy.25), kind=kOutput, calls=%fused_computation.28 | convolution fusion | flops 6817505280 | bytes 10930296 | tf_op jit(solution)/shard_map/conv_general_dilated | solution.py:27
  117.8 4.5 %collective-permute-start.8 = (bf16[3,1,8,32,128]{4,2,3,0,1:T(8,128)(2,1)}, bf16[3,1,8,32,128]{4,2,3,0,1:T(8,128)(2,1)}, u32[]{:S(2)}, u32[]{:S(2)}) collective-permute-start(bf16[3,1,8,32,128]{4,2,3,0,1:T(8,128)(2,1)} %get-tuple-element.16), channel_id=1, source_target_pairs={{0,8},{8,16},{16,24},{1,9},{9,17},{17,25},{2,10},{10,18},{18,26},{... | collective-permute-start | bytes 589832 | tf_op jit(solution)/shard_map/ppermute | solution.py:15
  123.7 24.2 %fusion.27 = f32[3,3,3,128,128]{4,3,2,1,0:T(8,128)S(1)} fusion(bf16[3,8,8,32,128]{4,2,3,0,1:T(8,128)(2,1)S(1)} %fusion.24, bf16[3,10,1,32,128]{4,0,3,2,1:T(4,128)(2,1)} %collective-permute-done.7, bf16[3,1,8,32,128]{4,0,3,2,1:T(4,128)(2,1)S(1)} %collective-permute-done.5, bf16[3,8,8,32,128]{4,0,3,2,1:T(4,128)(2,1)S(1)} %multiply_convert_fusion, ...), kind=kOutput, calls=%fused_computation.38 | convolution fusion | flops 5334859776 | bytes 5799936 | tf_op jit(solution)/shard_map/conv_general_dilated | solution.py:39
  148.0 2.7 pad_maximum_fusion.6
  154.5 5.6 %collective-permute-done.10 = bf16[3,10,1,32,128]{4,2,3,0,1:T(2,128)(2,1)S(1)} collective-permute-done((bf16[3,10,1,32,128]{4,2,3,0,1:T(2,128)(2,1)S(1)}, bf16[3,10,1,32,128]{4,2,3,0,1:T(2,128)(2,1)S(1)}, u32[]{:S(2)}, u32[]{:S(2)}) %collective-permute-start.10) | collective-permute-done | bytes 245792 | tf_op jit(solution)/shard_map/ppermute | solution.py:15
  160.1 11.3 %collective-permute-done.11 = bf16[3,10,1,32,128]{4,2,3,0,1:T(2,128)(2,1)S(1)} collective-permute-done((bf16[3,10,1,32,128]{4,2,3,0,1:T(2,128)(2,1)S(1)}, bf16[3,10,1,32,128]{4,2,3,0,1:T(2,128)(2,1)S(1)}, u32[]{:S(2)}, u32[]{:S(2)}) %collective-permute-start.11) | collective-permute-done | bytes 245792 | tf_op jit(solution)/shard_map/ppermute | solution.py:17
  171.4 3.8 %maximum_bitcast_fusion = bf16[10,10,3,32,128]{4,1,3,2,0:T(8,128)(2,1)S(1)} fusion(bf16[3,10,1,32,128]{4,2,3,0,1:T(2,128)(2,1)S(1)} %collective-permute-done.11, bf16[3,1,8,32,128]{4,2,3,0,1:T(8,128)(2,1)} %collective-permute-done.9, bf16[3,8,8,32,128]{4,2,3,0,1:T(8,128)(2,1)S(1)} %fusion.24, bf16[3,1,8,32,128]{4,2,3,0,1:T(8,128)(2,1)} %collective-permute-done.8, ...), kind=kLoop, calls=%fused_computation.27 | loop fusion | flops 12288000 | bytes 4915200 | tf_op jit(solution)/shard_map/concatenate | solution.py:13
  178.6 2.8 fusion.3
  181.4 20.5 %broadcast_select_fusion = f32[8,8,24,5,128]{4,2,3,1,0:T(8,128)S(1)} fusion(pred[24,5]{0,1:T(8,128)(4,1)S(1)} %copy-done.16, bf16[3,3,3,128,128]{3,4,2,1,0:T(8,128)(2,1)S(1)} %bitcast.80, bf16[10,10,3,8,7,128]{5,4,3,2,1,0:T(8,128)(2,1)S(1)} %fusion.3), kind=kOutput, calls=%fused_computation.41 | convolution fusion | flops 6795755520 | bytes 9117816 | tf_op jit(solution)/shard_map/conv_general_dilated | solution.py:27
  205.1 27.5 %fusion.29 = f32[3,3,3,128,128]{4,3,2,1,0:T(8,128)S(1)} fusion(f32[8,8,3,32,128]{4,1,3,2,0:T(8,128)S(1)} %slice.79, f32[3,8,8,32,128]{4,0,3,2,1:T(4,128)S(1)} %bitcast.68, bf16[3,10,1,32,128]{4,0,3,2,1:T(4,128)(2,1)S(1)} %copy-done.14, bf16[3,10,8,32,128]{4,0,3,2,1:T(4,128)(2,1)S(1)} %copy-done.7, bf16[3,10,1,32,128]{4,0,3,2,1:T(4,128)(2,1)S(1)} %copy-done.12), kind=kOutput, calls=%fused_computation.40 | convolution fusion | flops 5337022464 | bytes 10518528 | tf_op jit(solution)/shard_map/conv_general_dilated | solution.py:39
  237.8 10.3 %collective-permute-done.23 = f32[896,128]{1,0:T(8,128)} collective-permute-done((f32[896,128]{1,0:T(8,128)S(1)}, f32[896,128]{1,0:T(8,128)}, u32[]{:S(2)}, u32[]{:S(2)}) %collective-permute-start.23) | collective-permute-done | bytes 458784 | tf_op jit(solution)/shard_map/ppermute | solution.py:78
  250.6 5.1 %collective-permute-done.24 = f32[448,128]{1,0:T(8,128)S(1)} collective-permute-done((f32[448,128]{1,0:T(8,128)S(1)}, f32[448,128]{1,0:T(8,128)S(1)}, u32[]{:S(2)}, u32[]{:S(2)}) %collective-permute-start.24) | collective-permute-done | bytes 229408 | tf_op jit(solution)/shard_map/ppermute | solution.py:78
  266.5 2.6 collective-permute-start.27
  277.2 3.3 %collective-permute-done.15 = f32[224,128]{1,0:T(8,128)S(1)} collective-permute-done((f32[224,128]{1,0:T(8,128)S(1)}, f32[224,128]{1,0:T(8,128)S(1)}, u32[]{:S(2)}, u32[]{:S(2)}) %collective-permute-start.15) | collective-permute-done | bytes 114720 | tf_op jit(solution)/shard_map/ppermute | solution.py:78
  281.7 4.0 %collective-permute-done.16 = f32[112,128]{1,0:T(8,128)S(1)} collective-permute-done((f32[112,128]{1,0:T(8,128)S(1)}, f32[112,128]{1,0:T(8,128)S(1)}, u32[]{:S(2)}, u32[]{:S(2)}) %collective-permute-start.16) | collective-permute-done | bytes 57376 | tf_op jit(solution)/shard_map/ppermute | solution.py:78
  286.3 4.3 %collective-permute-done.17 = bf16[112,128]{1,0:T(8,128)(2,1)S(1)} collective-permute-done((bf16[112,128]{1,0:T(8,128)(2,1)S(1)}, bf16[112,128]{1,0:T(8,128)(2,1)S(1)}, u32[]{:S(2)}, u32[]{:S(2)}) %collective-permute-start.17) | collective-permute-done | bytes 28704 | tf_op jit(solution)/shard_map/ppermute | solution.py:83
  301.6 4.3 %collective-permute-done.20 = bf16[896,128]{1,0:T(8,128)(2,1)S(1)} collective-permute-done((bf16[896,128]{1,0:T(8,128)(2,1)S(1)}, bf16[896,128]{1,0:T(8,128)(2,1)S(1)}, u32[]{:S(2)}, u32[]{:S(2)}) %collective-permute-start.20) | collective-permute-done | bytes 229408 | tf_op jit(solution)/shard_map/ppermute | solution.py:83
  (151 shorter events, 79.2 us)
Async XLA Ops:
  2.0 10.5 %collective-permute-start = (bf16[3,1,8,32,128]{4,0,3,2,1:T(4,128)(2,1)S(1)}, bf16[3,1,8,32,128]{4,0,3,2,1:T(4,128)(2,1)S(1)}, u32[]{:S(2)}, u32[]{:S(2)}) collective-permute-start(bf16[3,1,8,32,128]{4,0,3,2,1:T(4,128)(2,1)S(1)} %copy.55), channel_id=1, source_target_pairs={{0,8},{8,16},{16,24},{1,9},{9,17},{17,25},{2,10},{10,18},{18,26},{... | collective-permute-start | bytes 589832 | tf_op jit(solution)/shard_map/ppermute | solution.py:15
  7.1 9.7 %collective-permute-start.1 = (bf16[3,1,8,32,128]{4,0,3,2,1:T(4,128)(2,1)S(1)}, bf16[3,1,8,32,128]{4,0,3,2,1:T(4,128)(2,1)S(1)}, u32[]{:S(2)}, u32[]{:S(2)}) collective-permute-start(bf16[3,1,8,32,128]{4,0,3,2,1:T(4,128)(2,1)S(1)} %copy.56), channel_id=1, source_target_pairs={{8,0},{16,8},{24,16},{9,1},{17,9},{25,17},{10,2},{18,10},{26,18},{... | collective-permute-start | bytes 589832 | tf_op jit(solution)/shard_map/ppermute | solution.py:17
  17.2 9.2 %collective-permute-start.2 = (bf16[3,10,1,32,128]{4,0,3,2,1:T(4,128)(2,1)S(1)}, bf16[3,10,1,32,128]{4,0,3,2,1:T(4,128)(2,1)S(1)}, u32[]{:S(2)}, u32[]{:S(2)}) collective-permute-start(bf16[3,10,1,32,128]{4,0,3,2,1:T(4,128)(2,1)S(1)} %get-tuple-element.10), channel_id=1, source_target_pairs={{0,2},{2,4},{4,6},{1,3},{3,5},{5,7},{8,10},{10,12},{12,14},{9,11},... | collective-permute-start | bytes 737288 | tf_op jit(solution)/shard_map/ppermute | solution.py:15
  20.6 14.7 %collective-permute-start.3 = (bf16[3,10,1,32,128]{4,0,3,2,1:T(4,128)(2,1)S(1)}, bf16[3,10,1,32,128]{4,0,3,2,1:T(4,128)(2,1)S(1)}, u32[]{:S(2)}, u32[]{:S(2)}) collective-permute-start(bf16[3,10,1,32,128]{4,0,3,2,1:T(4,128)(2,1)S(1)} %get-tuple-element.11), channel_id=1, source_target_pairs={{2,0},{4,2},{6,4},{3,1},{5,3},{7,5},{10,8},{12,10},{14,12},{11,9},... | collective-permute-start | bytes 737288 | tf_op jit(solution)/shard_map/ppermute | solution.py:17
  62.3 7.3 %collective-permute-start.4 = (bf16[3,1,8,32,128]{4,0,3,2,1:T(4,128)(2,1)S(1)}, bf16[3,1,8,32,128]{4,0,3,2,1:T(4,128)(2,1)S(1)}, u32[]{:S(2)}, u32[]{:S(2)}) collective-permute-start(bf16[3,1,8,32,128]{4,0,3,2,1:T(4,128)(2,1)S(1)} %get-tuple-element.12), channel_id=1, source_target_pairs={{0,8},{8,16},{16,24},{1,9},{9,17},{17,25},{2,10},{10,18},{18,26},{... | collective-permute-start | bytes 589832 | tf_op jit(solution)/shard_map/ppermute | solution.py:15
  65.7 8.3 %collective-permute-start.5 = (bf16[3,1,8,32,128]{4,0,3,2,1:T(4,128)(2,1)S(1)}, bf16[3,1,8,32,128]{4,0,3,2,1:T(4,128)(2,1)S(1)}, u32[]{:S(2)}, u32[]{:S(2)}) collective-permute-start(bf16[3,1,8,32,128]{4,0,3,2,1:T(4,128)(2,1)S(1)} %get-tuple-element.13), channel_id=1, source_target_pairs={{8,0},{16,8},{24,16},{9,1},{17,9},{25,17},{10,2},{18,10},{26,18},{... | collective-permute-start | bytes 589832 | tf_op jit(solution)/shard_map/ppermute | solution.py:17
  75.3 8.3 %collective-permute-start.6 = (bf16[3,10,1,32,128]{4,0,3,2,1:T(4,128)(2,1)}, bf16[3,10,1,32,128]{4,0,3,2,1:T(4,128)(2,1)}, u32[]{:S(2)}, u32[]{:S(2)}) collective-permute-start(bf16[3,10,1,32,128]{4,0,3,2,1:T(4,128)(2,1)} %get-tuple-element.8), channel_id=1, source_target_pairs={{0,2},{2,4},{4,6},{1,3},{3,5},{5,7},{8,10},{10,12},{12,14},{9,11},... | collective-permute-start | bytes 737288 | tf_op jit(solution)/shard_map/ppermute | solution.py:15
  79.4 11.3 %collective-permute-start.7 = (bf16[3,10,1,32,128]{4,0,3,2,1:T(4,128)(2,1)}, bf16[3,10,1,32,128]{4,0,3,2,1:T(4,128)(2,1)}, u32[]{:S(2)}, u32[]{:S(2)}) collective-permute-start(bf16[3,10,1,32,128]{4,0,3,2,1:T(4,128)(2,1)} %get-tuple-element.9), channel_id=1, source_target_pairs={{2,0},{4,2},{6,4},{3,1},{5,3},{7,5},{10,8},{12,10},{14,12},{11,9},... | collective-permute-start | bytes 737288 | tf_op jit(solution)/shard_map/ppermute | solution.py:17
  117.8 30.2 %collective-permute-start.8 = (bf16[3,1,8,32,128]{4,2,3,0,1:T(8,128)(2,1)}, bf16[3,1,8,32,128]{4,2,3,0,1:T(8,128)(2,1)}, u32[]{:S(2)}, u32[]{:S(2)}) collective-permute-start(bf16[3,1,8,32,128]{4,2,3,0,1:T(8,128)(2,1)} %get-tuple-element.16), channel_id=1, source_target_pairs={{0,8},{8,16},{16,24},{1,9},{9,17},{17,25},{2,10},{10,18},{18,26},{... | collective-permute-start | bytes 589832 | tf_op jit(solution)/shard_map/ppermute | solution.py:15
  122.3 25.8 %collective-permute-start.9 = (bf16[3,1,8,32,128]{4,2,3,0,1:T(8,128)(2,1)}, bf16[3,1,8,32,128]{4,2,3,0,1:T(8,128)(2,1)}, u32[]{:S(2)}, u32[]{:S(2)}) collective-permute-start(bf16[3,1,8,32,128]{4,2,3,0,1:T(8,128)(2,1)} %get-tuple-element.17), channel_id=1, source_target_pairs={{8,0},{16,8},{24,16},{9,1},{17,9},{25,17},{10,2},{18,10},{26,18},{... | collective-permute-start | bytes 589832 | tf_op jit(solution)/shard_map/ppermute | solution.py:17
  150.8 9.3 %collective-permute-start.10 = (bf16[3,10,1,32,128]{4,2,3,0,1:T(2,128)(2,1)S(1)}, bf16[3,10,1,32,128]{4,2,3,0,1:T(2,128)(2,1)S(1)}, u32[]{:S(2)}, u32[]{:S(2)}) collective-permute-start(bf16[3,10,1,32,128]{4,2,3,0,1:T(2,128)(2,1)S(1)} %get-tuple-element.14), channel_id=1, source_target_pairs={{0,2},{2,4},{4,6},{1,3},{3,5},{5,7},{8,10},{10,12},{12,14},{9,11},... | collective-permute-start | bytes 737288 | tf_op jit(solution)/shard_map/ppermute | solution.py:15
  152.2 19.1 %collective-permute-start.11 = (bf16[3,10,1,32,128]{4,2,3,0,1:T(2,128)(2,1)S(1)}, bf16[3,10,1,32,128]{4,2,3,0,1:T(2,128)(2,1)S(1)}, u32[]{:S(2)}, u32[]{:S(2)}) collective-permute-start(bf16[3,10,1,32,128]{4,2,3,0,1:T(2,128)(2,1)S(1)} %get-tuple-element.15), channel_id=1, source_target_pairs={{2,0},{4,2},{6,4},{3,1},{5,3},{7,5},{10,8},{12,10},{14,12},{11,9},... | collective-permute-start | bytes 737288 | tf_op jit(solution)/shard_map/ppermute | solution.py:17
  154.5 79.2 %collective-permute-start.22 = (f32[1792,128]{1,0:T(8,128)}, f32[1792,128]{1,0:T(8,128)}, u32[]{:S(2)}, u32[]{:S(2)}) collective-permute-start(f32[1792,128]{1,0:T(8,128)} %constant_dynamic-slice_fusion.4), channel_id=1, source_target_pairs={{0,1},{1,0},{2,3},{3,2},{4,5},{5,4},{6,7},{7,6},{8,9},{9,8},{10,11... | collective-permute-start | bytes 2752520 | tf_op jit(solution)/shard_map/ppermute | solution.py:78
  233.7 15.7 %collective-permute-start.12 = (f32[1792,128]{1,0:T(8,128)}, f32[1792,128]{1,0:T(8,128)}, u32[]{:S(2)}, u32[]{:S(2)}) collective-permute-start(f32[1792,128]{1,0:T(8,128)} %constant_dynamic-slice_fusion.9), channel_id=1, source_target_pairs={{0,1},{1,0},{2,3},{3,2},{4,5},{5,4},{6,7},{7,6},{8,9},{9,8},{10,11... | collective-permute-start | bytes 2752520 | tf_op jit(solution)/shard_map/ppermute | solution.py:78
  235.8 12.4 %collective-permute-start.23 = (f32[896,128]{1,0:T(8,128)S(1)}, f32[896,128]{1,0:T(8,128)}, u32[]{:S(2)}, u32[]{:S(2)}) collective-permute-start(f32[896,128]{1,0:T(8,128)S(1)} %constant_dynamic-slice_fusion.3), channel_id=1, source_target_pairs={{0,2},{2,0},{4,6},{6,4},{1,3},{3,1},{5,7},{7,5},{8,10},{10,8},{12,... | collective-permute-start | bytes 1376264 | tf_op jit(solution)/shard_map/ppermute | solution.py:78
  249.3 6.5 %collective-permute-start.24 = (f32[448,128]{1,0:T(8,128)S(1)}, f32[448,128]{1,0:T(8,128)S(1)}, u32[]{:S(2)}, u32[]{:S(2)}) collective-permute-start(f32[448,128]{1,0:T(8,128)S(1)} %constant_dynamic-slice_fusion.2), channel_id=1, source_target_pairs={{0,4},{2,6},{4,0},{6,2},{1,5},{3,7},{5,1},{7,3},{8,12},{10,14},{12... | collective-permute-start | bytes 688136 | tf_op jit(solution)/shard_map/ppermute | solution.py:78
  255.8 5.2 %collective-permute-start.25 = (f32[224,128]{1,0:T(8,128)S(1)}, f32[224,128]{1,0:T(8,128)S(1)}, u32[]{:S(2)}, u32[]{:S(2)}) collective-permute-start(f32[224,128]{1,0:T(8,128)S(1)} %constant_dynamic-slice_fusion.1), channel_id=1, source_target_pairs={{0,8},{8,0},{16,24},{24,16},{1,9},{9,1},{17,25},{25,17},{2,10},{10... | collective-permute-start | bytes 344072 | tf_op jit(solution)/shard_map/ppermute | solution.py:78
  258.3 10.8 %collective-permute-start.13 = (f32[896,128]{1,0:T(8,128)S(1)}, f32[896,128]{1,0:T(8,128)S(1)}, u32[]{:S(2)}, u32[]{:S(2)}) collective-permute-start(f32[896,128]{1,0:T(8,128)S(1)} %constant_dynamic-slice_fusion.8), channel_id=1, source_target_pairs={{0,2},{2,0},{4,6},{6,4},{1,3},{3,1},{5,7},{7,5},{8,10},{10,8},{12,... | collective-permute-start | bytes 1376264 | tf_op jit(solution)/shard_map/ppermute | solution.py:78
  261.1 5.4 %collective-permute-start.26 = (f32[112,128]{1,0:T(8,128)S(1)}, f32[112,128]{1,0:T(8,128)S(1)}, u32[]{:S(2)}, u32[]{:S(2)}) collective-permute-start(f32[112,128]{1,0:T(8,128)S(1)} %constant_dynamic-slice_fusion), channel_id=1, source_target_pairs={{0,16},{8,24},{16,0},{24,8},{1,17},{9,25},{17,1},{25,9},{2,18},{10... | collective-permute-start | bytes 172040 | tf_op jit(solution)/shard_map/ppermute | solution.py:78
  266.5 4.8 %collective-permute-start.27 = (bf16[112,128]{1,0:T(8,128)(2,1)S(1)}, bf16[112,128]{1,0:T(8,128)(2,1)S(1)}, u32[]{:S(2)}, u32[]{:S(2)}) collective-permute-start(bf16[112,128]{1,0:T(8,128)(2,1)S(1)} %add_convert_fusion), channel_id=1, source_target_pairs={{0,16},{8,24},{16,0},{24,8},{1,17},{9,25},{17,1},{25,9},{2,18},{10... | collective-permute-start | bytes 86024 | tf_op jit(solution)/shard_map/ppermute | solution.py:83
  269.2 6.1 %collective-permute-start.14 = (f32[448,128]{1,0:T(8,128)S(1)}, f32[448,128]{1,0:T(8,128)S(1)}, u32[]{:S(2)}, u32[]{:S(2)}) collective-permute-start(f32[448,128]{1,0:T(8,128)S(1)} %constant_dynamic-slice_fusion.7), channel_id=1, source_target_pairs={{0,4},{2,6},{4,0},{6,2},{1,5},{3,7},{5,1},{7,3},{8,12},{10,14},{12... | collective-permute-start | bytes 688136 | tf_op jit(solution)/shard_map/ppermute | solution.py:78
  271.4 5.7 %collective-permute-start.28 = (bf16[224,128]{1,0:T(8,128)(2,1)S(1)}, bf16[224,128]{1,0:T(8,128)(2,1)S(1)}, u32[]{:S(2)}, u32[]{:S(2)}) collective-permute-start(bf16[224,128]{1,0:T(8,128)(2,1)S(1)} %pad_maximum_fusion.17), channel_id=1, source_target_pairs={{0,8},{8,0},{16,24},{24,16},{1,9},{9,1},{17,25},{25,17},{2,10},{10... | collective-permute-start | bytes 172040 | tf_op jit(solution)/shard_map/ppermute | solution.py:83
  275.3 5.1 %collective-permute-start.15 = (f32[224,128]{1,0:T(8,128)S(1)}, f32[224,128]{1,0:T(8,128)S(1)}, u32[]{:S(2)}, u32[]{:S(2)}) collective-permute-start(f32[224,128]{1,0:T(8,128)S(1)} %constant_dynamic-slice_fusion.6), channel_id=1, source_target_pairs={{0,8},{8,0},{16,24},{24,16},{1,9},{9,1},{17,25},{25,17},{2,10},{10... | collective-permute-start | bytes 344072 | tf_op jit(solution)/shard_map/ppermute | solution.py:78
  280.5 5.2 %collective-permute-start.16 = (f32[112,128]{1,0:T(8,128)S(1)}, f32[112,128]{1,0:T(8,128)S(1)}, u32[]{:S(2)}, u32[]{:S(2)}) collective-permute-start(f32[112,128]{1,0:T(8,128)S(1)} %constant_dynamic-slice_fusion.5), channel_id=1, source_target_pairs={{0,16},{8,24},{16,0},{24,8},{1,17},{9,25},{17,1},{25,9},{2,18},{10... | collective-permute-start | bytes 172040 | tf_op jit(solution)/shard_map/ppermute | solution.py:78
  281.0 5.2 %collective-permute-start.29 = (bf16[448,128]{1,0:T(8,128)(2,1)S(1)}, bf16[448,128]{1,0:T(8,128)(2,1)S(1)}, u32[]{:S(2)}, u32[]{:S(2)}) collective-permute-start(bf16[448,128]{1,0:T(8,128)(2,1)S(1)} %pad_maximum_fusion.15), channel_id=1, source_target_pairs={{0,4},{2,6},{4,0},{6,2},{1,5},{3,7},{5,1},{7,3},{8,12},{10,14},{12... | collective-permute-start | bytes 344072 | tf_op jit(solution)/shard_map/ppermute | solution.py:83
  285.7 4.8 %collective-permute-start.17 = (bf16[112,128]{1,0:T(8,128)(2,1)S(1)}, bf16[112,128]{1,0:T(8,128)(2,1)S(1)}, u32[]{:S(2)}, u32[]{:S(2)}) collective-permute-start(bf16[112,128]{1,0:T(8,128)(2,1)S(1)} %add_convert_fusion.1), channel_id=1, source_target_pairs={{0,16},{8,24},{16,0},{24,8},{1,17},{9,25},{17,1},{25,9},{2,18},{10... | collective-permute-start | bytes 86024 | tf_op jit(solution)/shard_map/ppermute | solution.py:83
  290.5 4.2 %collective-permute-start.18 = (bf16[224,128]{1,0:T(8,128)(2,1)S(1)}, bf16[224,128]{1,0:T(8,128)(2,1)S(1)}, u32[]{:S(2)}, u32[]{:S(2)}) collective-permute-start(bf16[224,128]{1,0:T(8,128)(2,1)S(1)} %pad_maximum_fusion.16), channel_id=1, source_target_pairs={{0,8},{8,0},{16,24},{24,16},{1,9},{9,1},{17,25},{25,17},{2,10},{10... | collective-permute-start | bytes 172040 | tf_op jit(solution)/shard_map/ppermute | solution.py:83
  292.6 6.1 %collective-permute-start.30 = (bf16[896,128]{1,0:T(8,128)(2,1)S(1)}, bf16[896,128]{1,0:T(8,128)(2,1)S(1)}, u32[]{:S(2)}, u32[]{:S(2)}) collective-permute-start(bf16[896,128]{1,0:T(8,128)(2,1)S(1)} %pad_maximum_fusion.13), channel_id=1, source_target_pairs={{0,2},{2,0},{4,6},{6,4},{1,3},{3,1},{5,7},{7,5},{8,10},{10,8},{12,... | collective-permute-start | bytes 688136 | tf_op jit(solution)/shard_map/ppermute | solution.py:83
  294.8 4.9 %collective-permute-start.19 = (bf16[448,128]{1,0:T(8,128)(2,1)S(1)}, bf16[448,128]{1,0:T(8,128)(2,1)S(1)}, u32[]{:S(2)}, u32[]{:S(2)}) collective-permute-start(bf16[448,128]{1,0:T(8,128)(2,1)S(1)} %pad_maximum_fusion.14), channel_id=1, source_target_pairs={{0,4},{2,6},{4,0},{6,2},{1,5},{3,7},{5,1},{7,3},{8,12},{10,14},{12... | collective-permute-start | bytes 344072 | tf_op jit(solution)/shard_map/ppermute | solution.py:83
  299.8 6.1 %collective-permute-start.20 = (bf16[896,128]{1,0:T(8,128)(2,1)S(1)}, bf16[896,128]{1,0:T(8,128)(2,1)S(1)}, u32[]{:S(2)}, u32[]{:S(2)}) collective-permute-start(bf16[896,128]{1,0:T(8,128)(2,1)S(1)} %pad_maximum_fusion.12), channel_id=1, source_target_pairs={{0,2},{2,0},{4,6},{6,4},{1,3},{3,1},{5,7},{7,5},{8,10},{10,8},{12,... | collective-permute-start | bytes 688136 | tf_op jit(solution)/shard_map/ppermute | solution.py:83
  301.5 4.6 %collective-permute-start.31 = (bf16[1792,128]{1,0:T(8,128)(2,1)S(1)}, bf16[1792,128]{1,0:T(8,128)(2,1)S(1)}, u32[]{:S(2)}, u32[]{:S(2)}) collective-permute-start(bf16[1792,128]{1,0:T(8,128)(2,1)S(1)} %pad_maximum_fusion.8), channel_id=1, source_target_pairs={{0,1},{1,0},{2,3},{3,2},{4,5},{5,4},{6,7},{7,6},{8,9},{9,8},{10,11... | collective-permute-start | bytes 1376264 | tf_op jit(solution)/shard_map/ppermute | solution.py:83
  306.0 1.9 collective-permute-start.21
  (17 other events, 150.3 us)

commit v6 on v5

--- a/solution.py
+++ b/solution.py
@@ -103,11 +103,12 @@
     act_two = conv_block(rim_hidden, weight_two)
     features = jax.nn.silu(act_two).astype(jnp.bfloat16)
     delta_two = (cotangent.astype(jnp.float32) * swish_slope(act_two)).astype(jnp.bfloat16)
-    grad_two = weight_grad(rim_hidden, delta_two)
+    local_two = kernel_grad(rim_hidden, delta_two)
     rim_delta = extended(delta_two, (("gx", 1), ("gy", 2)), 1)
     back_grad = conv_block(rim_delta, flipped)
     delta_one = (back_grad * swish_slope(act_one)).astype(jnp.bfloat16)
-    grad_one = weight_grad(rim_input, delta_one)
+    local_one = kernel_grad(rim_input, delta_one)
+    grad_one, grad_two = tree_sum(jnp.stack([local_one, local_two]), ("dp", "gy", "gx"))
     return (features, grad_one.reshape(27, depth, depth), grad_two.reshape(27, depth, depth))
 
 

time: 313 us -> 314 us (level)
  waiting for transfers between devices: 95.5 us -> 83.1 us
  starting transfers between devices: 49.4 us -> 59.4 us
  local copies, waits for them, and re-layouts: 29.8 us -> 33.2 us
    ppermute x6, waiting for transfers between devices: 33.1 us -> 15.9 us  [extended(): lax.ppermute(head, axis, [((i + 1) % count, i) for i in range(ends)])]
    ppermute x10 -> x5, waiting for transfers between devices: 28.1 us -> 41.6 us  [tree_sum(): rows = keep + lax.ppermute(send, axis, pairs)]
    ppermute x6, waiting for transfers between devices: 18.3 us -> 6.81 us  [extended(): lax.ppermute(tail, axis, [(i, (i + 1) % count) for i in range(ends)])]
    ppermute x6, starting transfers between devices: 21.9 us -> 32.7 us  [extended(): lax.ppermute(tail, axis, [(i, (i + 1) % count) for i in range(ends)])]
    unnamed x40 -> x52, local copies, waits for them, and re-layouts: 10.7 us -> 14.7 us
    ppermute x10 -> x5, starting transfers between devices: 11 us -> 7.38 us  [tree_sum(): other = lax.ppermute(rows, axis, pairs)]
    ppermute x10 -> x5, starting transfers between devices: 8.38 us -> 11.6 us  [tree_sum(): rows = keep + lax.ppermute(send, axis, pairs)]
    ppermute x10 -> x5, waiting for transfers between devices: 16 us -> 18.8 us  [tree_sum(): other = lax.ppermute(rows, axis, pairs)]
  transfers between devices with their start and end apart: 32 -> 22, of which waited for: 24 -> 17; matrix products, arithmetic and copies ran while one was open for 32% -> 11% of each run, Pallas kernels for 0% -> 0%
where the time goes in v6:
time: 314 us; the launch traced here: 311 us
  matrix products  107 us (34%)
  waiting for transfers between devices  83.1 us (26%)
  starting transfers between devices  59.4 us (19%)
  local copies, waits for them, and re-layouts  33.2 us (11%)
  other arithmetic  26.6 us (8%)
    conv_general_dilated x2, matrix products, kernel_grad(): lax.conv_general_dilated(padded, delta_field, (1, 1, 1), ((0, 0), (0, 0),...  53.7 us
    conv_general_dilated x3, matrix products, conv_block(): lax.conv_general_dilated(padded, cube_kernel, (1, 1, 1), ((0, 0), (0, 0),...  53.1 us
    ppermute x5, waiting for transfers between devices, tree_sum(): rows = keep + lax.ppermute(send, axis, pairs)  41.6 us
    ppermute x6, starting transfers between devices, extended(): lax.ppermute(tail, axis, [(i, (i + 1) % count) for i in range(ends)])  32.7 us
    ppermute x5, waiting for transfers between devices, tree_sum(): other = lax.ppermute(rows, axis, pairs)  18.8 us
    ppermute x6, waiting for transfers between devices, extended(): lax.ppermute(head, axis, [((i + 1) % count, i) for i in range(ends)])  15.9 us
    unnamed x52, local copies, waits for them, and re-layouts  14.7 us
    ppermute x5, starting transfers between devices, tree_sum(): rows = keep + lax.ppermute(send, axis, pairs)  11.6 us
  transfers between devices with their start and end apart: 22, of which 17 were waited for; matrix products, arithmetic and copies ran while one was open for 11% of the time, Pallas kernels for 0%

profile of v6, /device:TPU:0, one launch (start us, length us, event | category | flops | bytes accessed | tf_op | source)
XLA Modules:
  0.0 310.6 jit_solution(3675319621742035418)
XLA Ops:
  2.0 4.9 %collective-permute-start = (bf16[3,1,8,32,128]{4,0,3,2,1:T(4,128)(2,1)S(1)}, bf16[3,1,8,32,128]{4,0,3,2,1:T(4,128)(2,1)S(1)}, u32[]{:S(2)}, u32[]{:S(2)}) collective-permute-start(bf16[3,1,8,32,128]{4,0,3,2,1:T(4,128)(2,1)S(1)} %copy.55), channel_id=1, source_target_pairs={{0,8},{8,16},{16,24},{1,9},{9,17},{17,25},{2,10},{10,18},{18,26},{... | collective-permute-start | bytes 589832 | tf_op jit(solution)/shard_map/ppermute | solution.py:15
  8.4 4.1 %collective-permute-done = bf16[3,1,8,32,128]{4,0,3,2,1:T(4,128)(2,1)S(1)} collective-permute-done((bf16[3,1,8,32,128]{4,0,3,2,1:T(4,128)(2,1)S(1)}, bf16[3,1,8,32,128]{4,0,3,2,1:T(4,128)(2,1)S(1)}, u32[]{:S(2)}, u32[]{:S(2)}) %collective-permute-start) | collective-permute-done | bytes 196640 | tf_op jit(solution)/shard_map/ppermute | solution.py:15
  12.5 2.9 constant_dynamic-update-slice_fusion.1
  18.5 4.7 %collective-permute-start.2 = (bf16[3,10,1,32,128]{4,0,3,2,1:T(4,128)(2,1)S(1)}, bf16[3,10,1,32,128]{4,0,3,2,1:T(4,128)(2,1)S(1)}, u32[]{:S(2)}, u32[]{:S(2)}) collective-permute-start(bf16[3,10,1,32,128]{4,0,3,2,1:T(4,128)(2,1)S(1)} %get-tuple-element.12), channel_id=1, source_target_pairs={{0,2},{2,4},{4,6},{1,3},{3,5},{5,7},{8,10},{10,12},{12,14},{9,11},... | collective-permute-start | bytes 737288 | tf_op jit(solution)/shard_map/ppermute | solution.py:15
  23.2 6.5 %collective-permute-done.3 = bf16[3,10,1,32,128]{4,0,3,2,1:T(4,128)(2,1)S(1)} collective-permute-done((bf16[3,10,1,32,128]{4,0,3,2,1:T(4,128)(2,1)S(1)}, bf16[3,10,1,32,128]{4,0,3,2,1:T(4,128)(2,1)S(1)}, u32[]{:S(2)}, u32[]{:S(2)}) %collective-permute-start.3) | collective-permute-done | bytes 245792 | tf_op jit(solution)/shard_map/ppermute | solution.py:17
  36.4 15.5 %broadcast_select_fusion.1 = f32[8,8,24,5,128]{4,2,3,1,0:T(8,128)S(1)} fusion(pred[24,5]{0,1:T(8,128)(4,1)S(1)} %copy-done.21, bf16[3,3,3,128,128]{4,3,2,1,0:T(8,128)(2,1)S(1)} %bitcast.60, bf16[10,10,3,7,2,128]{5,3,2,4,1,0:T(8,128)(2,1)S(1)} %slice.61, bf16[10,10,3,8,5,128]{5,3,2,4,1,0:T(8,128)(2,1)S(1)} %copy.21), kind=kOutput, calls=%fused_computation.43 | convolution fusion | flops 6808657920 | bytes 8964216 | tf_op jit(solution)/shard_map/conv_general_dilated | solution.py:27
  59.3 4.6 %collective-permute-start.4 = (bf16[3,1,8,32,128]{4,0,3,2,1:T(4,128)(2,1)S(1)}, bf16[3,1,8,32,128]{4,0,3,2,1:T(4,128)(2,1)S(1)}, u32[]{:S(2)}, u32[]{:S(2)}) collective-permute-start(bf16[3,1,8,32,128]{4,0,3,2,1:T(4,128)(2,1)S(1)} %get-tuple-element.14), channel_id=1, source_target_pairs={{0,8},{8,16},{16,24},{1,9},{9,17},{17,25},{2,10},{10,18},{18,26},{... | collective-permute-start | bytes 589832 | tf_op jit(solution)/shard_map/ppermute | solution.py:15
  69.5 6.0 %collective-permute-start.6 = (bf16[3,10,1,32,128]{4,0,3,2,1:T(4,128)(2,1)S(1)}, bf16[3,10,1,32,128]{4,0,3,2,1:T(4,128)(2,1)S(1)}, u32[]{:S(2)}, u32[]{:S(2)}) collective-permute-start(bf16[3,10,1,32,128]{4,0,3,2,1:T(4,128)(2,1)S(1)} %get-tuple-element.10), channel_id=1, source_target_pairs={{0,2},{2,4},{4,6},{1,3},{3,5},{5,7},{8,10},{10,12},{12,14},{9,11},... | collective-permute-start | bytes 737288 | tf_op jit(solution)/shard_map/ppermute | solution.py:15
  75.6 5.7 %collective-permute-done.7 = bf16[3,10,1,32,128]{4,0,3,2,1:T(4,128)(2,1)S(1)} collective-permute-done((bf16[3,10,1,32,128]{4,0,3,2,1:T(4,128)(2,1)S(1)}, bf16[3,10,1,32,128]{4,0,3,2,1:T(4,128)(2,1)S(1)}, u32[]{:S(2)}, u32[]{:S(2)}) %collective-permute-start.7) | collective-permute-done | bytes 245792 | tf_op jit(solution)/shard_map/ppermute | solution.py:17
  81.3 3.1 %fusion.52 = bf16[10,10,3,32,128]{4,2,3,1,0:T(4,128)(2,1)S(1)} fusion(bf16[3,10,1,32,128]{4,0,3,2,1:T(4,128)(2,1)S(1)} %collective-permute-done.7, bf16[3,1,8,32,128]{4,0,3,2,1:T(4,128)(2,1)S(1)} %collective-permute-done.5, bf16[3,8,8,32,128]{4,0,3,2,1:T(4,128)(2,1)S(1)} %multiply_convert_fusion, bf16[3,1,8,32,128]{4,0,3,2,1:T(4,128)(2,1)S(1)} %collective-permute-done.4, ...), kind=kLoop, calls=%fused_computation.92 | loop fusion | flops 4915200 | bytes 4915200 | tf_op jit(solution)/shard_map/concatenate | solution.py:13
  87.3 17.1 %add_multiply_fusion = (f32[8,8,24,5,128]{4,2,3,1,0:T(8,128)S(1)}, bf16[8,8,24,5,128]{4,2,3,1,0:T(8,128)(2,1)}) fusion(pred[24,5]{0,1:T(8,128)(4,1)S(1)} %copy-done.21, bf16[3,3,3,128,128]{4,3,2,1,0:T(8,128)(2,1)S(1)} %bitcast.76, bf16[10,10,3,7,2,128]{5,3,2,4,1,0:T(8,128)(2,1)S(1)} %slice.65, bf16[10,10,3,8,5,128]{5,3,2,4,1,0:T(8,128)(2,1)S(1)} %copy.25), kind=kOutput, calls=%fused_computation.28 | convolution fusion | flops 6817505280 | bytes 10930296 | tf_op jit(solution)/shard_map/conv_general_dilated | solution.py:27
  110.1 5.0 %collective-permute-start.8 = (bf16[3,1,8,32,128]{4,2,3,0,1:T(8,128)(2,1)}, bf16[3,1,8,32,128]{4,2,3,0,1:T(8,128)(2,1)S(1)}, u32[]{:S(2)}, u32[]{:S(2)}) collective-permute-start(bf16[3,1,8,32,128]{4,2,3,0,1:T(8,128)(2,1)} %get-tuple-element.20), channel_id=1, source_target_pairs={{0,8},{8,16},{16,24},{1,9},{9,17},{17,25},{2,10},{10,18},{18,26},{... | collective-permute-start | bytes 589832 | tf_op jit(solution)/shard_map/ppermute | solution.py:15
  118.6 3.2 %pad_maximum_fusion.6 = (bf16[3,10,1,32,128]{4,2,3,0,1:T(2,128)(2,1)}, bf16[3,10,1,32,128]{4,2,3,0,1:T(2,128)(2,1)}) fusion(bf16[3,1,8,32,128]{4,2,3,0,1:T(8,128)(2,1)S(1)} %collective-permute-done.9, bf16[3,8,8,32,128]{4,2,3,0,1:T(8,128)(2,1)} %copy-done.4, bf16[3,1,8,32,128]{4,2,3,0,1:T(8,128)(2,1)S(1)} %collective-permute-done.8), kind=kLoop, calls=%fused_computation.53 | loop fusion | flops 1474560 | bytes 2457600 | tf_op jit(solution)/shard_map/slice | solution.py:12
  123.0 7.4 %collective-permute-start.10 = (bf16[3,10,1,32,128]{4,2,3,0,1:T(2,128)(2,1)}, bf16[3,10,1,32,128]{4,2,3,0,1:T(2,128)(2,1)}, u32[]{:S(2)}, u32[]{:S(2)}) collective-permute-start(bf16[3,10,1,32,128]{4,2,3,0,1:T(2,128)(2,1)} %get-tuple-element.16), channel_id=1, source_target_pairs={{0,2},{2,4},{4,6},{1,3},{3,5},{5,7},{8,10},{10,12},{12,14},{9,11},... | collective-permute-start | bytes 737288 | tf_op jit(solution)/shard_map/ppermute | solution.py:15
  130.5 26.3 %fusion.27 = f32[3,3,3,128,128]{4,3,2,1,0:T(8,128)} fusion(bf16[3,8,8,32,128]{4,2,3,0,1:T(8,128)(2,1)} %copy-done.4, bf16[3,10,1,32,128]{4,0,3,2,1:T(4,128)(2,1)S(1)} %collective-permute-done.7, bf16[3,1,8,32,128]{4,0,3,2,1:T(4,128)(2,1)S(1)} %collective-permute-done.5, bf16[3,8,8,32,128]{4,0,3,2,1:T(4,128)(2,1)S(1)} %multiply_convert_fusion, ...), kind=kOutput, calls=%fused_computation.39 | convolution fusion | flops 5334859776 | bytes 5799936 | tf_op jit(solution)/shard_map/conv_general_dilated | solution.py:39
  156.8 4.0 %maximum_bitcast_fusion = bf16[10,10,3,32,128]{4,1,3,2,0:T(8,128)(2,1)S(1)} fusion(bf16[3,10,1,32,128]{4,2,3,0,1:T(2,128)(2,1)} %collective-permute-done.11, bf16[3,1,8,32,128]{4,2,3,0,1:T(8,128)(2,1)} %copy-done.14, bf16[3,8,8,32,128]{4,2,3,0,1:T(8,128)(2,1)S(1)} %copy-done.5, bf16[3,1,8,32,128]{4,2,3,0,1:T(8,128)(2,1)} %copy-done.15, ...), kind=kLoop, calls=%fused_computation.27 | loop fusion | flops 12288000 | bytes 4915200 | tf_op jit(solution)/shard_map/concatenate | solution.py:13
  164.2 2.8 fusion.3
  167.1 20.5 %broadcast_select_fusion = f32[8,8,24,5,128]{4,2,3,1,0:T(8,128)S(1)} fusion(pred[24,5]{0,1:T(8,128)(4,1)S(1)} %copy-done.22, bf16[3,3,3,128,128]{3,4,2,1,0:T(8,128)(2,1)S(1)} %bitcast.77, bf16[10,10,3,8,7,128]{5,4,3,2,1,0:T(8,128)(2,1)S(1)} %fusion.3), kind=kOutput, calls=%fused_computation.42 | convolution fusion | flops 6795755520 | bytes 9117816 | tf_op jit(solution)/shard_map/conv_general_dilated | solution.py:27
  190.7 27.4 %fusion.29 = f32[3,3,3,128,128]{4,3,2,1,0:T(8,128)S(1)} fusion(f32[8,8,3,32,128]{4,1,3,2,0:T(8,128)S(1)} %slice.71, f32[3,8,8,32,128]{4,0,3,2,1:T(4,128)S(1)} %bitcast.63, bf16[3,10,1,32,128]{4,0,3,2,1:T(4,128)(2,1)S(1)} %copy-done.17, bf16[3,10,8,32,128]{4,0,3,2,1:T(4,128)(2,1)S(1)} %copy-done.8, bf16[3,10,1,32,128]{4,0,3,2,1:T(4,128)(2,1)S(1)} %copy-done.19), kind=kOutput, calls=%fused_computation.41 | convolution fusion | flops 5337022464 | bytes 10518528 | tf_op jit(solution)/shard_map/conv_general_dilated | solution.py:39
  220.4 3.8 %collective-permute-done.12 = f32[3456,128]{1,0:T(8,128)} collective-permute-done((f32[3456,128]{1,0:T(8,128)S(1)}, f32[3456,128]{1,0:T(8,128)}, u32[]{:S(2)}, u32[]{:S(2)}) %collective-permute-start.12) | collective-permute-done | bytes 1769504 | tf_op jit(solution)/shard_map/ppermute | solution.py:78
  226.5 2.7 collective-permute-start.13
  229.1 19.9 %collective-permute-done.13 = f32[1728,128]{1,0:T(8,128)S(1)} collective-permute-done((f32[1728,128]{1,0:T(8,128)S(1)}, f32[1728,128]{1,0:T(8,128)S(1)}, u32[]{:S(2)}, u32[]{:S(2)}) %collective-permute-start.13) | collective-permute-done | bytes 884768 | tf_op jit(solution)/shard_map/ppermute | solution.py:78
  249.2 3.1 %collective-permute-start.14 = (f32[864,128]{1,0:T(8,128)S(1)}, f32[864,128]{1,0:T(8,128)S(1)}, u32[]{:S(2)}, u32[]{:S(2)}) collective-permute-start(f32[864,128]{1,0:T(8,128)S(1)} %constant_dynamic-slice_fusion.2), channel_id=1, source_target_pairs={{0,4},{2,6},{4,0},{6,2},{1,5},{3,7},{5,1},{7,3},{8,12},{10,14},{12... | collective-permute-start | bytes 1327112 | tf_op jit(solution)/shard_map/ppermute | solution.py:78
  252.4 9.6 %collective-permute-done.14 = f32[864,128]{1,0:T(8,128)S(1)} collective-permute-done((f32[864,128]{1,0:T(8,128)S(1)}, f32[864,128]{1,0:T(8,128)S(1)}, u32[]{:S(2)}, u32[]{:S(2)}) %collective-permute-start.14) | collective-permute-done | bytes 442400 | tf_op jit(solution)/shard_map/ppermute | solution.py:78
  264.5 4.3 %collective-permute-done.15 = f32[432,128]{1,0:T(8,128)S(1)} collective-permute-done((f32[432,128]{1,0:T(8,128)S(1)}, f32[432,128]{1,0:T(8,128)S(1)}, u32[]{:S(2)}, u32[]{:S(2)}) %collective-permute-start.15) | collective-permute-done | bytes 221216 | tf_op jit(solution)/shard_map/ppermute | solution.py:78
  268.9 3.3 %collective-permute-start.16 = (f32[216,128]{1,0:T(8,128)S(1)}, f32[216,128]{1,0:T(8,128)S(1)}, u32[]{:S(2)}, u32[]{:S(2)}) collective-permute-start(f32[216,128]{1,0:T(8,128)S(1)} %constant_dynamic-slice_fusion), channel_id=1, source_target_pairs={{0,16},{8,24},{16,0},{24,8},{1,17},{9,25},{17,1},{25,9},{2,18},{10... | collective-permute-start | bytes 331784 | tf_op jit(solution)/shard_map/ppermute | solution.py:78
  272.1 3.9 %collective-permute-done.16 = f32[216,128]{1,0:T(8,128)S(1)} collective-permute-done((f32[216,128]{1,0:T(8,128)S(1)}, f32[216,128]{1,0:T(8,128)S(1)}, u32[]{:S(2)}, u32[]{:S(2)}) %collective-permute-start.16) | collective-permute-done | bytes 110624 | tf_op jit(solution)/shard_map/ppermute | solution.py:78
  278.0 3.3 %collective-permute-done.17 = bf16[216,128]{1,0:T(8,128)(2,1)S(1)} collective-permute-done((bf16[216,128]{1,0:T(8,128)(2,1)S(1)}, bf16[216,128]{1,0:T(8,128)(2,1)S(1)}, u32[]{:S(2)}, u32[]{:S(2)}) %collective-permute-start.17) | collective-permute-done | bytes 55328 | tf_op jit(solution)/shard_map/ppermute | solution.py:83
  281.3 2.9 collective-permute-start.18
  284.2 2.7 collective-permute-done.18
  288.8 4.2 %collective-permute-done.19 = bf16[864,128]{1,0:T(8,128)(2,1)S(1)} collective-permute-done((bf16[864,128]{1,0:T(8,128)(2,1)S(1)}, bf16[864,128]{1,0:T(8,128)(2,1)S(1)}, u32[]{:S(2)}, u32[]{:S(2)}) %collective-permute-start.19) | collective-permute-done | bytes 221216 | tf_op jit(solution)/shard_map/ppermute | solution.py:83
  294.0 7.6 %collective-permute-done.20 = bf16[1728,128]{1,0:T(8,128)(2,1)} collective-permute-done((bf16[1728,128]{1,0:T(8,128)(2,1)S(1)}, bf16[1728,128]{1,0:T(8,128)(2,1)}, u32[]{:S(2)}, u32[]{:S(2)}) %collective-permute-start.20) | collective-permute-done | bytes 442400 | tf_op jit(solution)/shard_map/ppermute | solution.py:83
  (121 shorter events, 65.9 us)
Async XLA Ops:
  0.6 35.8 %copy-start = (bf16[27,128,128]{2,1,0:T(8,128)(2,1)S(1)}, bf16[27,128,128]{2,1,0:T(8,128)(2,1)}, u32[]{:S(2)}) copy-start(bf16[27,128,128]{2,1,0:T(8,128)(2,1)} %param.5) | copy-start | bytes 2654212
  2.0 10.5 %collective-permute-start = (bf16[3,1,8,32,128]{4,0,3,2,1:T(4,128)(2,1)S(1)}, bf16[3,1,8,32,128]{4,0,3,2,1:T(4,128)(2,1)S(1)}, u32[]{:S(2)}, u32[]{:S(2)}) collective-permute-start(bf16[3,1,8,32,128]{4,0,3,2,1:T(4,128)(2,1)S(1)} %copy.55), channel_id=1, source_target_pairs={{0,8},{8,16},{16,24},{1,9},{9,17},{17,25},{2,10},{10,18},{18,26},{... | collective-permute-start | bytes 589832 | tf_op jit(solution)/shard_map/ppermute | solution.py:15
  7.1 9.7 %collective-permute-start.1 = (bf16[3,1,8,32,128]{4,0,3,2,1:T(4,128)(2,1)S(1)}, bf16[3,1,8,32,128]{4,0,3,2,1:T(4,128)(2,1)S(1)}, u32[]{:S(2)}, u32[]{:S(2)}) collective-permute-start(bf16[3,1,8,32,128]{4,0,3,2,1:T(4,128)(2,1)S(1)} %copy.56), channel_id=1, source_target_pairs={{8,0},{16,8},{24,16},{9,1},{17,9},{25,17},{10,2},{18,10},{26,18},{... | collective-permute-start | bytes 589832 | tf_op jit(solution)/shard_map/ppermute | solution.py:17
  16.9 12.8 %copy-start.7 = (bf16[3,10,8,32,128]{4,0,3,2,1:T(4,128)(2,1)}, bf16[3,10,8,32,128]{4,0,3,2,1:T(4,128)(2,1)S(1)}, u32[]{:S(2)}) copy-start(bf16[3,10,8,32,128]{4,0,3,2,1:T(4,128)(2,1)S(1)} %constant_dynamic-update-slice_fusion) | copy-start | bytes 5898244
  17.2 12.5 %collective-permute-start.3 = (bf16[3,10,1,32,128]{4,0,3,2,1:T(4,128)(2,1)S(1)}, bf16[3,10,1,32,128]{4,0,3,2,1:T(4,128)(2,1)S(1)}, u32[]{:S(2)}, u32[]{:S(2)}) collective-permute-start(bf16[3,10,1,32,128]{4,0,3,2,1:T(4,128)(2,1)S(1)} %get-tuple-element.13), channel_id=1, source_target_pairs={{2,0},{4,2},{6,4},{3,1},{5,3},{7,5},{10,8},{12,10},{14,12},{11,9},... | collective-permute-start | bytes 737288 | tf_op jit(solution)/shard_map/ppermute | solution.py:17
  18.5 11.2 %collective-permute-start.2 = (bf16[3,10,1,32,128]{4,0,3,2,1:T(4,128)(2,1)S(1)}, bf16[3,10,1,32,128]{4,0,3,2,1:T(4,128)(2,1)S(1)}, u32[]{:S(2)}, u32[]{:S(2)}) collective-permute-start(bf16[3,10,1,32,128]{4,0,3,2,1:T(4,128)(2,1)S(1)} %get-tuple-element.12), channel_id=1, source_target_pairs={{0,2},{2,4},{4,6},{1,3},{3,5},{5,7},{8,10},{10,12},{12,14},{9,11},... | collective-permute-start | bytes 737288 | tf_op jit(solution)/shard_map/ppermute | solution.py:15
  55.1 2.8 copy-start.2
  58.0 8.3 %collective-permute-start.5 = (bf16[3,1,8,32,128]{4,0,3,2,1:T(4,128)(2,1)S(1)}, bf16[3,1,8,32,128]{4,0,3,2,1:T(4,128)(2,1)S(1)}, u32[]{:S(2)}, u32[]{:S(2)}) collective-permute-start(bf16[3,1,8,32,128]{4,0,3,2,1:T(4,128)(2,1)S(1)} %get-tuple-element.15), channel_id=1, source_target_pairs={{8,0},{16,8},{24,16},{9,1},{17,9},{25,17},{10,2},{18,10},{26,18},{... | collective-permute-start | bytes 589832 | tf_op jit(solution)/shard_map/ppermute | solution.py:17
  59.3 8.4 %collective-permute-start.4 = (bf16[3,1,8,32,128]{4,0,3,2,1:T(4,128)(2,1)S(1)}, bf16[3,1,8,32,128]{4,0,3,2,1:T(4,128)(2,1)S(1)}, u32[]{:S(2)}, u32[]{:S(2)}) collective-permute-start(bf16[3,1,8,32,128]{4,0,3,2,1:T(4,128)(2,1)S(1)} %get-tuple-element.14), channel_id=1, source_target_pairs={{0,8},{8,16},{16,24},{1,9},{9,17},{17,25},{2,10},{10,18},{18,26},{... | collective-permute-start | bytes 589832 | tf_op jit(solution)/shard_map/ppermute | solution.py:15
  68.2 13.0 %collective-permute-start.7 = (bf16[3,10,1,32,128]{4,0,3,2,1:T(4,128)(2,1)S(1)}, bf16[3,10,1,32,128]{4,0,3,2,1:T(4,128)(2,1)S(1)}, u32[]{:S(2)}, u32[]{:S(2)}) collective-permute-start(bf16[3,10,1,32,128]{4,0,3,2,1:T(4,128)(2,1)S(1)} %get-tuple-element.11), channel_id=1, source_target_pairs={{2,0},{4,2},{6,4},{3,1},{5,3},{7,5},{10,8},{12,10},{14,12},{11,9},... | collective-permute-start | bytes 737288 | tf_op jit(solution)/shard_map/ppermute | solution.py:17
  69.5 11.7 %collective-permute-start.6 = (bf16[3,10,1,32,128]{4,0,3,2,1:T(4,128)(2,1)S(1)}, bf16[3,10,1,32,128]{4,0,3,2,1:T(4,128)(2,1)S(1)}, u32[]{:S(2)}, u32[]{:S(2)}) collective-permute-start(bf16[3,10,1,32,128]{4,0,3,2,1:T(4,128)(2,1)S(1)} %get-tuple-element.10), channel_id=1, source_target_pairs={{0,2},{2,4},{4,6},{1,3},{3,5},{5,7},{8,10},{10,12},{12,14},{9,11},... | collective-permute-start | bytes 737288 | tf_op jit(solution)/shard_map/ppermute | solution.py:15
  81.3 4.9 %copy-start.20 = (bf16[3,10,1,32,128]{4,0,3,2,1:T(4,128)(2,1)}, bf16[3,10,1,32,128]{4,0,3,2,1:T(4,128)(2,1)S(1)}, u32[]{:S(2)}) copy-start(bf16[3,10,1,32,128]{4,0,3,2,1:T(4,128)(2,1)S(1)} %collective-permute-done.6) | copy-start | bytes 737284
  108.8 8.5 %collective-permute-start.9 = (bf16[3,1,8,32,128]{4,2,3,0,1:T(8,128)(2,1)}, bf16[3,1,8,32,128]{4,2,3,0,1:T(8,128)(2,1)S(1)}, u32[]{:S(2)}, u32[]{:S(2)}) collective-permute-start(bf16[3,1,8,32,128]{4,2,3,0,1:T(8,128)(2,1)} %get-tuple-element.21), channel_id=1, source_target_pairs={{8,0},{16,8},{24,16},{9,1},{17,9},{25,17},{10,2},{18,10},{26,18},{... | collective-permute-start | bytes 589832 | tf_op jit(solution)/shard_map/ppermute | solution.py:17
  110.1 8.5 %collective-permute-start.8 = (bf16[3,1,8,32,128]{4,2,3,0,1:T(8,128)(2,1)}, bf16[3,1,8,32,128]{4,2,3,0,1:T(8,128)(2,1)S(1)}, u32[]{:S(2)}, u32[]{:S(2)}) collective-permute-start(bf16[3,1,8,32,128]{4,2,3,0,1:T(8,128)(2,1)} %get-tuple-element.20), channel_id=1, source_target_pairs={{0,8},{8,16},{16,24},{1,9},{9,17},{17,25},{2,10},{10,18},{18,26},{... | collective-permute-start | bytes 589832 | tf_op jit(solution)/shard_map/ppermute | solution.py:15
  117.3 39.5 %copy-start.14 = (bf16[3,1,8,32,128]{4,2,3,0,1:T(8,128)(2,1)}, bf16[3,1,8,32,128]{4,2,3,0,1:T(8,128)(2,1)S(1)}, u32[]{:S(2)}) copy-start(bf16[3,1,8,32,128]{4,2,3,0,1:T(8,128)(2,1)S(1)} %collective-permute-done.9) | copy-start | bytes 589828
  118.6 38.2 %copy-start.15 = (bf16[3,1,8,32,128]{4,2,3,0,1:T(8,128)(2,1)}, bf16[3,1,8,32,128]{4,2,3,0,1:T(8,128)(2,1)S(1)}, u32[]{:S(2)}) copy-start(bf16[3,1,8,32,128]{4,2,3,0,1:T(8,128)(2,1)S(1)} %collective-permute-done.8) | copy-start | bytes 589828
  121.8 35.0 %collective-permute-start.11 = (bf16[3,10,1,32,128]{4,2,3,0,1:T(2,128)(2,1)}, bf16[3,10,1,32,128]{4,2,3,0,1:T(2,128)(2,1)}, u32[]{:S(2)}, u32[]{:S(2)}) collective-permute-start(bf16[3,10,1,32,128]{4,2,3,0,1:T(2,128)(2,1)} %get-tuple-element.17), channel_id=1, source_target_pairs={{2,0},{4,2},{6,4},{3,1},{5,3},{7,5},{10,8},{12,10},{14,12},{11,9},... | collective-permute-start | bytes 737288 | tf_op jit(solution)/shard_map/ppermute | solution.py:17
  123.0 33.7 %collective-permute-start.10 = (bf16[3,10,1,32,128]{4,2,3,0,1:T(2,128)(2,1)}, bf16[3,10,1,32,128]{4,2,3,0,1:T(2,128)(2,1)}, u32[]{:S(2)}, u32[]{:S(2)}) collective-permute-start(bf16[3,10,1,32,128]{4,2,3,0,1:T(2,128)(2,1)} %get-tuple-element.16), channel_id=1, source_target_pairs={{0,2},{2,4},{4,6},{1,3},{3,5},{5,7},{8,10},{10,12},{12,14},{9,11},... | collective-permute-start | bytes 737288 | tf_op jit(solution)/shard_map/ppermute | solution.py:15
  130.5 26.3 %copy-start.5 = (bf16[3,8,8,32,128]{4,2,3,0,1:T(8,128)(2,1)S(1)}, bf16[3,8,8,32,128]{4,2,3,0,1:T(8,128)(2,1)}, u32[]{:S(2)}) copy-start(bf16[3,8,8,32,128]{4,2,3,0,1:T(8,128)(2,1)} %copy-done.4) | copy-start | bytes 4718596
  164.2 2.8 copy-start.13
  190.7 27.4 %copy-start.10 = (f32[3,3,3,128,128]{4,3,2,1,0:T(8,128)S(1)}, f32[3,3,3,128,128]{4,3,2,1,0:T(8,128)}, u32[]{:S(2)}) copy-start(f32[3,3,3,128,128]{4,3,2,1,0:T(8,128)} %fusion.27) | copy-start | bytes 5308420
  220.3 3.9 %collective-permute-start.12 = (f32[3456,128]{1,0:T(8,128)S(1)}, f32[3456,128]{1,0:T(8,128)}, u32[]{:S(2)}, u32[]{:S(2)}) collective-permute-start(f32[3456,128]{1,0:T(8,128)S(1)} %constant_dynamic-slice_fusion.4), channel_id=1, source_target_pairs={{0,1},{1,0},{2,3},{3,2},{4,5},{5,4},{6,7},{7,6},{8,9},{9,8},{10,11... | collective-permute-start | bytes 5308424 | tf_op jit(solution)/shard_map/ppermute | solution.py:78
  226.5 22.6 %collective-permute-start.13 = (f32[1728,128]{1,0:T(8,128)S(1)}, f32[1728,128]{1,0:T(8,128)S(1)}, u32[]{:S(2)}, u32[]{:S(2)}) collective-permute-start(f32[1728,128]{1,0:T(8,128)S(1)} %constant_dynamic-slice_fusion.3), channel_id=1, source_target_pairs={{0,2},{2,0},{4,6},{6,4},{1,3},{3,1},{5,7},{7,5},{8,10},{10,8},{12,... | collective-permute-start | bytes 2654216 | tf_op jit(solution)/shard_map/ppermute | solution.py:78
  249.2 12.8 %collective-permute-start.14 = (f32[864,128]{1,0:T(8,128)S(1)}, f32[864,128]{1,0:T(8,128)S(1)}, u32[]{:S(2)}, u32[]{:S(2)}) collective-permute-start(f32[864,128]{1,0:T(8,128)S(1)} %constant_dynamic-slice_fusion.2), channel_id=1, source_target_pairs={{0,4},{2,6},{4,0},{6,2},{1,5},{3,7},{5,1},{7,3},{8,12},{10,14},{12... | collective-permute-start | bytes 1327112 | tf_op jit(solution)/shard_map/ppermute | solution.py:78
  262.1 6.7 %collective-permute-start.15 = (f32[432,128]{1,0:T(8,128)S(1)}, f32[432,128]{1,0:T(8,128)S(1)}, u32[]{:S(2)}, u32[]{:S(2)}) collective-permute-start(f32[432,128]{1,0:T(8,128)S(1)} %constant_dynamic-slice_fusion.1), channel_id=1, source_target_pairs={{0,8},{8,0},{16,24},{24,16},{1,9},{9,1},{17,25},{25,17},{2,10},{10... | collective-permute-start | bytes 663560 | tf_op jit(solution)/shard_map/ppermute | solution.py:78
  268.8 35.0 %copy-start.9 = (bf16[8,8,24,5,128]{4,2,3,1,0:T(8,128)(2,1)S(1)}, bf16[8,8,24,5,128]{4,2,3,1,0:T(8,128)(2,1)}, u32[]{:S(2)}) copy-start(bf16[8,8,24,5,128]{4,2,3,1,0:T(8,128)(2,1)} %get-tuple-element.7) | copy-start | bytes 5898244
  268.9 7.2 %collective-permute-start.16 = (f32[216,128]{1,0:T(8,128)S(1)}, f32[216,128]{1,0:T(8,128)S(1)}, u32[]{:S(2)}, u32[]{:S(2)}) collective-permute-start(f32[216,128]{1,0:T(8,128)S(1)} %constant_dynamic-slice_fusion), channel_id=1, source_target_pairs={{0,16},{8,24},{16,0},{24,8},{1,17},{9,25},{17,1},{25,9},{2,18},{10... | collective-permute-start | bytes 331784 | tf_op jit(solution)/shard_map/ppermute | solution.py:78
  276.1 5.2 %collective-permute-start.17 = (bf16[216,128]{1,0:T(8,128)(2,1)S(1)}, bf16[216,128]{1,0:T(8,128)(2,1)S(1)}, u32[]{:S(2)}, u32[]{:S(2)}) collective-permute-start(bf16[216,128]{1,0:T(8,128)(2,1)S(1)} %add_convert_fusion), channel_id=1, source_target_pairs={{0,16},{8,24},{16,0},{24,8},{1,17},{9,25},{17,1},{25,9},{2,18},{10... | collective-permute-start | bytes 165896 | tf_op jit(solution)/shard_map/ppermute | solution.py:83
  281.3 5.6 %collective-permute-start.18 = (bf16[432,128]{1,0:T(8,128)(2,1)S(1)}, bf16[432,128]{1,0:T(8,128)(2,1)S(1)}, u32[]{:S(2)}, u32[]{:S(2)}) collective-permute-start(bf16[432,128]{1,0:T(8,128)(2,1)S(1)} %pad_maximum_fusion.12), channel_id=1, source_target_pairs={{0,8},{8,0},{16,24},{24,16},{1,9},{9,1},{17,25},{25,17},{2,10},{10... | collective-permute-start | bytes 331784 | tf_op jit(solution)/shard_map/ppermute | solution.py:83
  287.0 6.0 %collective-permute-start.19 = (bf16[864,128]{1,0:T(8,128)(2,1)S(1)}, bf16[864,128]{1,0:T(8,128)(2,1)S(1)}, u32[]{:S(2)}, u32[]{:S(2)}) collective-permute-start(bf16[864,128]{1,0:T(8,128)(2,1)S(1)} %pad_maximum_fusion.11), channel_id=1, source_target_pairs={{0,4},{2,6},{4,0},{6,2},{1,5},{3,7},{5,1},{7,3},{8,12},{10,14},{12... | collective-permute-start | bytes 663560 | tf_op jit(solution)/shard_map/ppermute | solution.py:83
  293.1 8.5 %collective-permute-start.20 = (bf16[1728,128]{1,0:T(8,128)(2,1)S(1)}, bf16[1728,128]{1,0:T(8,128)(2,1)}, u32[]{:S(2)}, u32[]{:S(2)}) collective-permute-start(bf16[1728,128]{1,0:T(8,128)(2,1)S(1)} %pad_maximum_fusion.7), channel_id=1, source_target_pairs={{0,2},{2,0},{4,6},{6,4},{1,3},{3,1},{5,7},{7,5},{8,10},{10,8},{12,... | collective-permute-start | bytes 1327112 | tf_op jit(solution)/shard_map/ppermute | solution.py:83
  303.8 2.8 collective-permute-start.21
  (13 other events, 22.0 us)

commit v7 on v5

--- a/solution.py
+++ b/solution.py
@@ -96,15 +96,15 @@
     layout = volumes.shape
     depth = layout[4]
     flipped = jnp.transpose(weight_two[::-1], (0, 2, 1))
-    rim_input = extended(volumes, (("gx", 1), ("gy", 2)), 1)
+    rim_input = extended(volumes, (("gy", 2), ("gx", 1)), 1)
     act_one = lax.optimization_barrier(conv_block(rim_input, weight_one))
     hidden = jax.nn.silu(act_one).astype(jnp.bfloat16)
-    rim_hidden = extended(hidden, (("gx", 1), ("gy", 2)), 1)
+    rim_hidden = extended(hidden, (("gy", 2), ("gx", 1)), 1)
     act_two = conv_block(rim_hidden, weight_two)
     features = jax.nn.silu(act_two).astype(jnp.bfloat16)
     delta_two = (cotangent.astype(jnp.float32) * swish_slope(act_two)).astype(jnp.bfloat16)
     grad_two = weight_grad(rim_hidden, delta_two)
-    rim_delta = extended(delta_two, (("gx", 1), ("gy", 2)), 1)
+    rim_delta = extended(delta_two, (("gy", 2), ("gx", 1)), 1)
     back_grad = conv_block(rim_delta, flipped)
     delta_one = (back_grad * swish_slope(act_one)).astype(jnp.bfloat16)
     grad_one = weight_grad(rim_input, delta_one)

time: 313 us -> 300 us (0.958)
  waiting for transfers between devices: 95.5 us -> 87.4 us
  starting transfers between devices: 49.4 us -> 45.3 us
    ppermute x6, waiting for transfers between devices: 33.1 us -> 24.1 us  [extended(): lax.ppermute(head, axis, [((i + 1) % count, i) for i in range(ends)])]
    ppermute x10, starting transfers between devices: 11 us -> 6.48 us  [tree_sum(): other = lax.ppermute(rows, axis, pairs)]
    ppermute x10, waiting for transfers between devices: 16 us -> 19.4 us  [tree_sum(): other = lax.ppermute(rows, axis, pairs)]
  transfers between devices with their start and end apart: 32 -> 32, of which waited for: 24 -> 25; matrix products, arithmetic and copies ran while one was open for 32% -> 33% of each run, Pallas kernels for 0% -> 0%
where the time goes in v7:
time: 300 us; the launch traced here: 296 us
  matrix products  104 us (35%)
  waiting for transfers between devices  87.4 us (29%)
  starting transfers between devices  45.3 us (15%)
  local copies, waits for them, and re-layouts  30.8 us (10%)
  other arithmetic  26.9 us (9%)
    conv_general_dilated x3, matrix products, conv_block(): lax.conv_general_dilated(padded, cube_kernel, (1, 1, 1), ((0, 0), (0, 0),...  53.1 us
    conv_general_dilated x2, matrix products, kernel_grad(): lax.conv_general_dilated(padded, delta_field, (1, 1, 1), ((0, 0), (0, 0),...  51.2 us
    ppermute x10, waiting for transfers between devices, tree_sum(): rows = keep + lax.ppermute(send, axis, pairs)  27.7 us
    ppermute x6, waiting for transfers between devices, extended(): lax.ppermute(head, axis, [((i + 1) % count, i) for i in range(ends)])  24.1 us
    ppermute x6, starting transfers between devices, extended(): lax.ppermute(tail, axis, [(i, (i + 1) % count) for i in range(ends)])  21 us
    ppermute x10, waiting for transfers between devices, tree_sum(): other = lax.ppermute(rows, axis, pairs)  19.4 us
    ppermute x6, waiting for transfers between devices, extended(): lax.ppermute(tail, axis, [(i, (i + 1) % count) for i in range(ends)])  16.2 us
    unnamed x40, local copies, waits for them, and re-layouts  10.7 us
  transfers between devices with their start and end apart: 32, of which 25 were waited for; matrix products, arithmetic and copies ran while one was open for 33% of the time, Pallas kernels for 0%

profile of v7, /device:TPU:0, one launch (start us, length us, event | category | flops | bytes accessed | tf_op | source)
XLA Modules:
  0.0 296.4 jit_solution(6841767011578305749)
XLA Ops:
  2.0 4.9 %collective-permute-start = (bf16[3,8,1,32,128]{4,0,3,2,1:T(4,128)(2,1)S(1)}, bf16[3,8,1,32,128]{4,0,3,2,1:T(4,128)(2,1)S(1)}, u32[]{:S(2)}, u32[]{:S(2)}) collective-permute-start(bf16[3,8,1,32,128]{4,0,3,2,1:T(4,128)(2,1)S(1)} %copy.55), channel_id=1, source_target_pairs={{0,2},{2,4},{4,6},{1,3},{3,5},{5,7},{8,10},{10,12},{12,14},{9,11},... | collective-permute-start | bytes 589832 | tf_op jit(solution)/shard_map/ppermute | solution.py:15
  8.3 4.1 %collective-permute-done = bf16[3,8,1,32,128]{4,0,3,2,1:T(4,128)(2,1)S(1)} collective-permute-done((bf16[3,8,1,32,128]{4,0,3,2,1:T(4,128)(2,1)S(1)}, bf16[3,8,1,32,128]{4,0,3,2,1:T(4,128)(2,1)S(1)}, u32[]{:S(2)}, u32[]{:S(2)}) %collective-permute-start) | collective-permute-done | bytes 196640 | tf_op jit(solution)/shard_map/ppermute | solution.py:15
  12.5 2.9 constant_dynamic-update-slice_fusion.1
  15.4 4.6 %collective-permute-done.1 = bf16[3,8,1,32,128]{4,0,3,2,1:T(4,128)(2,1)S(1)} collective-permute-done((bf16[3,8,1,32,128]{4,0,3,2,1:T(4,128)(2,1)S(1)}, bf16[3,8,1,32,128]{4,0,3,2,1:T(4,128)(2,1)S(1)}, u32[]{:S(2)}, u32[]{:S(2)}) %collective-permute-start.1) | collective-permute-done | bytes 196640 | tf_op jit(solution)/shard_map/ppermute | solution.py:17
  20.4 3.5 %collective-permute-start.2 = (bf16[3,1,10,32,128]{4,0,3,2,1:T(4,128)(2,1)S(1)}, bf16[3,1,10,32,128]{4,0,3,2,1:T(4,128)(2,1)S(1)}, u32[]{:S(2)}, u32[]{:S(2)}) collective-permute-start(bf16[3,1,10,32,128]{4,0,3,2,1:T(4,128)(2,1)S(1)} %get-tuple-element.10), channel_id=1, source_target_pairs={{0,8},{8,16},{16,24},{1,9},{9,17},{17,25},{2,10},{10,18},{18,26},{... | collective-permute-start | bytes 737288 | tf_op jit(solution)/shard_map/ppermute | solution.py:15
  25.4 4.6 %collective-permute-done.2 = bf16[3,1,10,32,128]{4,0,3,2,1:T(4,128)(2,1)S(1)} collective-permute-done((bf16[3,1,10,32,128]{4,0,3,2,1:T(4,128)(2,1)S(1)}, bf16[3,1,10,32,128]{4,0,3,2,1:T(4,128)(2,1)S(1)}, u32[]{:S(2)}, u32[]{:S(2)}) %collective-permute-start.2) | collective-permute-done | bytes 245792 | tf_op jit(solution)/shard_map/ppermute | solution.py:15
  30.0 4.1 %collective-permute-done.3 = bf16[3,1,10,32,128]{4,0,3,2,1:T(4,128)(2,1)S(1)} collective-permute-done((bf16[3,1,10,32,128]{4,0,3,2,1:T(4,128)(2,1)S(1)}, bf16[3,1,10,32,128]{4,0,3,2,1:T(4,128)(2,1)S(1)}, u32[]{:S(2)}, u32[]{:S(2)}) %collective-permute-start.3) | collective-permute-done | bytes 245792 | tf_op jit(solution)/shard_map/ppermute | solution.py:17
  34.1 2.6 fusion.42
  39.4 15.5 %broadcast_select_fusion.1 = f32[8,8,24,5,128]{4,2,3,1,0:T(8,128)S(1)} fusion(pred[24,5]{0,1:T(8,128)(4,1)S(1)} %copy-done.15, bf16[3,3,3,128,128]{4,3,2,1,0:T(8,128)(2,1)S(1)} %bitcast.65, bf16[10,10,3,7,2,128]{5,3,2,4,1,0:T(8,128)(2,1)S(1)} %slice.69, bf16[10,10,3,8,5,128]{5,3,2,4,1,0:T(8,128)(2,1)S(1)} %copy.21), kind=kOutput, calls=%fused_computation.42 | convolution fusion | flops 6808657920 | bytes 8964216 | tf_op jit(solution)/shard_map/conv_general_dilated | solution.py:27
  61.1 3.4 %collective-permute-start.4 = (bf16[3,8,1,32,128]{4,0,3,2,1:T(4,128)(2,1)S(1)}, bf16[3,8,1,32,128]{4,0,3,2,1:T(4,128)(2,1)S(1)}, u32[]{:S(2)}, u32[]{:S(2)}) collective-permute-start(bf16[3,8,1,32,128]{4,0,3,2,1:T(4,128)(2,1)S(1)} %get-tuple-element.14), channel_id=1, source_target_pairs={{0,2},{2,4},{4,6},{1,3},{3,5},{5,7},{8,10},{10,12},{12,14},{9,11},... | collective-permute-start | bytes 589832 | tf_op jit(solution)/shard_map/ppermute | solution.py:15
  68.3 6.1 %collective-permute-done.5 = bf16[3,8,1,32,128]{4,0,3,2,1:T(4,128)(2,1)S(1)} collective-permute-done((bf16[3,8,1,32,128]{4,0,3,2,1:T(4,128)(2,1)S(1)}, bf16[3,8,1,32,128]{4,0,3,2,1:T(4,128)(2,1)S(1)}, u32[]{:S(2)}, u32[]{:S(2)}) %collective-permute-start.5) | collective-permute-done | bytes 196640 | tf_op jit(solution)/shard_map/ppermute | solution.py:17
  75.7 4.2 %collective-permute-start.6 = (bf16[3,1,10,32,128]{4,0,3,2,1:T(4,128)(2,1)}, bf16[3,1,10,32,128]{4,0,3,2,1:T(4,128)(2,1)}, u32[]{:S(2)}, u32[]{:S(2)}) collective-permute-start(bf16[3,1,10,32,128]{4,0,3,2,1:T(4,128)(2,1)} %get-tuple-element.8), channel_id=1, source_target_pairs={{0,8},{8,16},{16,24},{1,9},{9,17},{17,25},{2,10},{10,18},{18,26},{... | collective-permute-start | bytes 737288 | tf_op jit(solution)/shard_map/ppermute | solution.py:15
  84.3 4.9 %collective-permute-done.7 = bf16[3,1,10,32,128]{4,0,3,2,1:T(4,128)(2,1)} collective-permute-done((bf16[3,1,10,32,128]{4,0,3,2,1:T(4,128)(2,1)}, bf16[3,1,10,32,128]{4,0,3,2,1:T(4,128)(2,1)}, u32[]{:S(2)}, u32[]{:S(2)}) %collective-permute-start.7) | collective-permute-done | bytes 245792 | tf_op jit(solution)/shard_map/ppermute | solution.py:17
  89.2 4.1 %fusion.51 = bf16[10,10,3,32,128]{4,2,3,1,0:T(4,128)(2,1)S(1)} fusion(bf16[3,1,10,32,128]{4,0,3,2,1:T(4,128)(2,1)} %collective-permute-done.7, bf16[3,8,1,32,128]{4,0,3,2,1:T(4,128)(2,1)S(1)} %collective-permute-done.5, bf16[3,8,8,32,128]{4,0,3,2,1:T(4,128)(2,1)S(1)} %multiply_convert_fusion, bf16[3,8,1,32,128]{4,0,3,2,1:T(4,128)(2,1)S(1)} %collective-permute-done.4, ...), kind=kLoop, calls=%fused_computation.117 | loop fusion | flops 4915200 | bytes 4915200 | tf_op jit(solution)/shard_map/concatenate | solution.py:13
  95.9 17.1 %add_multiply_fusion = (f32[8,8,24,5,128]{4,2,3,1,0:T(8,128)S(1)}, bf16[8,8,24,5,128]{4,2,3,1,0:T(8,128)(2,1)}) fusion(pred[24,5]{0,1:T(8,128)(4,1)S(1)} %copy-done.15, bf16[3,3,3,128,128]{4,3,2,1,0:T(8,128)(2,1)S(1)} %bitcast.79, bf16[10,10,3,7,2,128]{5,3,2,4,1,0:T(8,128)(2,1)S(1)} %slice.73, bf16[10,10,3,8,5,128]{5,3,2,4,1,0:T(8,128)(2,1)S(1)} %copy.25), kind=kOutput, calls=%fused_computation.28 | convolution fusion | flops 6817505280 | bytes 10930296 | tf_op jit(solution)/shard_map/conv_general_dilated | solution.py:27
  120.8 24.2 %fusion.27 = f32[3,3,3,128,128]{4,3,2,1,0:T(8,128)S(1)} fusion(bf16[3,8,8,32,128]{4,2,3,0,1:T(8,128)(2,1)S(1)} %fusion.24, bf16[3,1,10,32,128]{4,0,3,2,1:T(4,128)(2,1)} %collective-permute-done.7, bf16[3,8,1,32,128]{4,0,3,2,1:T(4,128)(2,1)S(1)} %collective-permute-done.5, bf16[3,8,8,32,128]{4,0,3,2,1:T(4,128)(2,1)S(1)} %multiply_convert_fusion, ...), kind=kOutput, calls=%fused_computation.38 | convolution fusion | flops 5334859776 | bytes 5799936 | tf_op jit(solution)/shard_map/conv_general_dilated | solution.py:39
  146.7 2.8 collective-permute-start.10
  151.8 3.0 collective-permute-done.10
  154.8 4.4 %collective-permute-done.11 = bf16[3,1,10,32,128]{4,2,3,0,1:T(8,128)(2,1)S(1)} collective-permute-done((bf16[3,1,10,32,128]{4,2,3,0,1:T(8,128)(2,1)S(1)}, bf16[3,1,10,32,128]{4,2,3,0,1:T(8,128)(2,1)S(1)}, u32[]{:S(2)}, u32[]{:S(2)}) %collective-permute-start.11) | collective-permute-done | bytes 245792 | tf_op jit(solution)/shard_map/ppermute | solution.py:17
  159.2 3.3 %maximum_bitcast_fusion = bf16[10,10,3,32,128]{4,1,3,2,0:T(8,128)(2,1)S(1)} fusion(bf16[3,1,10,32,128]{4,2,3,0,1:T(8,128)(2,1)S(1)} %collective-permute-done.11, bf16[3,8,1,32,128]{4,2,3,0,1:T(2,128)(2,1)} %collective-permute-done.9, bf16[3,8,8,32,128]{4,2,3,0,1:T(8,128)(2,1)S(1)} %fusion.24, bf16[3,8,1,32,128]{4,2,3,0,1:T(2,128)(2,1)} %collective-permute-done.8, ...), kind=kLoop, calls=%fused_computation.27 | loop fusion | flops 12288000 | bytes 4915200 | tf_op jit(solution)/shard_map/concatenate | solution.py:13
  165.9 2.8 fusion.3
  168.7 20.5 %broadcast_select_fusion = f32[8,8,24,5,128]{4,2,3,1,0:T(8,128)S(1)} fusion(pred[24,5]{0,1:T(8,128)(4,1)S(1)} %copy-done.16, bf16[3,3,3,128,128]{3,4,2,1,0:T(8,128)(2,1)S(1)} %bitcast.80, bf16[10,10,3,8,7,128]{5,4,3,2,1,0:T(8,128)(2,1)S(1)} %fusion.3), kind=kOutput, calls=%fused_computation.41 | convolution fusion | flops 6795755520 | bytes 9117816 | tf_op jit(solution)/shard_map/conv_general_dilated | solution.py:27
  192.4 27.0 %fusion.29 = f32[3,3,3,128,128]{4,3,2,1,0:T(8,128)S(1)} fusion(f32[8,8,3,32,128]{4,1,3,2,0:T(8,128)S(1)} %slice.79, f32[3,8,8,32,128]{4,0,3,2,1:T(4,128)S(1)} %bitcast.68, bf16[3,1,10,32,128]{4,0,3,2,1:T(4,128)(2,1)S(1)} %copy-done.14, bf16[3,8,10,32,128]{4,0,3,2,1:T(4,128)(2,1)S(1)} %copy-done.7, bf16[3,1,10,32,128]{4,0,3,2,1:T(4,128)(2,1)S(1)} %copy-done.12), kind=kOutput, calls=%fused_computation.40 | convolution fusion | flops 5337022464 | bytes 10518528 | tf_op jit(solution)/shard_map/conv_general_dilated | solution.py:39
  222.6 2.7 collective-permute-start.23
  227.2 8.7 %collective-permute-done.23 = f32[896,128]{1,0:T(8,128)} collective-permute-done((f32[896,128]{1,0:T(8,128)S(1)}, f32[896,128]{1,0:T(8,128)}, u32[]{:S(2)}, u32[]{:S(2)}) %collective-permute-start.23) | collective-permute-done | bytes 458784 | tf_op jit(solution)/shard_map/ppermute | solution.py:78
  239.0 4.9 %collective-permute-done.24 = f32[448,128]{1,0:T(8,128)S(1)} collective-permute-done((f32[448,128]{1,0:T(8,128)S(1)}, f32[448,128]{1,0:T(8,128)S(1)}, u32[]{:S(2)}, u32[]{:S(2)}) %collective-permute-start.24) | collective-permute-done | bytes 229408 | tf_op jit(solution)/shard_map/ppermute | solution.py:78
  245.7 3.1 %collective-permute-done.25 = f32[224,128]{1,0:T(8,128)S(1)} collective-permute-done((f32[224,128]{1,0:T(8,128)S(1)}, f32[224,128]{1,0:T(8,128)S(1)}, u32[]{:S(2)}, u32[]{:S(2)}) %collective-permute-start.25) | collective-permute-done | bytes 114720 | tf_op jit(solution)/shard_map/ppermute | solution.py:78
  250.5 4.3 %collective-permute-done.26 = f32[112,128]{1,0:T(8,128)S(1)} collective-permute-done((f32[112,128]{1,0:T(8,128)S(1)}, f32[112,128]{1,0:T(8,128)S(1)}, u32[]{:S(2)}, u32[]{:S(2)}) %collective-permute-start.26) | collective-permute-done | bytes 57376 | tf_op jit(solution)/shard_map/ppermute | solution.py:78
  255.5 4.2 %collective-permute-done.27 = bf16[112,128]{1,0:T(8,128)(2,1)S(1)} collective-permute-done((bf16[112,128]{1,0:T(8,128)(2,1)S(1)}, bf16[112,128]{1,0:T(8,128)(2,1)S(1)}, u32[]{:S(2)}, u32[]{:S(2)}) %collective-permute-start.27) | collective-permute-done | bytes 28704 | tf_op jit(solution)/shard_map/ppermute | solution.py:83
  269.5 2.7 collective-permute-done.16
  274.3 2.9 collective-permute-done.17
  287.6 4.9 %collective-permute-done.20 = bf16[896,128]{1,0:T(8,128)(2,1)S(1)} collective-permute-done((bf16[896,128]{1,0:T(8,128)(2,1)S(1)}, bf16[896,128]{1,0:T(8,128)(2,1)S(1)}, u32[]{:S(2)}, u32[]{:S(2)}) %collective-permute-start.20) | collective-permute-done | bytes 229408 | tf_op jit(solution)/shard_map/ppermute | solution.py:83
  (151 shorter events, 82.0 us)
Async XLA Ops:
  2.0 10.4 %collective-permute-start = (bf16[3,8,1,32,128]{4,0,3,2,1:T(4,128)(2,1)S(1)}, bf16[3,8,1,32,128]{4,0,3,2,1:T(4,128)(2,1)S(1)}, u32[]{:S(2)}, u32[]{:S(2)}) collective-permute-start(bf16[3,8,1,32,128]{4,0,3,2,1:T(4,128)(2,1)S(1)} %copy.55), channel_id=1, source_target_pairs={{0,2},{2,4},{4,6},{1,3},{3,5},{5,7},{8,10},{10,12},{12,14},{9,11},... | collective-permute-start | bytes 589832 | tf_op jit(solution)/shard_map/ppermute | solution.py:15
  7.0 12.9 %collective-permute-start.1 = (bf16[3,8,1,32,128]{4,0,3,2,1:T(4,128)(2,1)S(1)}, bf16[3,8,1,32,128]{4,0,3,2,1:T(4,128)(2,1)S(1)}, u32[]{:S(2)}, u32[]{:S(2)}) collective-permute-start(bf16[3,8,1,32,128]{4,0,3,2,1:T(4,128)(2,1)S(1)} %copy.56), channel_id=1, source_target_pairs={{2,0},{4,2},{6,4},{3,1},{5,3},{7,5},{10,8},{12,10},{14,12},{11,9},... | collective-permute-start | bytes 589832 | tf_op jit(solution)/shard_map/ppermute | solution.py:17
  20.4 9.6 %collective-permute-start.2 = (bf16[3,1,10,32,128]{4,0,3,2,1:T(4,128)(2,1)S(1)}, bf16[3,1,10,32,128]{4,0,3,2,1:T(4,128)(2,1)S(1)}, u32[]{:S(2)}, u32[]{:S(2)}) collective-permute-start(bf16[3,1,10,32,128]{4,0,3,2,1:T(4,128)(2,1)S(1)} %get-tuple-element.10), channel_id=1, source_target_pairs={{0,8},{8,16},{16,24},{1,9},{9,17},{17,25},{2,10},{10,18},{18,26},{... | collective-permute-start | bytes 737288 | tf_op jit(solution)/shard_map/ppermute | solution.py:15
  23.9 10.2 %collective-permute-start.3 = (bf16[3,1,10,32,128]{4,0,3,2,1:T(4,128)(2,1)S(1)}, bf16[3,1,10,32,128]{4,0,3,2,1:T(4,128)(2,1)S(1)}, u32[]{:S(2)}, u32[]{:S(2)}) collective-permute-start(bf16[3,1,10,32,128]{4,0,3,2,1:T(4,128)(2,1)S(1)} %get-tuple-element.11), channel_id=1, source_target_pairs={{8,0},{16,8},{24,16},{9,1},{17,9},{25,17},{10,2},{18,10},{26,18},{... | collective-permute-start | bytes 737288 | tf_op jit(solution)/shard_map/ppermute | solution.py:17
  61.1 7.3 %collective-permute-start.4 = (bf16[3,8,1,32,128]{4,0,3,2,1:T(4,128)(2,1)S(1)}, bf16[3,8,1,32,128]{4,0,3,2,1:T(4,128)(2,1)S(1)}, u32[]{:S(2)}, u32[]{:S(2)}) collective-permute-start(bf16[3,8,1,32,128]{4,0,3,2,1:T(4,128)(2,1)S(1)} %get-tuple-element.14), channel_id=1, source_target_pairs={{0,2},{2,4},{4,6},{1,3},{3,5},{5,7},{8,10},{10,12},{12,14},{9,11},... | collective-permute-start | bytes 589832 | tf_op jit(solution)/shard_map/ppermute | solution.py:15
  64.5 9.9 %collective-permute-start.5 = (bf16[3,8,1,32,128]{4,0,3,2,1:T(4,128)(2,1)S(1)}, bf16[3,8,1,32,128]{4,0,3,2,1:T(4,128)(2,1)S(1)}, u32[]{:S(2)}, u32[]{:S(2)}) collective-permute-start(bf16[3,8,1,32,128]{4,0,3,2,1:T(4,128)(2,1)S(1)} %get-tuple-element.15), channel_id=1, source_target_pairs={{2,0},{4,2},{6,4},{3,1},{5,3},{7,5},{10,8},{12,10},{14,12},{11,9},... | collective-permute-start | bytes 589832 | tf_op jit(solution)/shard_map/ppermute | solution.py:17
  75.7 8.6 %collective-permute-start.6 = (bf16[3,1,10,32,128]{4,0,3,2,1:T(4,128)(2,1)}, bf16[3,1,10,32,128]{4,0,3,2,1:T(4,128)(2,1)}, u32[]{:S(2)}, u32[]{:S(2)}) collective-permute-start(bf16[3,1,10,32,128]{4,0,3,2,1:T(4,128)(2,1)} %get-tuple-element.8), channel_id=1, source_target_pairs={{0,8},{8,16},{16,24},{1,9},{9,17},{17,25},{2,10},{10,18},{18,26},{... | collective-permute-start | bytes 737288 | tf_op jit(solution)/shard_map/ppermute | solution.py:15
  79.9 9.3 %collective-permute-start.7 = (bf16[3,1,10,32,128]{4,0,3,2,1:T(4,128)(2,1)}, bf16[3,1,10,32,128]{4,0,3,2,1:T(4,128)(2,1)}, u32[]{:S(2)}, u32[]{:S(2)}) collective-permute-start(bf16[3,1,10,32,128]{4,0,3,2,1:T(4,128)(2,1)} %get-tuple-element.9), channel_id=1, source_target_pairs={{8,0},{16,8},{24,16},{9,1},{17,9},{25,17},{10,2},{18,10},{26,18},{... | collective-permute-start | bytes 737288 | tf_op jit(solution)/shard_map/ppermute | solution.py:17
  117.1 28.0 %collective-permute-start.8 = (bf16[3,8,1,32,128]{4,2,3,0,1:T(2,128)(2,1)}, bf16[3,8,1,32,128]{4,2,3,0,1:T(2,128)(2,1)}, u32[]{:S(2)}, u32[]{:S(2)}) collective-permute-start(bf16[3,8,1,32,128]{4,2,3,0,1:T(2,128)(2,1)} %get-tuple-element.16), channel_id=1, source_target_pairs={{0,2},{2,4},{4,6},{1,3},{3,5},{5,7},{8,10},{10,12},{12,14},{9,11},... | collective-permute-start | bytes 589832 | tf_op jit(solution)/shard_map/ppermute | solution.py:15
  119.4 25.8 %collective-permute-start.9 = (bf16[3,8,1,32,128]{4,2,3,0,1:T(2,128)(2,1)}, bf16[3,8,1,32,128]{4,2,3,0,1:T(2,128)(2,1)}, u32[]{:S(2)}, u32[]{:S(2)}) collective-permute-start(bf16[3,8,1,32,128]{4,2,3,0,1:T(2,128)(2,1)} %get-tuple-element.17), channel_id=1, source_target_pairs={{2,0},{4,2},{6,4},{3,1},{5,3},{7,5},{10,8},{12,10},{14,12},{11,9},... | collective-permute-start | bytes 589832 | tf_op jit(solution)/shard_map/ppermute | solution.py:17
  146.7 8.1 %collective-permute-start.10 = (bf16[3,1,10,32,128]{4,2,3,0,1:T(8,128)(2,1)S(1)}, bf16[3,1,10,32,128]{4,2,3,0,1:T(8,128)(2,1)S(1)}, u32[]{:S(2)}, u32[]{:S(2)}) collective-permute-start(bf16[3,1,10,32,128]{4,2,3,0,1:T(8,128)(2,1)S(1)} %get-tuple-element.12), channel_id=1, source_target_pairs={{0,8},{8,16},{16,24},{1,9},{9,17},{17,25},{2,10},{10,18},{18,26},{... | collective-permute-start | bytes 737288 | tf_op jit(solution)/shard_map/ppermute | solution.py:15
  149.5 9.7 %collective-permute-start.11 = (bf16[3,1,10,32,128]{4,2,3,0,1:T(8,128)(2,1)S(1)}, bf16[3,1,10,32,128]{4,2,3,0,1:T(8,128)(2,1)S(1)}, u32[]{:S(2)}, u32[]{:S(2)}) collective-permute-start(bf16[3,1,10,32,128]{4,2,3,0,1:T(8,128)(2,1)S(1)} %get-tuple-element.13), channel_id=1, source_target_pairs={{8,0},{16,8},{24,16},{9,1},{17,9},{25,17},{10,2},{18,10},{26,18},{... | collective-permute-start | bytes 737288 | tf_op jit(solution)/shard_map/ppermute | solution.py:17
  151.8 68.8 %collective-permute-start.22 = (f32[1792,128]{1,0:T(8,128)}, f32[1792,128]{1,0:T(8,128)}, u32[]{:S(2)}, u32[]{:S(2)}) collective-permute-start(f32[1792,128]{1,0:T(8,128)} %constant_dynamic-slice_fusion.4), channel_id=1, source_target_pairs={{0,1},{1,0},{2,3},{3,2},{4,5},{5,4},{6,7},{7,6},{8,9},{9,8},{10,11... | collective-permute-start | bytes 2752520 | tf_op jit(solution)/shard_map/ppermute | solution.py:78
  220.5 17.2 %collective-permute-start.12 = (f32[1792,128]{1,0:T(8,128)}, f32[1792,128]{1,0:T(8,128)}, u32[]{:S(2)}, u32[]{:S(2)}) collective-permute-start(f32[1792,128]{1,0:T(8,128)} %constant_dynamic-slice_fusion.9), channel_id=1, source_target_pairs={{0,1},{1,0},{2,3},{3,2},{4,5},{5,4},{6,7},{7,6},{8,9},{9,8},{10,11... | collective-permute-start | bytes 2752520 | tf_op jit(solution)/shard_map/ppermute | solution.py:78
  222.6 13.3 %collective-permute-start.23 = (f32[896,128]{1,0:T(8,128)S(1)}, f32[896,128]{1,0:T(8,128)}, u32[]{:S(2)}, u32[]{:S(2)}) collective-permute-start(f32[896,128]{1,0:T(8,128)S(1)} %constant_dynamic-slice_fusion.3), channel_id=1, source_target_pairs={{0,2},{2,0},{4,6},{6,4},{1,3},{3,1},{5,7},{7,5},{8,10},{10,8},{12,... | collective-permute-start | bytes 1376264 | tf_op jit(solution)/shard_map/ppermute | solution.py:78
  237.0 6.8 %collective-permute-start.24 = (f32[448,128]{1,0:T(8,128)S(1)}, f32[448,128]{1,0:T(8,128)S(1)}, u32[]{:S(2)}, u32[]{:S(2)}) collective-permute-start(f32[448,128]{1,0:T(8,128)S(1)} %constant_dynamic-slice_fusion.2), channel_id=1, source_target_pairs={{0,4},{2,6},{4,0},{6,2},{1,5},{3,7},{5,1},{7,3},{8,12},{10,14},{12... | collective-permute-start | bytes 688136 | tf_op jit(solution)/shard_map/ppermute | solution.py:78
  243.9 4.9 %collective-permute-start.25 = (f32[224,128]{1,0:T(8,128)S(1)}, f32[224,128]{1,0:T(8,128)S(1)}, u32[]{:S(2)}, u32[]{:S(2)}) collective-permute-start(f32[224,128]{1,0:T(8,128)S(1)} %constant_dynamic-slice_fusion.1), channel_id=1, source_target_pairs={{0,8},{8,0},{16,24},{24,16},{1,9},{9,1},{17,25},{25,17},{2,10},{10... | collective-permute-start | bytes 344072 | tf_op jit(solution)/shard_map/ppermute | solution.py:78
  244.2 10.7 %collective-permute-start.13 = (f32[896,128]{1,0:T(8,128)S(1)}, f32[896,128]{1,0:T(8,128)S(1)}, u32[]{:S(2)}, u32[]{:S(2)}) collective-permute-start(f32[896,128]{1,0:T(8,128)S(1)} %constant_dynamic-slice_fusion.8), channel_id=1, source_target_pairs={{0,2},{2,0},{4,6},{6,4},{1,3},{3,1},{5,7},{7,5},{8,10},{10,8},{12,... | collective-permute-start | bytes 1376264 | tf_op jit(solution)/shard_map/ppermute | solution.py:78
  248.8 6.0 %collective-permute-start.26 = (f32[112,128]{1,0:T(8,128)S(1)}, f32[112,128]{1,0:T(8,128)S(1)}, u32[]{:S(2)}, u32[]{:S(2)}) collective-permute-start(f32[112,128]{1,0:T(8,128)S(1)} %constant_dynamic-slice_fusion), channel_id=1, source_target_pairs={{0,16},{8,24},{16,0},{24,8},{1,17},{9,25},{17,1},{25,9},{2,18},{10... | collective-permute-start | bytes 172040 | tf_op jit(solution)/shard_map/ppermute | solution.py:78
  254.9 4.8 %collective-permute-start.27 = (bf16[112,128]{1,0:T(8,128)(2,1)S(1)}, bf16[112,128]{1,0:T(8,128)(2,1)S(1)}, u32[]{:S(2)}, u32[]{:S(2)}) collective-permute-start(bf16[112,128]{1,0:T(8,128)(2,1)S(1)} %add_convert_fusion), channel_id=1, source_target_pairs={{0,16},{8,24},{16,0},{24,8},{1,17},{9,25},{17,1},{25,9},{2,18},{10... | collective-permute-start | bytes 86024 | tf_op jit(solution)/shard_map/ppermute | solution.py:83
  255.1 6.1 %collective-permute-start.14 = (f32[448,128]{1,0:T(8,128)S(1)}, f32[448,128]{1,0:T(8,128)S(1)}, u32[]{:S(2)}, u32[]{:S(2)}) collective-permute-start(f32[448,128]{1,0:T(8,128)S(1)} %constant_dynamic-slice_fusion.7), channel_id=1, source_target_pairs={{0,4},{2,6},{4,0},{6,2},{1,5},{3,7},{5,1},{7,3},{8,12},{10,14},{12... | collective-permute-start | bytes 688136 | tf_op jit(solution)/shard_map/ppermute | solution.py:78
  259.7 4.2 %collective-permute-start.28 = (bf16[224,128]{1,0:T(8,128)(2,1)S(1)}, bf16[224,128]{1,0:T(8,128)(2,1)S(1)}, u32[]{:S(2)}, u32[]{:S(2)}) collective-permute-start(bf16[224,128]{1,0:T(8,128)(2,1)S(1)} %pad_maximum_fusion.17), channel_id=1, source_target_pairs={{0,8},{8,0},{16,24},{24,16},{1,9},{9,1},{17,25},{25,17},{2,10},{10... | collective-permute-start | bytes 172040 | tf_op jit(solution)/shard_map/ppermute | solution.py:83
  261.2 5.4 %collective-permute-start.15 = (f32[224,128]{1,0:T(8,128)S(1)}, f32[224,128]{1,0:T(8,128)S(1)}, u32[]{:S(2)}, u32[]{:S(2)}) collective-permute-start(f32[224,128]{1,0:T(8,128)S(1)} %constant_dynamic-slice_fusion.6), channel_id=1, source_target_pairs={{0,8},{8,0},{16,24},{24,16},{1,9},{9,1},{17,25},{25,17},{2,10},{10... | collective-permute-start | bytes 344072 | tf_op jit(solution)/shard_map/ppermute | solution.py:78
  266.7 5.6 %collective-permute-start.16 = (f32[112,128]{1,0:T(8,128)S(1)}, f32[112,128]{1,0:T(8,128)S(1)}, u32[]{:S(2)}, u32[]{:S(2)}) collective-permute-start(f32[112,128]{1,0:T(8,128)S(1)} %constant_dynamic-slice_fusion.5), channel_id=1, source_target_pairs={{0,16},{8,24},{16,0},{24,8},{1,17},{9,25},{17,1},{25,9},{2,18},{10... | collective-permute-start | bytes 172040 | tf_op jit(solution)/shard_map/ppermute | solution.py:78
  269.1 5.1 %collective-permute-start.29 = (bf16[448,128]{1,0:T(8,128)(2,1)S(1)}, bf16[448,128]{1,0:T(8,128)(2,1)S(1)}, u32[]{:S(2)}, u32[]{:S(2)}) collective-permute-start(bf16[448,128]{1,0:T(8,128)(2,1)S(1)} %pad_maximum_fusion.15), channel_id=1, source_target_pairs={{0,4},{2,6},{4,0},{6,2},{1,5},{3,7},{5,1},{7,3},{8,12},{10,14},{12... | collective-permute-start | bytes 344072 | tf_op jit(solution)/shard_map/ppermute | solution.py:83
  272.3 4.8 %collective-permute-start.17 = (bf16[112,128]{1,0:T(8,128)(2,1)S(1)}, bf16[112,128]{1,0:T(8,128)(2,1)S(1)}, u32[]{:S(2)}, u32[]{:S(2)}) collective-permute-start(bf16[112,128]{1,0:T(8,128)(2,1)S(1)} %add_convert_fusion.1), channel_id=1, source_target_pairs={{0,16},{8,24},{16,0},{24,8},{1,17},{9,25},{17,1},{25,9},{2,18},{10... | collective-permute-start | bytes 86024 | tf_op jit(solution)/shard_map/ppermute | solution.py:83
  277.2 4.2 %collective-permute-start.18 = (bf16[224,128]{1,0:T(8,128)(2,1)S(1)}, bf16[224,128]{1,0:T(8,128)(2,1)S(1)}, u32[]{:S(2)}, u32[]{:S(2)}) collective-permute-start(bf16[224,128]{1,0:T(8,128)(2,1)S(1)} %pad_maximum_fusion.16), channel_id=1, source_target_pairs={{0,8},{8,0},{16,24},{24,16},{1,9},{9,1},{17,25},{25,17},{2,10},{10... | collective-permute-start | bytes 172040 | tf_op jit(solution)/shard_map/ppermute | solution.py:83
  278.1 6.1 %collective-permute-start.30 = (bf16[896,128]{1,0:T(8,128)(2,1)S(1)}, bf16[896,128]{1,0:T(8,128)(2,1)S(1)}, u32[]{:S(2)}, u32[]{:S(2)}) collective-permute-start(bf16[896,128]{1,0:T(8,128)(2,1)S(1)} %pad_maximum_fusion.13), channel_id=1, source_target_pairs={{0,2},{2,0},{4,6},{6,4},{1,3},{3,1},{5,7},{7,5},{8,10},{10,8},{12,... | collective-permute-start | bytes 688136 | tf_op jit(solution)/shard_map/ppermute | solution.py:83
  281.4 4.9 %collective-permute-start.19 = (bf16[448,128]{1,0:T(8,128)(2,1)S(1)}, bf16[448,128]{1,0:T(8,128)(2,1)S(1)}, u32[]{:S(2)}, u32[]{:S(2)}) collective-permute-start(bf16[448,128]{1,0:T(8,128)(2,1)S(1)} %pad_maximum_fusion.14), channel_id=1, source_target_pairs={{0,4},{2,6},{4,0},{6,2},{1,5},{3,7},{5,1},{7,3},{8,12},{10,14},{12... | collective-permute-start | bytes 344072 | tf_op jit(solution)/shard_map/ppermute | solution.py:83
  286.4 6.1 %collective-permute-start.20 = (bf16[896,128]{1,0:T(8,128)(2,1)S(1)}, bf16[896,128]{1,0:T(8,128)(2,1)S(1)}, u32[]{:S(2)}, u32[]{:S(2)}) collective-permute-start(bf16[896,128]{1,0:T(8,128)(2,1)S(1)} %pad_maximum_fusion.12), channel_id=1, source_target_pairs={{0,2},{2,0},{4,6},{6,4},{1,3},{3,1},{5,7},{7,5},{8,10},{10,8},{12,... | collective-permute-start | bytes 688136 | tf_op jit(solution)/shard_map/ppermute | solution.py:83
  287.5 5.2 %collective-permute-start.31 = (bf16[1792,128]{1,0:T(8,128)(2,1)S(1)}, bf16[1792,128]{1,0:T(8,128)(2,1)S(1)}, u32[]{:S(2)}, u32[]{:S(2)}) collective-permute-start(bf16[1792,128]{1,0:T(8,128)(2,1)S(1)} %pad_maximum_fusion.5), channel_id=1, source_target_pairs={{0,1},{1,0},{2,3},{3,2},{4,5},{5,4},{6,7},{7,6},{8,9},{9,8},{10,11... | collective-permute-start | bytes 1376264 | tf_op jit(solution)/shard_map/ppermute | solution.py:83
  292.6 1.9 collective-permute-start.21
  (17 other events, 140.9 us)
